TPU v7x, 32 devices: a whole 2x2x4 slice. The times are simulated.
32 devices in a mesh: groups: 2 (over y), tm: 16 (over z, x, core).
Axes of the slice: x: 2, y: 2, z: 4, core: 2. Of those that a mesh axis runs over, the one named last changes fastest.
Arguments:
- ref_traj: float32 [8, 1024, 256], P('groups', 'tm'), parts along dimension 0, may hold values from -6 to 6
- cost_weights: float32 [8, 1024, 256], P('groups', 'tm'), parts along dimension 0, may hold values from 0.1 to 10
- x_init: float32 [8, 256], P('groups'), parts along dimension 0, may hold values from -6 to 6
- decay: float32 [256], replicated, as said below
- coupling: float32 [3, 64, 64], replicated, may hold values from -0.00018310547 to 0.00018310547
- links: int32 [3, 2], replicated, may hold values from 0 to 3, as said below
- input_map: float32 [256, 64], replicated, may hold values from -0.0007324219 to 0.0007324219
- ff_gain: float32 [64, 256], replicated, may hold values from -0.01171875 to 0.01171875
- lengths: int32 [8, 4], P('groups'), parts along dimension 0, may hold values from 1 to 512, 1024 in all within a row
Outputs:
- states: float32 [8, 1024, 256], P('groups', 'tm'), parts along dimension 0
- weight_grad: float32 [8, 1024, 256], P('groups', 'tm'), parts along dimension 0
- cost: float32 [8], P('groups'), parts along dimension 0
There are 2 independent parts, one for each index of `groups`. A program takes and returns all parts, laid end to end along the dimension named above; an argument that names none is the same for every part. Nothing has to cross between parts.
Inputs may be any that keep to these rules, and one draw needn't show every extreme that they name: `links`: each pair names two different blocks, the row before the column, and no pair twice. The lengths of a scenario sum to 1024, and the longest is exactly 512. `decay`: every entry lies strictly between 0 and 1.
All inputs are finite; a program needn't handle non-finite values.
Results may differ from a plain program's by a relative error of at most 0.0003.
Values sent between devices are 32-bit elements; how exact they have to be, the bound alone decides.
No kernel may reach another device: no remote copies, remote signals or barrier semaphores. Data moves between devices by JAX's collectives and lax.ppermute only.
A program may use at most 64 MiB of HBM per device.

v0:
```python
import jax
import jax.numpy as jnp
from jax import lax
from jax.sharding import PartitionSpec as P


def build_dynamics(decay, coupling, links):
    size = decay.shape[0]
    width = coupling.shape[1]
    lanes = jnp.arange(size, dtype=jnp.int32)
    offsets = jnp.arange(width, dtype=jnp.int32)
    row_hot = (lanes[None, :, None] == links[:, 0:1, None] * width + offsets[None, None, :]).astype(
        jnp.float32
    )
    col_hot = (lanes[None, :, None] == links[:, 1:2, None] * width + offsets[None, None, :]).astype(
        jnp.float32
    )
    placed = jnp.einsum(
        "lia,lab,ljb->ij", row_hot, coupling, col_hot, precision=lax.Precision.HIGHEST
    )
    return jnp.diag(decay) + placed


def row_times(values, matrix):
    width = values.shape[-1]
    flat = jnp.dot(values.reshape(-1, width), matrix, precision=lax.Precision.HIGHEST)
    return flat.reshape(values.shape)


def run_chain(inputs, frame_starts, powers, backward, local_levels, device_levels):
    scen_count, seg_steps, width = inputs.shape
    devices = lax.axis_size("tm")
    device = lax.axis_index("tm")
    if backward:
        driven = inputs[:, ::-1]
        frame_device = devices - 1 - device
    else:
        driven = inputs
        frame_device = device
    positions = frame_device * seg_steps + jnp.arange(seg_steps, dtype=jnp.int32)
    cut_here = jnp.any(positions[None, :, None] == frame_starts[:, None, :], axis=-1)
    values = driven
    flags = 1.0 - cut_here.astype(jnp.float32)
    for level in range(local_levels):
        stride = 2**level
        prior_values = jnp.pad(values[:, : seg_steps - stride], ((0, 0), (stride, 0), (0, 0)))
        prior_flags = jnp.pad(
            flags[:, : seg_steps - stride], ((0, 0), (stride, 0)), constant_values=1.0
        )
        values = values + flags[:, :, None] * row_times(prior_values, powers[level])
        flags = flags * prior_flags
    last_value = values[:, -1]
    last_flag = flags[:, -1]
    all_values, all_flags = (
        lax.all_gather(last_value[None], "tm", axis=0, tiled=True),
        lax.all_gather(last_flag[None], "tm", axis=0, tiled=True),
    )
    if backward:
        all_values = all_values[::-1]
        all_flags = all_flags[::-1]
    roll_by = devices - frame_device
    all_values = jnp.roll(all_values, roll_by, axis=0)
    all_flags = jnp.roll(all_flags, roll_by, axis=0)
    keep = (jnp.arange(devices, dtype=jnp.int32) >= roll_by).astype(jnp.float32)
    all_values = all_values * keep[:, None, None]
    all_flags = all_flags * keep[:, None] + (1.0 - keep[:, None])
    for level in range(device_levels):
        half = all_values.shape[0] // 2
        paired_values = all_values.reshape(half, 2, scen_count, width)
        paired_flags = all_flags.reshape(half, 2, scen_count)
        moved = row_times(paired_values[:, 0], powers[local_levels + level])
        all_values = paired_flags[:, 1, :, None] * moved + paired_values[:, 1]
        all_flags = paired_flags[:, 0] * paired_flags[:, 1]
    entering = all_values[0]
    table = row_times(entering[:, None, :], powers[0])
    for level in range(local_levels):
        table = jnp.concatenate([table, row_times(table, powers[level])], axis=1)
    result = values + flags[:, :, None] * table
    if backward:
        result = result[:, ::-1]
    return result


def per_device(ref_traj, cost_weights, x_init, decay, coupling, links, input_map, ff_gain, lengths):
    scen_count, seg_steps, width = ref_traj.shape
    devices = lax.axis_size("tm")
    device = lax.axis_index("tm")
    total = seg_steps * devices
    high = lax.Precision.HIGHEST
    dynamics = build_dynamics(decay, coupling, links)
    local_levels = seg_steps.bit_length() - 1
    device_levels = (devices - 1).bit_length()
    power_count = local_levels + max(device_levels, 1)
    squares = [dynamics]
    for level in range(power_count - 1):
        squares.append(jnp.dot(squares[-1], squares[-1], precision=high))
    forward_powers = [matrix.T for matrix in squares]
    ends_incl = jnp.cumsum(lengths, axis=1)
    starts = ends_incl - lengths
    mirrored = total - ends_incl
    value_term = run_chain(
        cost_weights * ref_traj, mirrored, squares, True, local_levels, device_levels
    )
    controls = jnp.einsum("stn,cn->stc", value_term, ff_gain, precision=high)
    forcing = -jnp.einsum("stc,nc->stn", controls, input_map, precision=high)
    positions = device * seg_steps + jnp.arange(seg_steps, dtype=jnp.int32)
    start_flag = jnp.any(positions[None, :, None] == starts[:, None, :], axis=-1).astype(
        jnp.float32
    )
    init_image = jnp.dot(x_init, dynamics.T, precision=high)
    driven = forcing + start_flag[:, :, None] * init_image[:, None, :]
    states = run_chain(driven, starts, forward_powers, False, local_levels, device_levels)
    offset = states - ref_traj
    local_cost = jnp.sum(cost_weights * offset * offset, axis=(1, 2)) * (0.5 / total)
    cost = lax.psum(local_cost, "tm")
    adjoint = run_chain(cost_weights * offset, mirrored, squares, True, local_levels, device_levels)
    pulled = jnp.einsum("stn,nc->stc", adjoint, input_map, precision=high)
    source = -jnp.einsum("stc,cn->stn", pulled, ff_gain, precision=high)
    value_adjoint = run_chain(source, starts, forward_powers, False, local_levels, device_levels)
    weight_grad = 0.5 * offset * offset + ref_traj * value_adjoint
    return (states, weight_grad, cost)


def solution(mesh):
    placed = (
        P("groups", "tm", None),
        P("groups", "tm", None),
        P("groups", None),
        P(),
        P(),
        P(),
        P(),
        P(),
        P("groups", None),
    )
    return jax.shard_map(
        per_device,
        mesh=mesh,
        in_specs=placed,
        out_specs=(P("groups", "tm", None), P("groups", "tm", None), P("groups")),
        check_vma=False,
    )
```

profile of v0, /device:TPU:0, one launch (start us, length us, event | category | flops | bytes accessed | tf_op | source)
XLA Modules:
  0.0 228.4 jit_solution(11940536303902532036)
XLA Ops:
  0.7 0.6 copy-done.79
  2.7 0.7 copy-done.78
  3.3 0.7 copy-done.66
  9.9 34.9 %all-reduce.38 = (f32[64]{0:T(128)S(1)}, f32[64]{0:T(128)S(1)}) all-reduce(f32[64]{0:T(128)S(1)} %dynamic-update-slice, f32[64]{0:T(128)S(1)} %dynamic-update-slice.1), channel_id=2, replica_groups=mesh['groups'=2,'tm'=16] {'tm'}, use_global_device_ids=true, to_apply=%add.36 | all-reduce | flops 128 | bytes 1024
  47.5 0.7 copy.317
  49.6 0.9 convolution_bitcast_fusion.2
  54.7 0.8 rev.22
  55.4 0.8 slice.317
  56.4 1.3 fusion.23
  59.8 17.5 %all-gather.1 = f32[64,1,256]{2,1,0:T(1,128)S(1)} all-gather(f32[4,1,256]{2,1,0:T(1,128)S(1)} %slice.420), channel_id=3, replica_groups=mesh['groups'=2,'tm'=16] {'tm'}, dimensions={0}, use_global_device_ids=true | all-gather | bytes 69632 | tf_op jit(solution)/shard_map/all_gather | solution.py:55
  81.0 0.9 fusion.68
  81.9 2.5 %concatenate.103 = f32[4,64,256]{2,1,0:T(8,128)S(1)} concatenate(f32[4,1,256]{2,1,0:T(1,128)} %copy-done.14, f32[4,1,256]{2,1,0:T(1,128)} %copy-done.16, f32[4,2,256]{2,1,0:T(2,128)} %copy-done.12, f32[4,4,256]{2,1,0:T(4,128)S(1)} %fusion.104, f32[4,8,256]{2,1,0:T(8,128)S(1)} %fusion.92, f32[4,16,256]{2,1,0:T(8,128)} %copy-done.6, f32[4,32,256]{2,1,0:T(8,128)} %fusion.68), dimensions={1} | concatenate | bytes 524288 | tf_op jit(solution)/shard_map/concatenate | solution.py:77
  84.4 1.5 multiply_add_fusion.2
  85.9 1.0 rev.25
  90.2 0.6 copy-done.25
  91.3 0.6 copy-done.22
  92.4 0.6 copy-done.19
  93.5 19.2 %all-gather.3 = f32[64,1,256]{2,1,0:T(1,128)S(1)} all-gather(f32[4,1,256]{2,1,0:T(1,128)S(1)} %slice.441), channel_id=5, replica_groups=mesh['groups'=2,'tm'=16] {'tm'}, dimensions={0}, use_global_device_ids=true | all-gather | bytes 69632 | tf_op jit(solution)/shard_map/all_gather | solution.py:55
  113.6 0.7 copy-done.52
  114.7 0.7 copy-done.56
  115.7 0.6 copy-done.61
  119.4 1.1 fusion.65
  120.5 3.5 %concatenate.109 = f32[4,64,256]{2,1,0:T(8,128)} concatenate(f32[4,1,256]{2,1,0:T(1,128)S(1)} %reshape.528, f32[4,1,256]{2,1,0:T(1,128)S(1)} %reshape.529, f32[4,2,256]{2,1,0:T(2,128)S(1)} %copy.331, f32[4,4,256]{2,1,0:T(4,128)S(1)} %fusion.101, f32[4,8,256]{2,1,0:T(8,128)S(1)} %fusion.89, f32[4,16,256]{2,1,0:T(8,128)S(1)} %fusion.77, f32[4,32,256]{2,1,0:T(8,128)} %fusion.65), dimensions={1} | concatenate | bytes 524288 | tf_op jit(solution)/shard_map/concatenate | solution.py:77
  124.0 1.9 multiply_reduce_fusion
  125.9 30.3 %psum.7 = f32[4]{0:T(128)} all-reduce(f32[4]{0:T(128)S(1)} %broadcast_multiply_fusion), channel_id=1, replica_groups=mesh['groups'=2,'tm'=16] {'tm'}, use_global_device_ids=true, to_apply=%region_4.7 | all-reduce | flops 4 | bytes 32 | tf_op jit(solution)/shard_map/psum | solution.py:115
  156.3 0.8 rev.26
  157.0 0.8 slice.378
  158.0 1.3 fusion.11
  161.5 0.7 copy-done.36
  162.5 0.7 copy-done.34
  163.6 17.5 %all-gather.4 = f32[64,1,256]{2,1,0:T(1,128)S(1)} all-gather(f32[4,1,256]{2,1,0:T(1,128)S(1)} %slice.456), channel_id=6, replica_groups=mesh['groups'=2,'tm'=16] {'tm'}, dimensions={0}, use_global_device_ids=true | all-gather | bytes 69632 | tf_op jit(solution)/shard_map/all_gather | solution.py:55
  181.3 0.6 copy-done.71
  182.1 0.7 copy-done.55
  183.1 0.7 copy-done.59
  184.0 0.7 copy-done.64
  187.8 0.9 fusion.62
  188.7 2.5 %concatenate.115 = f32[4,64,256]{2,1,0:T(8,128)S(1)} concatenate(f32[4,1,256]{2,1,0:T(1,128)} %copy-done.15, f32[4,1,256]{2,1,0:T(1,128)} %copy-done.17, f32[4,2,256]{2,1,0:T(2,128)} %copy-done.13, f32[4,4,256]{2,1,0:T(4,128)S(1)} %fusion.98, f32[4,8,256]{2,1,0:T(8,128)S(1)} %fusion.86, f32[4,16,256]{2,1,0:T(8,128)} %copy-done.7, f32[4,32,256]{2,1,0:T(8,128)} %fusion.62), dimensions={1} | concatenate | bytes 524288 | tf_op jit(solution)/shard_map/concatenate | solution.py:77
  191.2 1.5 multiply_add_fusion
  192.7 1.0 rev.28
  197.0 0.6 copy-done.26
  198.1 0.6 copy-done.23
  199.2 0.6 copy-done.20
  200.3 19.2 %all-gather.5 = f32[64,1,256]{2,1,0:T(1,128)S(1)} all-gather(f32[4,1,256]{2,1,0:T(1,128)S(1)} %slice.471), channel_id=7, replica_groups=mesh['groups'=2,'tm'=16] {'tm'}, dimensions={0}, use_global_device_ids=true | all-gather | bytes 69632 | tf_op jit(solution)/shard_map/all_gather | solution.py:55
  220.4 0.7 copy-done.53
  221.5 0.7 copy-done.57
  222.5 0.6 copy-done.62
  226.7 0.9 copy-done.3
  227.6 0.8 fusion.46
  (344 shorter events, 45.6 us)
Async XLA Ops:
  0.6 47.6 %copy-start = (f32[3,64,64]{2,1,0:T(8,128)S(1)}, f32[3,64,64]{2,1,0:T(8,128)}, u32[]{:S(2)}) copy-start(f32[3,64,64]{2,1,0:T(8,128)} %param.17) | copy-start | bytes 147460
  2.6 74.9 %copy-start.70 = (f32[16]{0:T(128)}, f32[16]{0:T(128)S(1)}, u32[]{:S(2)}) copy-start(f32[16]{0:T(128)S(1)} %compare_convert_fusion.1) | copy-start | bytes 196
  2.6 43.0 %copy-start.67 = (f32[16]{0:T(128)}, f32[16]{0:T(128)S(1)}, u32[]{:S(2)}) copy-start(f32[16]{0:T(128)S(1)} %compare_convert_fusion) | copy-start | bytes 196
  2.7 0.7 copy-start.78
  3.3 0.7 copy-start.66
  4.3 51.9 %copy-start.50 = (f32[4,64]{1,0:T(4,128)}, f32[4,64]{1,0:T(4,128)S(1)}, u32[]{:S(2)}) copy-start(f32[4,64]{1,0:T(4,128)S(1)} %convert_subtract_fusion) | copy-start | bytes 3076
  4.4 53.3 %copy-start.41 = (f32[4,64]{1,0:T(4,128)}, f32[4,64]{1,0:T(4,128)S(1)}, u32[]{:S(2)}) copy-start(f32[4,64]{1,0:T(4,128)S(1)} %pad_multiply_fusion.11) | copy-start | bytes 3076
  4.5 53.7 %copy-start.39 = (f32[4,64]{1,0:T(4,128)}, f32[4,64]{1,0:T(4,128)S(1)}, u32[]{:S(2)}) copy-start(f32[4,64]{1,0:T(4,128)S(1)} %pad_multiply_fusion.10) | copy-start | bytes 3076
  4.6 54.0 %copy-start.37 = (f32[4,64]{1,0:T(4,128)}, f32[4,64]{1,0:T(4,128)S(1)}, u32[]{:S(2)}) copy-start(f32[4,64]{1,0:T(4,128)S(1)} %pad_multiply_fusion.9) | copy-start | bytes 3076
  4.6 54.4 %copy-start.35 = (f32[4,64]{1,0:T(4,128)}, f32[4,64]{1,0:T(4,128)S(1)}, u32[]{:S(2)}) copy-start(f32[4,64]{1,0:T(4,128)S(1)} %pad_multiply_fusion.8) | copy-start | bytes 3076
  4.7 54.7 %copy-start.33 = (f32[4,64]{1,0:T(4,128)}, f32[4,64]{1,0:T(4,128)S(1)}, u32[]{:S(2)}) copy-start(f32[4,64]{1,0:T(4,128)S(1)} %pad_multiply_fusion.7) | copy-start | bytes 3076
  45.3 32.7 %copy-start.58 = (f32[4,1,4]{2,1,0:T(1,128)}, f32[4,1,4]{2,1,0:T(1,128)S(1)}, u32[]{:S(2)}) copy-start(f32[4,1,4]{2,1,0:T(1,128)S(1)} %get-tuple-element.34) | copy-start | bytes 196
  45.3 32.9 %copy-start.63 = (f32[2,1,4]{2,1,0:T(1,128)}, f32[2,1,4]{2,1,0:T(1,128)S(1)}, u32[]{:S(2)}) copy-start(f32[2,1,4]{2,1,0:T(1,128)S(1)} %get-tuple-element.38) | copy-start | bytes 100
  45.3 33.1 %copy-start.75 = (f32[4]{0:T(128)}, f32[4]{0:T(128)S(1)}, u32[]{:S(2)}) copy-start(f32[4]{0:T(128)S(1)} %slice_bitcast_fusion.25) | copy-start | bytes 52
  45.4 32.2 %copy-start.54 = (f32[8,1,4]{0,2,1:T(4,128)}, f32[8,1,4]{0,2,1:T(4,128)S(1)}, u32[]{:S(2)}) copy-start(f32[8,1,4]{0,2,1:T(4,128)S(1)} %copy.299) | copy-start | bytes 388
  48.2 0.7 copy-start.77
  48.9 0.7 copy-start.72
  53.6 1.0 copy-start.1
  53.6 1.0 copy-start.2
  55.4 0.9 copy-start.5
  79.0 1.4 copy-start.14
  79.2 1.1 copy-start.16
  79.5 0.8 copy-start.12
  85.9 1.0 copy-start.10
  86.9 0.8 copy-start.8
  86.9 0.8 copy-start.60
  87.0 0.8 copy-start.65
  89.1 0.7 copy-start.31
  90.2 0.7 copy-start.25
  91.3 0.7 copy-start.22
  113.6 0.7 copy-start.52
  120.5 3.5 %copy-start.44 = (f32[4,64]{1,0:T(4,128)S(1)}, f32[4,64]{1,0:T(4,128)}, u32[]{:S(2)}) copy-start(f32[4,64]{1,0:T(4,128)} %copy-done.43) | copy-start | bytes 3076
  157.0 0.9 copy-start.4
  157.0 1.0 copy-start.51
  158.0 1.4 copy-start.42
  161.4 0.7 copy-start.36
  162.5 0.7 copy-start.34
  182.1 0.7 copy-start.55
  185.7 1.4 copy-start.15
  186.0 1.1 copy-start.17
  186.3 0.8 copy-start.13
  192.7 1.0 copy-start.9
  193.7 0.8 copy-start.11
  195.9 0.7 copy-start.32
  197.0 0.7 copy-start.26
  220.3 0.7 copy-start.53
  226.6 1.0 copy-start.3
  226.6 0.9 copy-start.45
  (32 other events, 20.2 us)
where the time goes:
time: 230 us; the launch traced here: 228 us
  blocking collectives  139 us (60%)
  local copies, waits for them, and re-layouts  44.1 us (19%)
  matrix products  32.4 us (14%)
  other arithmetic  10.2 us (4%)
  between operations  3.01 us (1%)
    all_gather x4, blocking collectives, run_chain(): lax.all_gather(last_value[None], 'tm', axis=0, tiled=True)  73.5 us
    unnamed x1, blocking collectives  34.9 us
    psum x1, blocking collectives, per_device(): cost = lax.psum(local_cost, 'tm')  30.3 us
    unnamed x165, local copies, waits for them, and re-layouts  27.1 us
    dot_general x68, matrix products, row_times(): jnp.dot(values.reshape(-1, width), matrix, precision=lax.Precision.HIGHEST)  25.8 us
    concatenate x12, local copies, waits for them, and re-layouts, run_chain(): table = jnp.concatenate([table, row_times(table, powers[level])], axis=1)  8.84 us

commit v1 on v0

--- a/solution.py
+++ b/solution.py
@@ -27,7 +27,7 @@
     return flat.reshape(values.shape)
 
 
-def run_chain(inputs, frame_starts, powers, backward, local_levels, device_levels):
+def run_chain(inputs, frame_starts, powers, backward, local_levels, device_levels, extra=None):
     scen_count, seg_steps, width = inputs.shape
     devices = lax.axis_size("tm")
     device = lax.axis_index("tm")
@@ -50,14 +50,20 @@
         values = values + flags[:, :, None] * row_times(prior_values, powers[level])
         flags = flags * prior_flags
     last_value = values[:, -1]
-    last_flag = flags[:, -1]
-    all_values, all_flags = (
-        lax.all_gather(last_value[None], "tm", axis=0, tiled=True),
-        lax.all_gather(last_flag[None], "tm", axis=0, tiled=True),
-    )
+    if extra is None:
+        all_values = lax.all_gather(last_value[None], "tm", axis=0, tiled=True)
+        gathered_extra = None
+    else:
+        lanes = jnp.broadcast_to(extra[:, None], (scen_count, 128))
+        packed = jnp.concatenate([last_value, lanes], axis=1)
+        gathered = lax.all_gather(packed[None], "tm", axis=0, tiled=True)
+        all_values = gathered[:, :, :width]
+        gathered_extra = gathered[:, :, width]
+    seg_lo = jnp.arange(devices, dtype=jnp.int32)[:, None, None] * seg_steps
+    inside = (frame_starts[None] >= seg_lo) & (frame_starts[None] < seg_lo + seg_steps)
+    all_flags = 1.0 - jnp.any(inside, axis=-1).astype(jnp.float32)
     if backward:
         all_values = all_values[::-1]
-        all_flags = all_flags[::-1]
     roll_by = devices - frame_device
     all_values = jnp.roll(all_values, roll_by, axis=0)
     all_flags = jnp.roll(all_flags, roll_by, axis=0)
@@ -78,7 +84,9 @@
     result = values + flags[:, :, None] * table
     if backward:
         result = result[:, ::-1]
-    return result
+    if extra is None:
+        return result
+    return result, gathered_extra
 
 
 def per_device(ref_traj, cost_weights, x_init, decay, coupling, links, input_map, ff_gain, lengths):
@@ -112,8 +120,10 @@
     states = run_chain(driven, starts, forward_powers, False, local_levels, device_levels)
     offset = states - ref_traj
     local_cost = jnp.sum(cost_weights * offset * offset, axis=(1, 2)) * (0.5 / total)
-    cost = lax.psum(local_cost, "tm")
-    adjoint = run_chain(cost_weights * offset, mirrored, squares, True, local_levels, device_levels)
+    adjoint, all_costs = run_chain(
+        cost_weights * offset, mirrored, squares, True, local_levels, device_levels, local_cost
+    )
+    cost = jnp.sum(all_costs, axis=0)
     pulled = jnp.einsum("stn,nc->stc", adjoint, input_map, precision=high)
     source = -jnp.einsum("stc,cn->stn", pulled, ff_gain, precision=high)
     value_adjoint = run_chain(source, starts, forward_powers, False, local_levels, device_levels)

time: 230 us -> 167 us (0.73)
  blocking collectives: 139 us -> 78 us
  local copies, waits for them, and re-layouts: 44.1 us -> 40.9 us
    unnamed x1 -> x0, blocking collectives: 34.9 us -> none
    psum x1 -> x0, blocking collectives: 30.3 us -> none  [per_device(): cost = lax.psum(local_cost, 'tm')]
    all_gather x4, blocking collectives: 73.5 us -> 78 us  [the longest x3 58.7 us: run_chain(): all_values = lax.all_gather(last_value[None], 'tm', axis=0, tiled=True)]
    unnamed x165 -> x155, local copies, waits for them, and re-layouts: 27.1 us -> 24.6 us
where the time goes in v1:
time: 167 us; the launch traced here: 165 us
  blocking collectives  78 us (47%)
  local copies, waits for them, and re-layouts  40.9 us (24%)
  matrix products  32.3 us (19%)
  other arithmetic  12 us (7%)
  between operations  2.32 us (1%)
    all_gather x3, blocking collectives, run_chain(): all_values = lax.all_gather(last_value[None], 'tm', axis=0, tiled=True)  58.7 us
    dot_general x68, matrix products, row_times(): jnp.dot(values.reshape(-1, width), matrix, precision=lax.Precision.HIGHEST)  25.8 us
    unnamed x155, local copies, waits for them, and re-layouts  24.6 us
    all_gather x1, blocking collectives, run_chain(): gathered = lax.all_gather(packed[None], 'tm', axis=0, tiled=True)  19.2 us
    concatenate x12, local copies, waits for them, and re-layouts, run_chain(): table = jnp.concatenate([table, row_times(table, powers[level])], axis=1)  8.84 us
    dot_general x9, matrix products, per_device(): squares.append(jnp.dot(squares[-1], squares[-1], precision=high))  3.4 us

profile of v1, /device:TPU:0, one launch (start us, length us, event | category | flops | bytes accessed | tf_op | source)
XLA Modules:
  0.0 165.5 jit_solution(11104437400287315871)
XLA Ops:
  0.8 0.7 copy-done.76
  1.5 0.7 copy-done.64
  5.9 0.7 pad_multiply_fusion
  6.6 0.7 pad_multiply_fusion.6
  11.7 0.9 convolution_bitcast_fusion.2
  16.8 0.8 rev.18
  17.6 0.8 slice.315
  18.5 1.3 fusion.23
  22.0 23.4 %all-gather = f32[64,1,256]{2,1,0:T(1,128)S(1)} all-gather(f32[4,1,256]{2,1,0:T(1,128)S(1)} %slice.418), channel_id=2, replica_groups=mesh['groups'=2,'tm'=16] {'tm'}, dimensions={0}, use_global_device_ids=true | all-gather | bytes 69632 | tf_op jit(solution)/shard_map/all_gather | solution.py:54
  49.0 0.9 fusion.68
  50.0 2.5 %concatenate.106 = f32[4,64,256]{2,1,0:T(8,128)S(1)} concatenate(f32[4,1,256]{2,1,0:T(1,128)} %copy-done.14, f32[4,1,256]{2,1,0:T(1,128)} %copy-done.16, f32[4,2,256]{2,1,0:T(2,128)} %copy-done.12, f32[4,4,256]{2,1,0:T(4,128)S(1)} %fusion.104, f32[4,8,256]{2,1,0:T(8,128)S(1)} %fusion.92, f32[4,16,256]{2,1,0:T(8,128)} %copy-done.6, f32[4,32,256]{2,1,0:T(8,128)} %fusion.68), dimensions={1} | concatenate | bytes 524288 | tf_op jit(solution)/shard_map/concatenate | solution.py:83
  52.5 1.5 multiply_add_fusion.2
  54.0 1.0 rev.20
  58.3 0.6 copy-done.25
  59.4 0.6 copy-done.22
  60.5 0.6 copy-done.19
  61.6 17.6 %all-gather.1 = f32[64,1,256]{2,1,0:T(1,128)S(1)} all-gather(f32[4,1,256]{2,1,0:T(1,128)S(1)} %slice.439), channel_id=3, replica_groups=mesh['groups'=2,'tm'=16] {'tm'}, dimensions={0}, use_global_device_ids=true | all-gather | bytes 69632 | tf_op jit(solution)/shard_map/all_gather | solution.py:54
  79.4 0.6 copy-done.66
  81.2 0.7 copy-done.54
  82.2 0.7 copy-done.59
  86.0 1.1 fusion.65
  87.0 3.5 %concatenate.112 = f32[4,64,256]{2,1,0:T(8,128)} concatenate(f32[4,1,256]{2,1,0:T(1,128)S(1)} %reshape.543, f32[4,1,256]{2,1,0:T(1,128)S(1)} %reshape.544, f32[4,2,256]{2,1,0:T(2,128)S(1)} %copy.274, f32[4,4,256]{2,1,0:T(4,128)S(1)} %fusion.101, f32[4,8,256]{2,1,0:T(8,128)S(1)} %fusion.89, f32[4,16,256]{2,1,0:T(8,128)S(1)} %fusion.77, f32[4,32,256]{2,1,0:T(8,128)} %fusion.65), dimensions={1} | concatenate | bytes 524288 | tf_op jit(solution)/shard_map/concatenate | solution.py:83
  90.5 1.9 %multiply_reduce_fusion = (f32[4]{0:T(128)S(1)}, f32[4,64,256]{2,1,0:T(8,128)S(1)}, f32[4,64,256]{2,1,0:T(8,128)}, f32[4,64,256]{2,1,0:T(8,128)}) fusion(f32[4,64,256]{2,1,0:T(8,128)} %param.14, f32[4,64,256]{2,1,0:T(8,128)S(1)} %copy-done.1, f32[4,64,256]{2,1,0:T(8,128)S(1)} %fusion.12, f32[4,64,256]{2,1,0:T(8,128)} %concatenate.112, f32[4,64]{1,0:T(4,128)S(1)} %copy-done.48), kind=kLoop, calls=%fused_computation.176 | loop fusion | flops 393212 | bytes 1836048 | tf_op jit(solution)/shard_map/reduce_sum | solution.py:122
  92.6 0.8 rev.21
  93.3 0.8 slice.374
  94.3 1.3 fusion.11
  96.8 0.6 copy-done.38
  97.8 0.6 copy-done.36
  98.9 0.6 copy-done.34
  99.9 19.2 %all-gather.4 = f32[16,4,384]{2,1,0:T(4,128)S(1)} all-gather(f32[1,4,384]{2,1,0:T(4,128)S(1)} %maximum_bitcast_fusion), channel_id=4, replica_groups=mesh['groups'=2,'tm'=16] {'tm'}, dimensions={0}, use_global_device_ids=true | all-gather | bytes 104448 | tf_op jit(solution)/shard_map/all_gather | solution.py:59
  119.2 0.6 slice_reduce_fusion
  119.8 0.7 copy-done.69
  120.6 0.7 copy-done.53
  121.6 0.7 copy-done.57
  122.5 0.7 copy-done.62
  126.3 0.9 fusion.62
  127.2 2.5 %concatenate.119 = f32[4,64,256]{2,1,0:T(8,128)S(1)} concatenate(f32[4,1,256]{2,1,0:T(1,128)} %copy-done.15, f32[4,1,256]{2,1,0:T(1,128)} %copy-done.17, f32[4,2,256]{2,1,0:T(2,128)} %copy-done.13, f32[4,4,256]{2,1,0:T(4,128)S(1)} %fusion.98, f32[4,8,256]{2,1,0:T(8,128)S(1)} %fusion.86, f32[4,16,256]{2,1,0:T(8,128)} %copy-done.7, f32[4,32,256]{2,1,0:T(8,128)} %fusion.62), dimensions={1} | concatenate | bytes 524288 | tf_op jit(solution)/shard_map/concatenate | solution.py:83
  129.7 1.5 multiply_add_fusion
  131.2 1.0 rev.23
  135.6 0.6 copy-done.26
  136.7 0.6 copy-done.23
  137.8 0.6 copy-done.20
  138.8 17.7 %all-gather.3 = f32[64,1,256]{2,1,0:T(1,128)S(1)} all-gather(f32[4,1,256]{2,1,0:T(1,128)S(1)} %slice.470), channel_id=5, replica_groups=mesh['groups'=2,'tm'=16] {'tm'}, dimensions={0}, use_global_device_ids=true | all-gather | bytes 69632 | tf_op jit(solution)/shard_map/all_gather | solution.py:54
  156.7 0.6 copy-done.67
  158.5 0.7 copy-done.55
  159.5 0.7 copy-done.60
  163.8 0.9 copy-done.3
  164.7 0.8 fusion.46
  (331 shorter events, 43.0 us)
Async XLA Ops:
  0.6 9.7 %copy-start = (f32[3,64,64]{2,1,0:T(8,128)S(1)}, f32[3,64,64]{2,1,0:T(8,128)}, u32[]{:S(2)}) copy-start(f32[3,64,64]{2,1,0:T(8,128)} %param.17) | copy-start | bytes 147460
  0.7 44.9 %copy-start.68 = (f32[16]{0:T(128)}, f32[16]{0:T(128)S(1)}, u32[]{:S(2)}) copy-start(f32[16]{0:T(128)S(1)} %compare_convert_fusion.1) | copy-start | bytes 196
  0.8 6.6 %copy-start.65 = (f32[16]{0:T(128)}, f32[16]{0:T(128)S(1)}, u32[]{:S(2)}) copy-start(f32[16]{0:T(128)S(1)} %compare_convert_fusion) | copy-start | bytes 196
  0.8 0.7 copy-start.76
  1.5 0.7 copy-start.64
  2.5 15.8 %copy-start.46 = (f32[4,64]{1,0:T(4,128)}, f32[4,64]{1,0:T(4,128)S(1)}, u32[]{:S(2)}) copy-start(f32[4,64]{1,0:T(4,128)S(1)} %convert_subtract_fusion.2) | copy-start | bytes 3076
  2.6 17.2 %copy-start.41 = (f32[4,64]{1,0:T(4,128)}, f32[4,64]{1,0:T(4,128)S(1)}, u32[]{:S(2)}) copy-start(f32[4,64]{1,0:T(4,128)S(1)} %pad_multiply_fusion.11) | copy-start | bytes 3076
  2.7 17.6 %copy-start.39 = (f32[4,64]{1,0:T(4,128)}, f32[4,64]{1,0:T(4,128)S(1)}, u32[]{:S(2)}) copy-start(f32[4,64]{1,0:T(4,128)S(1)} %pad_multiply_fusion.10) | copy-start | bytes 3076
  2.8 17.9 %copy-start.37 = (f32[4,64]{1,0:T(4,128)}, f32[4,64]{1,0:T(4,128)S(1)}, u32[]{:S(2)}) copy-start(f32[4,64]{1,0:T(4,128)S(1)} %pad_multiply_fusion.9) | copy-start | bytes 3076
  2.9 18.3 %copy-start.35 = (f32[4,64]{1,0:T(4,128)}, f32[4,64]{1,0:T(4,128)S(1)}, u32[]{:S(2)}) copy-start(f32[4,64]{1,0:T(4,128)S(1)} %pad_multiply_fusion.8) | copy-start | bytes 3076
  2.9 18.6 %copy-start.33 = (f32[4,64]{1,0:T(4,128)}, f32[4,64]{1,0:T(4,128)S(1)}, u32[]{:S(2)}) copy-start(f32[4,64]{1,0:T(4,128)S(1)} %pad_multiply_fusion.7) | copy-start | bytes 3076
  7.8 38.2 %copy-start.56 = (f32[4,1,4]{2,1,0:T(1,128)}, f32[4,1,4]{2,1,0:T(1,128)S(1)}, u32[]{:S(2)}) copy-start(f32[4,1,4]{2,1,0:T(1,128)S(1)} %get-tuple-element.34) | copy-start | bytes 196
  7.8 38.5 %copy-start.61 = (f32[2,1,4]{2,1,0:T(1,128)}, f32[2,1,4]{2,1,0:T(1,128)S(1)}, u32[]{:S(2)}) copy-start(f32[2,1,4]{2,1,0:T(1,128)S(1)} %get-tuple-element.38) | copy-start | bytes 100
  7.8 38.7 %copy-start.73 = (f32[4]{0:T(128)}, f32[4]{0:T(128)S(1)}, u32[]{:S(2)}) copy-start(f32[4]{0:T(128)S(1)} %slice_bitcast_fusion.25) | copy-start | bytes 52
  7.9 37.8 %copy-start.52 = (f32[8,1,4]{0,2,1:T(4,128)}, f32[8,1,4]{0,2,1:T(4,128)S(1)}, u32[]{:S(2)}) copy-start(f32[8,1,4]{0,2,1:T(4,128)S(1)} %copy.244) | copy-start | bytes 388
  10.3 0.7 copy-start.75
  11.0 0.7 copy-start.70
  15.7 1.0 copy-start.1
  15.7 1.0 copy-start.2
  17.6 0.9 copy-start.5
  47.0 1.4 copy-start.14
  47.3 1.1 copy-start.16
  47.6 0.8 copy-start.12
  54.0 1.0 copy-start.10
  55.0 0.8 copy-start.8
  55.0 0.8 copy-start.58
  55.0 0.8 copy-start.63
  55.8 0.7 copy-start.44
  56.5 0.7 copy-start.28
  59.4 0.7 copy-start.22
  87.0 3.5 %copy-start.48 = (f32[4,64]{1,0:T(4,128)S(1)}, f32[4,64]{1,0:T(4,128)}, u32[]{:S(2)}) copy-start(f32[4,64]{1,0:T(4,128)} %pad_multiply_fusion) | copy-start | bytes 3076
  93.3 0.9 copy-start.4
  93.3 1.0 copy-start.47
  94.3 1.4 copy-start.42
  95.6 0.7 copy-start.40
  96.7 0.7 copy-start.38
  97.8 0.7 copy-start.36
  121.6 0.7 copy-start.57
  122.5 0.7 copy-start.62
  124.3 1.4 copy-start.15
  124.5 1.1 copy-start.17
  124.8 0.8 copy-start.13
  131.2 1.0 copy-start.9
  132.3 0.8 copy-start.11
  133.1 0.7 copy-start.45
  136.6 0.7 copy-start.23
  163.7 1.0 copy-start.3
  163.7 0.9 copy-start.49
  (29 other events, 18.7 us)

commit v2 on v1

v2 whole, which is shorter than its diff:
```python
import functools

import jax
import jax.numpy as jnp
from jax import lax
from jax.experimental import pallas as pl
from jax.experimental.pallas import tpu as pltpu
from jax.sharding import PartitionSpec as P

HIGH = lax.Precision.HIGHEST


def build_dynamics(decay, coupling, links):
    size = decay.shape[0]
    width = coupling.shape[1]
    lanes = jnp.arange(size, dtype=jnp.int32)
    offsets = jnp.arange(width, dtype=jnp.int32)
    row_hot = (lanes[None, :, None] == links[:, 0:1, None] * width + offsets[None, None, :]).astype(
        jnp.float32
    )
    col_hot = (lanes[None, :, None] == links[:, 1:2, None] * width + offsets[None, None, :]).astype(
        jnp.float32
    )
    placed = jnp.einsum(
        "lia,lab,ljb->ij", row_hot, coupling, col_hot, precision=lax.Precision.HIGHEST
    )
    return jnp.diag(decay) + placed


def row_times(values, matrix):
    width = values.shape[-1]
    flat = jnp.dot(values.reshape(-1, width), matrix, precision=lax.Precision.HIGHEST)
    return flat.reshape(values.shape)


def _dot(a, b):
    return jnp.dot(a, b, precision=HIGH, preferred_element_type=jnp.float32)


def _scan(v, cut, pw_ref, seg, backward, carry=None):
    rows, width = v.shape
    scen = rows // seg
    t = lax.broadcasted_iota(jnp.int32, (rows, width), 0) % seg
    flags = 1.0 - cut
    if carry is not None:
        pushed = _dot(carry, pw_ref[0])
        pushed = jnp.broadcast_to(pushed[:, None, :], (scen, seg, width)).reshape(rows, width)
        first = t == (seg - 1 if backward else 0)
        v = v + jnp.where(first, flags * pushed, 0.0)
    levels = pw_ref.shape[0]
    for level in range(levels):
        stride = 2**level
        if backward:
            prior_v = pltpu.roll(v, rows - stride, 0)
            prior_f = pltpu.roll(flags, rows - stride, 0)
            valid = t < seg - stride
        else:
            prior_v = pltpu.roll(v, stride, 0)
            prior_f = pltpu.roll(flags, stride, 0)
            valid = t >= stride
        prior_v = jnp.where(valid, prior_v, 0.0)
        prior_f = jnp.where(valid, prior_f, 1.0)
        v = v + flags * _dot(prior_v, pw_ref[level])
        flags = flags * prior_f
    return v


def _ends(v, seg, backward):
    rows, width = v.shape
    scen = rows // seg
    pick = lax.broadcasted_iota(jnp.int32, (scen, rows), 1)
    want = lax.broadcasted_iota(jnp.int32, (scen, rows), 0) * seg + (0 if backward else seg - 1)
    sel = (pick == want).astype(jnp.float32)
    return _dot(sel, v)


def _vmem(count):
    return [pl.BlockSpec(memory_space=pltpu.VMEM)] * count


def _call(kernel, outs, *args):
    return pl.pallas_call(
        kernel,
        out_shape=outs,
        in_specs=_vmem(len(args)),
        out_specs=tuple(_vmem(len(outs))),
    )(*args)


def k_first(seg, cw_ref, ref_ref, end_ref, pwb_ref, w1_ref, e1_ref):
    width = cw_ref.shape[1]
    cut = jnp.broadcast_to(end_ref[...], cw_ref.shape)
    w1 = cw_ref[...] * ref_ref[...]
    w1_ref[...] = w1
    e1_ref[...] = _ends(_scan(w1, cut, pwb_ref, seg, True), seg, True)


def k_states_in(seg, w1_ref, end_ref, start_ref, c1_ref, init_ref, gain_ref, imap_ref, pwb_ref,
                pwf_ref, d2_ref, e2_ref):
    shape = w1_ref.shape
    cut_e = jnp.broadcast_to(end_ref[...], shape)
    cut_s = jnp.broadcast_to(start_ref[...], shape)
    vt = _scan(w1_ref[...], cut_e, pwb_ref, seg, True, c1_ref[...])
    controls = lax.dot_general(
        vt, gain_ref[...], (((1,), (1,)), ((), ())), precision=HIGH,
        preferred_element_type=jnp.float32)
    forcing = -lax.dot_general(
        controls, imap_ref[...], (((1,), (1,)), ((), ())), precision=HIGH,
        preferred_element_type=jnp.float32)
    rows, width = shape
    scen = rows // seg
    init = jnp.broadcast_to(init_ref[...][:, None, :], (scen, seg, width)).reshape(rows, width)
    d2 = forcing + cut_s * init
    d2_ref[...] = d2
    e2_ref[...] = _ends(_scan(d2, cut_s, pwf_ref, seg, False), seg, False)


def k_adjoint_in(seg, scale, d2_ref, start_ref, end_ref, c2_ref, cw_ref, ref_ref, pwf_ref, pwb_ref,
                 x_ref, w3_ref, e3_ref, cost_ref):
    shape = d2_ref.shape
    rows, width = shape
    scen = rows // seg
    cut_s = jnp.broadcast_to(start_ref[...], shape)
    cut_e = jnp.broadcast_to(end_ref[...], shape)
    states = _scan(d2_ref[...], cut_s, pwf_ref, seg, False, c2_ref[...])
    x_ref[...] = states
    offset = states - ref_ref[...]
    cw = cw_ref[...]
    w3 = cw * offset
    w3_ref[...] = w3
    per_row = jnp.sum(w3 * offset, axis=1, keepdims=True)
    pick = lax.broadcasted_iota(jnp.int32, (scen, rows), 1) // seg
    want = lax.broadcasted_iota(jnp.int32, (scen, rows), 0)
    sel = (pick == want).astype(jnp.float32)
    per_scen = _dot(sel, jnp.broadcast_to(per_row, (rows, 128)))
    cost_ref[...] = per_scen * scale
    e3_ref[...] = _ends(_scan(w3, cut_e, pwb_ref, seg, True), seg, True)


def k_value_adjoint_in(seg, w3_ref, end_ref, start_ref, c3_ref, imap_ref, gain_ref, pwb_ref,
                       pwf_ref, s4_ref, e4_ref):
    shape = w3_ref.shape
    cut_e = jnp.broadcast_to(end_ref[...], shape)
    cut_s = jnp.broadcast_to(start_ref[...], shape)
    adjoint = _scan(w3_ref[...], cut_e, pwb_ref, seg, True, c3_ref[...])
    pulled = _dot(adjoint, imap_ref[...])
    source = -_dot(pulled, gain_ref[...])
    s4_ref[...] = source
    e4_ref[...] = _ends(_scan(source, cut_s, pwf_ref, seg, False), seg, False)


def k_last(seg, s4_ref, start_ref, c4_ref, x_ref, ref_ref, pwf_ref, g_ref):
    shape = s4_ref.shape
    cut_s = jnp.broadcast_to(start_ref[...], shape)
    va = _scan(s4_ref[...], cut_s, pwf_ref, seg, False, c4_ref[...])
    ref = ref_ref[...]
    offset = x_ref[...] - ref
    g_ref[...] = 0.5 * offset * offset + ref * va


def combine(last_value, frame_starts, powers, backward, seg_steps, local_levels, device_levels,
            extra=None):
    scen_count, width = last_value.shape
    devices = lax.axis_size("tm")
    device = lax.axis_index("tm")
    frame_device = devices - 1 - device if backward else device
    if extra is None:
        all_values = lax.all_gather(last_value[None], "tm", axis=0, tiled=True)
        gathered_extra = None
    else:
        lanes = jnp.broadcast_to(extra[:, None], (scen_count, 128))
        packed = jnp.concatenate([last_value, lanes], axis=1)
        gathered = lax.all_gather(packed[None], "tm", axis=0, tiled=True)
        all_values = gathered[:, :, :width]
        gathered_extra = gathered[:, :, width]
    seg_lo = jnp.arange(devices, dtype=jnp.int32)[:, None, None] * seg_steps
    inside = (frame_starts[None] >= seg_lo) & (frame_starts[None] < seg_lo + seg_steps)
    all_flags = 1.0 - jnp.any(inside, axis=-1).astype(jnp.float32)
    if backward:
        all_values = all_values[::-1]
    roll_by = devices - frame_device
    all_values = jnp.roll(all_values, roll_by, axis=0)
    all_flags = jnp.roll(all_flags, roll_by, axis=0)
    keep = (jnp.arange(devices, dtype=jnp.int32) >= roll_by).astype(jnp.float32)
    all_values = all_values * keep[:, None, None]
    all_flags = all_flags * keep[:, None] + (1.0 - keep[:, None])
    for level in range(device_levels):
        half = all_values.shape[0] // 2
        paired_values = all_values.reshape(half, 2, scen_count, width)
        paired_flags = all_flags.reshape(half, 2, scen_count)
        moved = row_times(paired_values[:, 0], powers[local_levels + level])
        all_values = paired_flags[:, 1, :, None] * moved + paired_values[:, 1]
        all_flags = paired_flags[:, 0] * paired_flags[:, 1]
    return all_values[0], gathered_extra


def per_device(ref_traj, cost_weights, x_init, decay, coupling, links, input_map, ff_gain, lengths):
    scen_count, seg_steps, width = ref_traj.shape
    rows = scen_count * seg_steps
    devices = lax.axis_size("tm")
    device = lax.axis_index("tm")
    total = seg_steps * devices
    dynamics = build_dynamics(decay, coupling, links)
    local_levels = seg_steps.bit_length() - 1
    device_levels = (devices - 1).bit_length()
    power_count = local_levels + max(device_levels, 1)
    squares = [dynamics]
    for level in range(power_count - 1):
        squares.append(jnp.dot(squares[-1], squares[-1], precision=HIGH))
    forward_powers = [matrix.T for matrix in squares]
    pwb = jnp.stack(squares[:local_levels])
    pwf = jnp.stack(forward_powers[:local_levels])
    ends_incl = jnp.cumsum(lengths, axis=1)
    starts = ends_incl - lengths
    mirrored = total - ends_incl
    positions = device * seg_steps + jnp.arange(seg_steps, dtype=jnp.int32)
    start_flag = jnp.any(positions[None, :, None] == starts[:, None, :], axis=-1)
    end_flag = jnp.any(positions[None, :, None] + 1 == ends_incl[:, None, :], axis=-1)
    start_col = start_flag.astype(jnp.float32).reshape(rows, 1)
    end_col = end_flag.astype(jnp.float32).reshape(rows, 1)
    init_image = jnp.dot(x_init, dynamics.T, precision=HIGH)
    cw = cost_weights.reshape(rows, width)
    ref = ref_traj.reshape(rows, width)
    f32 = jnp.float32
    full = jax.ShapeDtypeStruct((rows, width), f32)
    ends = jax.ShapeDtypeStruct((scen_count, width), f32)
    seg = seg_steps

    w1, e1 = _call(functools.partial(k_first, seg), (full, ends), cw, ref, end_col, pwb)
    c1, _ = combine(e1, mirrored, squares, True, seg, local_levels, device_levels)
    d2, e2 = _call(
        functools.partial(k_states_in, seg), (full, ends),
        w1, end_col, start_col, c1, init_image, ff_gain, input_map, pwb, pwf)
    c2, _ = combine(e2, starts, forward_powers, False, seg, local_levels, device_levels)
    cost_shape = jax.ShapeDtypeStruct((scen_count, 128), f32)
    states, w3, e3, cost_part = _call(
        functools.partial(k_adjoint_in, seg, 0.5 / total), (full, full, ends, cost_shape),
        d2, start_col, end_col, c2, cw, ref, pwf, pwb)
    c3, all_costs = combine(
        e3, mirrored, squares, True, seg, local_levels, device_levels, cost_part[:, 0])
    cost = jnp.sum(all_costs, axis=0)
    s4, e4 = _call(
        functools.partial(k_value_adjoint_in, seg), (full, ends),
        w3, end_col, start_col, c3, input_map, ff_gain, pwb, pwf)
    c4, _ = combine(e4, starts, forward_powers, False, seg, local_levels, device_levels)
    (grad,) = _call(
        functools.partial(k_last, seg), (full,), s4, start_col, c4, states, ref, pwf)
    shape3 = (scen_count, seg_steps, width)
    return (states.reshape(shape3), grad.reshape(shape3), cost)


def solution(mesh):
    placed = (
        P("groups", "tm", None),
        P("groups", "tm", None),
        P("groups", None),
        P(),
        P(),
        P(),
        P(),
        P(),
        P("groups", None),
    )
    return jax.shard_map(
        per_device,
        mesh=mesh,
        in_specs=placed,
        out_specs=(P("groups", "tm", None), P("groups", "tm", None), P("groups")),
        check_vma=False,
    )
```

time: 167 us -> 162 us (0.970)
  Pallas kernels: 0 us -> 40.8 us
  local copies, waits for them, and re-layouts: 40.9 us -> 13.8 us
  matrix products: 32.3 us -> 20.4 us
  other arithmetic: 12 us -> 5.77 us
    pallas_call x0 -> x5, Pallas kernels: none -> 40.8 us  [_call(): pl.pallas_call(kernel, out_shape=outs, in_specs=_vmem(len(args)), out_spe...]
    unnamed x155 -> x23, local copies, waits for them, and re-layouts: 24.6 us -> 4.29 us
    dot_general x68 -> x16, matrix products: 25.8 us -> 6.92 us  [row_times(): jnp.dot(values.reshape(-1, width), matrix, precision=lax.Precision.HIGHEST)]
    concatenate x12 -> x0, local copies, waits for them, and re-layouts: 8.84 us -> none  [run_chain(): table = jnp.concatenate([table, row_times(table, powers[level])], axis=1)]
    dot_general x14 -> x10, matrix products: 5.73 us -> 12.7 us  [the longest x9 11 us: per_device(): squares.append(jnp.dot(squares[-1], squares[-1], precision=HIGH))]
    dot_general x4 -> x6, local copies, waits for them, and re-layouts: 0.05 us -> 5.5 us  [the longest x5 4.66 us: per_device(): squares.append(jnp.dot(squares[-1], squares[-1], precision=HIGH))]
    add x7 -> x3, other arithmetic: 3.95 us -> 0.16 us  [the longest x2 0.15 us: combine(): all_flags = all_flags * keep[:, None] + (1.0 - keep[:, None])]
    rev x6 -> x2, local copies, waits for them, and re-layouts: 3.56 us -> 0.01 us  [combine(): all_values = all_values[::-1]]
where the time goes in v2:
time: 162 us; the launch traced here: 161 us
  blocking collectives  78.8 us (49%)
  Pallas kernels  40.8 us (25%)
  matrix products  20.4 us (13%)
  local copies, waits for them, and re-layouts  13.8 us (9%)
  other arithmetic  5.77 us (4%)
    all_gather x3, blocking collectives, combine(): all_values = lax.all_gather(last_value[None], 'tm', axis=0, tiled=True)  59.6 us
    pallas_call x5, Pallas kernels, _call(): pl.pallas_call(kernel, out_shape=outs, in_specs=_vmem(len(args)), out_spe...  40.8 us
    all_gather x1, blocking collectives, combine(): gathered = lax.all_gather(packed[None], 'tm', axis=0, tiled=True)  19.2 us
    dot_general x9, matrix products, per_device(): squares.append(jnp.dot(squares[-1], squares[-1], precision=HIGH))  11 us
    dot_general x16, matrix products, row_times(): jnp.dot(values.reshape(-1, width), matrix, precision=lax.Precision.HIGHEST)  6.92 us
    dot_general x5, local copies, waits for them, and re-layouts, per_device(): squares.append(jnp.dot(squares[-1], squares[-1], precision=HIGH))  4.66 us
    unnamed x23, local copies, waits for them, and re-layouts  4.29 us

profile of v2, /device:TPU:0, one launch (start us, length us, event | category | flops | bytes accessed | tf_op | source)
XLA Modules:
  0.0 160.8 jit_solution(2344053044493708070)
XLA Ops:
  0.8 0.8 multiply_bitcast_fusion
  1.5 0.9 reduce_window_sum.11
  2.5 0.7 broadcast_subtract_fusion
  4.2 0.8 reshape.387.start_ref
  5.0 0.8 reshape.386.end_ref
  5.8 1.6 copy.180.imap_ref
  7.7 0.5 convolution_bitcast_fusion
  8.2 1.7 %convolution_bitcast_fusion.2.init_ref = f32[4,256]{1,0:T(4,128)} fusion(f32[4,256]{1,0:T(4,128)} %param.15, f32[256,256]{1,0:T(8,128)S(1)} %convolution_bitcast_fusion, f32[256]{0:T(256)} %param.16), kind=kOutput, calls=%fused_computation.36 | convolution fusion | flops 3342336 | bytes 271360 | tf_op jit(solution)/shard_map/dot_general | solution.py:221
  9.9 0.8 copy.172
  10.7 1.1 bitcast_dynamic-update-slice_fusion.5
  11.8 1.2 bitcast_dynamic-update-slice_fusion.10
  13.0 1.1 copy.173
  14.1 1.4 bitcast_dynamic-update-slice_fusion.9
  15.5 0.8 copy.174
  16.3 1.0 bitcast_dynamic-update-slice_fusion.3
  17.3 1.1 bitcast_dynamic-update-slice_fusion.8
  18.4 1.1 copy.175
  19.5 1.4 bitcast_dynamic-update-slice_fusion.7
  20.9 0.8 copy.176
  21.8 1.0 bitcast_dynamic-update-slice_fusion.1
  22.7 1.4 bitcast_dynamic-update-slice_fusion.6
  24.2 1.2 fusion.61
  25.4 0.8 copy.177
  26.2 1.0 bitcast_dynamic-update-slice_fusion.pwf_ref
  27.2 1.8 %fusion.62 = f32[256,256]{1,0:T(8,128)S(1)} fusion(f32[256,256]{1,0:T(8,128)} %fusion.61), kind=kOutput, calls=%fused_computation.173 | convolution fusion | flops 201326592 | bytes 524288 | tf_op jit(solution)/shard_map/dot_general | solution.py:209
  29.0 0.4 fusion.63
  29.4 0.7 copy-done.3
  30.1 1.1 fusion.64
  31.2 5.4 %shard_map.112 = (f32[256,256]{1,0:T(8,128)}, f32[4,256]{1,0:T(4,128)}) custom-call(f32[256,256]{1,0:T(8,128)} %bitcast.280, f32[256,256]{1,0:T(8,128)} %bitcast.277, f32[256,1]{1,0:T(8,128)} %reshape.386.end_ref, f32[6,256,256]{2,1,0:T(8,128)} %copy-done.1), custom_call_target="tpu_custom_call" | custom-call | tf_op jit(solution)/shard_map/pallas_call | solution.py:82
  36.6 23.6 %all-gather.4 = f32[16,4,256]{2,1,0:T(4,128)S(1)} all-gather(f32[1,4,256]{2,1,0:T(4,128)} %bitcast.312), channel_id=2, replica_groups=mesh['groups'=2,'tm'=16] {'tm'}, dimensions={0}, use_global_device_ids=true | all-gather | bytes 69632 | tf_op jit(solution)/shard_map/all_gather | solution.py:168
  61.2 0.8 fusion.19.c1_ref
  62.0 10.1 %shard_map.113 = (f32[256,256]{1,0:T(8,128)}, f32[4,256]{1,0:T(4,128)}) custom-call(f32[256,256]{1,0:T(8,128)} %get-tuple-element.15.w1_ref, f32[256,1]{1,0:T(8,128)} %reshape.386.end_ref, f32[256,1]{1,0:T(8,128)} %reshape.387.start_ref, f32[4,256]{1,0:T(4,128)} %fusion.19.c1_ref, f32[4,256]{1,0:T(4,128)} %convolution_bitcast_fusion.2.init_ref, ...), custom_call_target="tpu_custom_call" | custom-call | tf_op jit(solution)/shard_map/pallas_call | solution.py:82
  72.2 18.1 %all-gather.5 = f32[16,4,256]{2,1,0:T(4,128)S(1)} all-gather(f32[1,4,256]{2,1,0:T(4,128)} %bitcast.311), channel_id=3, replica_groups=mesh['groups'=2,'tm'=16] {'tm'}, dimensions={0}, use_global_device_ids=true | all-gather | bytes 69632 | tf_op jit(solution)/shard_map/all_gather | solution.py:168
  90.4 0.3 fusion.2
  90.8 0.3 fusion.6
  91.4 0.9 fusion.18.c2_ref
  92.4 9.5 %shard_map.114 = (f32[256,256]{1,0:T(8,128)}, f32[256,256]{1,0:T(8,128)}, f32[4,256]{1,0:T(4,128)}, f32[4,128]{1,0:T(4,128)}) custom-call(f32[256,256]{1,0:T(8,128)} %get-tuple-element.17.d2_ref, f32[256,1]{1,0:T(8,128)} %reshape.387.start_ref, f32[256,1]{1,0:T(8,128)} %reshape.386.end_ref, f32[4,256]{1,0:T(4,128)} %fusion.18.c2_ref, f32[256,256]{1,0:T(8,128)} %bitcast.281, ...), custom_call_target="tpu_custom_call" | custom-call | tf_op jit(solution)/shard_map/pallas_call | solution.py:82
  101.8 0.8 slice_reduce_fusion.1
  102.7 0.7 maximum_bitcast_fusion
  103.4 19.2 %all-gather.6 = f32[16,4,384]{2,1,0:T(4,128)S(1)} all-gather(f32[1,4,384]{2,1,0:T(4,128)S(1)} %maximum_bitcast_fusion), channel_id=4, replica_groups=mesh['groups'=2,'tm'=16] {'tm'}, dimensions={0}, use_global_device_ids=true | all-gather | bytes 104448 | tf_op jit(solution)/shard_map/all_gather | solution.py:173
  122.6 0.6 slice_reduce_fusion
  124.2 0.8 fusion.17.c3_ref
  125.0 10.1 %shard_map.115 = (f32[256,256]{1,0:T(8,128)}, f32[4,256]{1,0:T(4,128)}) custom-call(f32[256,256]{1,0:T(8,128)} %get-tuple-element.20.w3_ref, f32[256,1]{1,0:T(8,128)} %reshape.386.end_ref, f32[256,1]{1,0:T(8,128)} %reshape.387.start_ref, f32[4,256]{1,0:T(4,128)} %fusion.17.c3_ref, f32[256,64]{1,0:T(8,128)} %copy.180.imap_ref, f32[64,256]{1,0:T(8,128)} %gain_ref.3, ...), custom_call_target="tpu_custom_call" | custom-call | tf_op jit(solution)/shard_map/pallas_call | solution.py:82
  135.1 17.9 %all-gather.7 = f32[16,4,256]{2,1,0:T(4,128)S(1)} all-gather(f32[1,4,256]{2,1,0:T(4,128)} %bitcast.310), channel_id=5, replica_groups=mesh['groups'=2,'tm'=16] {'tm'}, dimensions={0}, use_global_device_ids=true | all-gather | bytes 69632 | tf_op jit(solution)/shard_map/all_gather | solution.py:168
  153.1 0.3 fusion
  153.6 0.3 fusion.4
  154.2 0.9 fusion.16.c4_ref
  155.2 5.7 %shard_map.116 = f32[256,256]{1,0:T(8,128)} custom-call(f32[256,256]{1,0:T(8,128)} %get-tuple-element.23.s4_ref, f32[256,1]{1,0:T(8,128)} %reshape.387.start_ref, f32[4,256]{1,0:T(4,128)} %fusion.16.c4_ref, f32[256,256]{1,0:T(8,128)} %get-tuple-element.19.x_ref, f32[256,256]{1,0:T(8,128)} %bitcast.279, f32[6,256,256]{2,1,0:T(8,128)} %copy-done.2), custom_call_target="tpu_custom_call" | custom-call | tf_op jit(solution)/shard_map/pallas_call | solution.py:82
  (78 shorter events, 4.2 us)
Async XLA Ops:
  0.6 6.7 %copy-start = (f32[3,64,64]{2,1,0:T(8,128)S(1)}, f32[3,64,64]{2,1,0:T(8,128)}, u32[]{:S(2)}) copy-start(f32[3,64,64]{2,1,0:T(8,128)} %param.17) | copy-start | bytes 147460
  0.6 10.1 %copy-start.8 = (f32[256]{0:T(256)S(1)}, f32[256]{0:T(256)}, u32[]{:S(2)}) copy-start(f32[256]{0:T(256)} %param.16) | copy-start | bytes 3076
  20.9 0.9 copy-start.7
  24.2 5.2 %copy-start.1 = (f32[6,256,256]{2,1,0:T(8,128)}, f32[6,256,256]{2,1,0:T(8,128)S(1)}, u32[]{:S(2)}) copy-start(f32[6,256,256]{2,1,0:T(8,128)S(1)} %get-tuple-element.69.pwb_ref) | copy-start | bytes 4718596
  27.2 9.4 %copy-start.2 = (f32[6,256,256]{2,1,0:T(8,128)}, f32[6,256,256]{2,1,0:T(8,128)S(1)}, u32[]{:S(2)}) copy-start(f32[6,256,256]{2,1,0:T(8,128)S(1)} %bitcast_dynamic-update-slice_fusion.pwf_ref) | copy-start | bytes 4718596
  29.4 0.7 copy-start.3
  31.2 29.2 %copy-start.5 = (f32[256,256]{1,0:T(8,128)S(1)}, f32[256,256]{1,0:T(8,128)}, u32[]{:S(2)}) copy-start(f32[256,256]{1,0:T(8,128)} %fusion.61) | copy-start | bytes 786436
  31.2 29.7 %copy-start.4 = (f32[256,256]{1,0:T(8,128)S(1)}, f32[256,256]{1,0:T(8,128)}, u32[]{:S(2)}) copy-start(f32[256,256]{1,0:T(8,128)} %copy-done.3) | copy-start | bytes 786436
  31.2 30.0 %copy-start.6 = (f32[256,256]{1,0:T(8,128)S(1)}, f32[256,256]{1,0:T(8,128)}, u32[]{:S(2)}) copy-start(f32[256,256]{1,0:T(8,128)} %fusion.64) | copy-start | bytes 786436

commit v3 on v2

--- a/solution.py
+++ b/solution.py
@@ -37,17 +37,32 @@
     return jnp.dot(a, b, precision=HIGH, preferred_element_type=jnp.float32)
 
 
-def _scan(v, cut, pw_ref, seg, backward, carry=None):
+def _dot_nt(a, b):
+    return lax.dot_general(
+        a, b, (((1,), (1,)), ((), ())), precision=HIGH, preferred_element_type=jnp.float32)
+
+
+def k_powers(f_ref, out_ref):
+    power = f_ref[...]
+    out_ref[0] = power
+    for level in range(1, out_ref.shape[0]):
+        power = _dot(power, power)
+        out_ref[level] = power
+
+
+def _scan(v, cut, pw_ref, seg, backward, carry=None, levels=None):
     rows, width = v.shape
     scen = rows // seg
     t = lax.broadcasted_iota(jnp.int32, (rows, width), 0) % seg
     flags = 1.0 - cut
+    if levels is None:
+        levels = seg.bit_length() - 1
+    step = _dot if backward else _dot_nt
     if carry is not None:
-        pushed = _dot(carry, pw_ref[0])
+        pushed = step(carry, pw_ref[0])
         pushed = jnp.broadcast_to(pushed[:, None, :], (scen, seg, width)).reshape(rows, width)
         first = t == (seg - 1 if backward else 0)
         v = v + jnp.where(first, flags * pushed, 0.0)
-    levels = pw_ref.shape[0]
     for level in range(levels):
         stride = 2**level
         if backward:
@@ -60,7 +75,7 @@
             valid = t >= stride
         prior_v = jnp.where(valid, prior_v, 0.0)
         prior_f = jnp.where(valid, prior_f, 1.0)
-        v = v + flags * _dot(prior_v, pw_ref[level])
+        v = v + flags * step(prior_v, pw_ref[level])
         flags = flags * prior_f
     return v
 
@@ -188,7 +203,8 @@
         half = all_values.shape[0] // 2
         paired_values = all_values.reshape(half, 2, scen_count, width)
         paired_flags = all_flags.reshape(half, 2, scen_count)
-        moved = row_times(paired_values[:, 0], powers[local_levels + level])
+        power = powers[local_levels + level]
+        moved = row_times(paired_values[:, 0], power if backward else power.T)
         all_values = paired_flags[:, 1, :, None] * moved + paired_values[:, 1]
         all_flags = paired_flags[:, 0] * paired_flags[:, 1]
     return all_values[0], gathered_extra
@@ -204,12 +220,11 @@
     local_levels = seg_steps.bit_length() - 1
     device_levels = (devices - 1).bit_length()
     power_count = local_levels + max(device_levels, 1)
-    squares = [dynamics]
-    for level in range(power_count - 1):
-        squares.append(jnp.dot(squares[-1], squares[-1], precision=HIGH))
-    forward_powers = [matrix.T for matrix in squares]
-    pwb = jnp.stack(squares[:local_levels])
-    pwf = jnp.stack(forward_powers[:local_levels])
+    (squares,) = _call(
+        k_powers, (jax.ShapeDtypeStruct((power_count, width, width), jnp.float32),), dynamics)
+    forward_powers = squares
+    pwb = squares
+    pwf = squares
     ends_incl = jnp.cumsum(lengths, axis=1)
     starts = ends_incl - lengths
     mirrored = total - ends_incl

time: 162 us -> 166 us (1.025)
  Pallas kernels: 40.8 us -> 50.8 us
  local copies, waits for them, and re-layouts: 13.8 us -> 4.63 us
  matrix products: 20.4 us -> 25.2 us
    dot_general x16, matrix products: 6.92 us -> 22.1 us  [row_times(): jnp.dot(values.reshape(-1, width), matrix, precision=lax.Precision.HIGHEST)]
    dot_general x9 -> x0, matrix products: 11 us -> none  [per_device(): squares.append(jnp.dot(squares[-1], squares[-1], precision=HIGH))]
    pallas_call x5 -> x6, Pallas kernels: 40.8 us -> 50.8 us  [_call(): pl.pallas_call(kernel, out_shape=outs, in_specs=_vmem(len(args)), out_spe...]
    dot_general x6 -> x0, local copies, waits for them, and re-layouts: 5.5 us -> none  [the longest x5 4.66 us: per_device(): squares.append(jnp.dot(squares[-1], squares[-1], precision=HIGH))]
    unnamed x23 -> x5, local copies, waits for them, and re-layouts: 4.29 us -> 1.61 us
where the time goes in v3:
time: 166 us; the launch traced here: 165 us
  blocking collectives  78.8 us (47%)
  Pallas kernels  50.8 us (31%)
  matrix products  25.2 us (15%)
  other arithmetic  4.72 us (3%)
  local copies, waits for them, and re-layouts  4.63 us (3%)
    all_gather x3, blocking collectives, combine(): all_values = lax.all_gather(last_value[None], 'tm', axis=0, tiled=True)  59.6 us
    pallas_call x6, Pallas kernels, _call(): pl.pallas_call(kernel, out_shape=outs, in_specs=_vmem(len(args)), out_spe...  50.8 us
    dot_general x16, matrix products, row_times(): jnp.dot(values.reshape(-1, width), matrix, precision=lax.Precision.HIGHEST)  22.1 us
    all_gather x1, blocking collectives, combine(): gathered = lax.all_gather(packed[None], 'tm', axis=0, tiled=True)  19.2 us

profile of v3, /device:TPU:0, one launch (start us, length us, event | category | flops | bytes accessed | tf_op | source)
XLA Modules:
  0.0 165.1 jit_solution(10057877917825840148)
XLA Ops:
  0.8 0.8 multiply_bitcast_fusion
  1.5 0.9 reduce_window_sum.11
  2.4 0.1 compare_reduce_fusion.1
  2.5 0.7 broadcast_subtract_fusion
  3.2 0.1 and_reduce_fusion
  3.3 0.1 compare_reduce_fusion
  3.8 0.1 copy.140
  3.9 0.1 copy.141
  4.0 0.1 copy.151
  4.2 0.8 reshape.387.start_ref
  5.0 0.8 reshape.386.end_ref
  5.8 1.6 copy.150.imap_ref
  7.4 0.3 convolution_bitcast_fusion.1
  7.7 1.2 fusion.f_ref
  8.9 1.6 convolution_bitcast_fusion.2.init_ref
  10.5 7.1 %shard_map.112.pwb_ref.pwf_ref = f32[10,256,256]{2,1,0:T(8,128)} custom-call(f32[256,256]{1,0:T(8,128)} %copy-done.1), custom_call_target="tpu_custom_call" | custom-call | tf_op jit(solution)/shard_map/pallas_call | solution.py:97
  17.5 5.7 %shard_map.113 = (f32[256,256]{1,0:T(8,128)}, f32[4,256]{1,0:T(4,128)}) custom-call(f32[256,256]{1,0:T(8,128)} %bitcast.225, f32[256,256]{1,0:T(8,128)} %bitcast.222, f32[256,1]{1,0:T(8,128)} %reshape.386.end_ref, f32[10,256,256]{2,1,0:T(8,128)} %shard_map.112.pwb_ref.pwf_ref), custom_call_target="tpu_custom_call" | custom-call | tf_op jit(solution)/shard_map/pallas_call | solution.py:97
  23.2 23.6 %all-gather.4 = f32[16,4,256]{2,1,0:T(4,128)S(1)} all-gather(f32[1,4,256]{2,1,0:T(4,128)} %bitcast.257), channel_id=2, replica_groups=mesh['groups'=2,'tm'=16] {'tm'}, dimensions={0}, use_global_device_ids=true | all-gather | bytes 69632 | tf_op jit(solution)/shard_map/all_gather | solution.py:183
  46.9 0.1 fusion.30
  47.0 1.2 fusion.4
  48.2 1.2 fusion.8
  49.5 1.2 fusion.16
  50.6 1.8 %fusion.20.c1_ref = f32[4,256]{1,0:T(4,128)} fusion(f32[10,256,256]{2,1,0:T(8,128)} %shard_map.112.pwb_ref.pwf_ref, f32[1,2,4,256]{3,2,1,0:T(4,128)S(1)} %fusion.16, f32[4]{0:T(128)S(1)} %slice_bitcast_fusion.45), kind=kOutput, calls=%fused_computation.39 | convolution fusion | flops 3147776 | bytes 274448 | tf_op jit(solution)/shard_map/dot_general | solution.py:32
  52.4 10.8 %shard_map.114 = (f32[256,256]{1,0:T(8,128)}, f32[4,256]{1,0:T(4,128)}) custom-call(f32[256,256]{1,0:T(8,128)} %get-tuple-element.15.w1_ref, f32[256,1]{1,0:T(8,128)} %reshape.386.end_ref, f32[256,1]{1,0:T(8,128)} %reshape.387.start_ref, f32[4,256]{1,0:T(4,128)} %fusion.20.c1_ref, f32[4,256]{1,0:T(4,128)} %convolution_bitcast_fusion.2.init_ref, ...), custom_call_target="tpu_custom_call" | custom-call | tf_op jit(solution)/shard_map/pallas_call | solution.py:97
  63.2 18.1 %all-gather.5 = f32[16,4,256]{2,1,0:T(4,128)S(1)} all-gather(f32[1,4,256]{2,1,0:T(4,128)} %bitcast.256), channel_id=3, replica_groups=mesh['groups'=2,'tm'=16] {'tm'}, dimensions={0}, use_global_device_ids=true | all-gather | bytes 69632 | tf_op jit(solution)/shard_map/all_gather | solution.py:183
  81.3 0.1 fusion.28
  81.4 1.3 fusion.3
  82.8 1.3 fusion.7
  84.1 1.3 fusion.14
  85.3 1.9 %fusion.19.c2_ref = f32[4,256]{1,0:T(4,128)} fusion(f32[10,256,256]{2,1,0:T(8,128)} %shard_map.112.pwb_ref.pwf_ref, f32[1,2,4,256]{3,2,1,0:T(4,128)S(1)} %fusion.14, f32[4]{0:T(128)S(1)} %slice_bitcast_fusion.44), kind=kOutput, calls=%fused_computation.36 | convolution fusion | flops 3147776 | bytes 274448 | tf_op jit(solution)/shard_map/dot_general | solution.py:32
  87.2 10.3 %shard_map.115 = (f32[256,256]{1,0:T(8,128)}, f32[256,256]{1,0:T(8,128)}, f32[4,256]{1,0:T(4,128)}, f32[4,128]{1,0:T(4,128)}) custom-call(f32[256,256]{1,0:T(8,128)} %get-tuple-element.17.d2_ref, f32[256,1]{1,0:T(8,128)} %reshape.387.start_ref, f32[256,1]{1,0:T(8,128)} %reshape.386.end_ref, f32[4,256]{1,0:T(4,128)} %fusion.19.c2_ref, f32[256,256]{1,0:T(8,128)} %bitcast.226, ...), custom_call_target="tpu_custom_call" | custom-call | tf_op jit(solution)/shard_map/pallas_call | solution.py:97
  97.5 0.8 slice_reduce_fusion.1
  98.4 0.7 maximum_bitcast_fusion
  99.1 19.2 %all-gather.6 = f32[16,4,384]{2,1,0:T(4,128)S(1)} all-gather(f32[1,4,384]{2,1,0:T(4,128)S(1)} %maximum_bitcast_fusion), channel_id=4, replica_groups=mesh['groups'=2,'tm'=16] {'tm'}, dimensions={0}, use_global_device_ids=true | all-gather | bytes 104448 | tf_op jit(solution)/shard_map/all_gather | solution.py:188
  118.3 0.6 slice_reduce_fusion
  119.0 0.1 fusion.26
  119.1 1.2 fusion.2
  120.3 1.2 fusion.6
  121.5 1.2 fusion.12
  122.7 1.8 %fusion.18.c3_ref = f32[4,256]{1,0:T(4,128)} fusion(f32[10,256,256]{2,1,0:T(8,128)} %shard_map.112.pwb_ref.pwf_ref, f32[1,2,4,256]{3,2,1,0:T(4,128)S(1)} %fusion.12, f32[4]{0:T(128)S(1)} %slice_bitcast_fusion.45), kind=kOutput, calls=%fused_computation.34 | convolution fusion | flops 3147776 | bytes 274448 | tf_op jit(solution)/shard_map/dot_general | solution.py:32
  124.5 10.8 %shard_map.116 = (f32[256,256]{1,0:T(8,128)}, f32[4,256]{1,0:T(4,128)}) custom-call(f32[256,256]{1,0:T(8,128)} %get-tuple-element.20.w3_ref, f32[256,1]{1,0:T(8,128)} %reshape.386.end_ref, f32[256,1]{1,0:T(8,128)} %reshape.387.start_ref, f32[4,256]{1,0:T(4,128)} %fusion.18.c3_ref, f32[256,64]{1,0:T(8,128)} %copy.150.imap_ref, f32[64,256]{1,0:T(8,128)} %gain_ref.3, ...), custom_call_target="tpu_custom_call" | custom-call | tf_op jit(solution)/shard_map/pallas_call | solution.py:97
  135.3 17.9 %all-gather.7 = f32[16,4,256]{2,1,0:T(4,128)S(1)} all-gather(f32[1,4,256]{2,1,0:T(4,128)} %bitcast.255), channel_id=5, replica_groups=mesh['groups'=2,'tm'=16] {'tm'}, dimensions={0}, use_global_device_ids=true | all-gather | bytes 69632 | tf_op jit(solution)/shard_map/all_gather | solution.py:183
  153.2 0.1 fusion.24
  153.3 1.3 fusion.1
  154.7 1.3 fusion.5
  155.9 1.3 fusion.10
  157.2 1.9 %fusion.17.c4_ref = f32[4,256]{1,0:T(4,128)} fusion(f32[10,256,256]{2,1,0:T(8,128)} %shard_map.112.pwb_ref.pwf_ref, f32[1,2,4,256]{3,2,1,0:T(4,128)S(1)} %fusion.10, f32[4]{0:T(128)S(1)} %slice_bitcast_fusion.44), kind=kOutput, calls=%fused_computation.32 | convolution fusion | flops 3147776 | bytes 274448 | tf_op jit(solution)/shard_map/dot_general | solution.py:32
  159.1 6.1 %shard_map.117 = f32[256,256]{1,0:T(8,128)} custom-call(f32[256,256]{1,0:T(8,128)} %get-tuple-element.23.s4_ref, f32[256,1]{1,0:T(8,128)} %reshape.387.start_ref, f32[4,256]{1,0:T(4,128)} %fusion.17.c4_ref, f32[256,256]{1,0:T(8,128)} %get-tuple-element.19.x_ref, f32[256,256]{1,0:T(8,128)} %bitcast.224, f32[10,256,256]{2,1,0:T(8,128)} %shard_map.112.pwb_ref.pwf_ref), custom_call_target="tpu_custom_call" | custom-call | tf_op jit(solution)/shard_map/pallas_call | solution.py:97
  (44 shorter events, 0.9 us)
Async XLA Ops:
  0.6 6.7 %copy-start = (f32[3,64,64]{2,1,0:T(8,128)S(1)}, f32[3,64,64]{2,1,0:T(8,128)}, u32[]{:S(2)}) copy-start(f32[3,64,64]{2,1,0:T(8,128)} %param.17) | copy-start | bytes 147460
  8.8 1.6 copy-start.1

commit v4 on v3

--- a/solution.py
+++ b/solution.py
@@ -80,6 +80,36 @@
     return v
 
 
+def _carry(g_ref, fl_ref, pw_ref, scen, backward):
+    width = pw_ref.shape[1]
+    g = g_ref[...][:, :width]
+    rows = g.shape[0]
+    devices = rows // scen
+    local_levels = pw_ref.shape[0] - max((devices - 1).bit_length(), 1)
+    r = lax.broadcasted_iota(jnp.int32, (rows, width), 0)
+    flags = jnp.broadcast_to(fl_ref[...], (rows, width))
+    step = _dot if backward else _dot_nt
+    for level in range((devices - 1).bit_length()):
+        stride = scen * 2**level
+        if backward:
+            prior_g = pltpu.roll(g, rows - stride, 0)
+            prior_f = pltpu.roll(flags, rows - stride, 0)
+            valid = r < rows - stride
+        else:
+            prior_g = pltpu.roll(g, stride, 0)
+            prior_f = pltpu.roll(flags, stride, 0)
+            valid = r >= stride
+        prior_g = jnp.where(valid, prior_g, 0.0)
+        prior_f = jnp.where(valid, prior_f, 1.0)
+        g = g + flags * step(prior_g, pw_ref[local_levels + level])
+        flags = flags * prior_f
+    me = lax.axis_index("tm")
+    target = me + 1 if backward else me - 1
+    pick = lax.broadcasted_iota(jnp.int32, (scen, rows), 1)
+    want = lax.broadcasted_iota(jnp.int32, (scen, rows), 0) + target * scen
+    return _dot((pick == want).astype(jnp.float32), g)
+
+
 def _ends(v, seg, backward):
     rows, width = v.shape
     scen = rows // seg
@@ -110,12 +140,13 @@
     e1_ref[...] = _ends(_scan(w1, cut, pwb_ref, seg, True), seg, True)
 
 
-def k_states_in(seg, w1_ref, end_ref, start_ref, c1_ref, init_ref, gain_ref, imap_ref, pwb_ref,
+def k_states_in(seg, w1_ref, end_ref, start_ref, c1_ref, fb_ref, init_ref, gain_ref, imap_ref, pwb_ref,
                 pwf_ref, d2_ref, e2_ref):
     shape = w1_ref.shape
     cut_e = jnp.broadcast_to(end_ref[...], shape)
     cut_s = jnp.broadcast_to(start_ref[...], shape)
-    vt = _scan(w1_ref[...], cut_e, pwb_ref, seg, True, c1_ref[...])
+    c1 = _carry(c1_ref, fb_ref, pwb_ref, w1_ref.shape[0] // seg, True)
+    vt = _scan(w1_ref[...], cut_e, pwb_ref, seg, True, c1)
     controls = lax.dot_general(
         vt, gain_ref[...], (((1,), (1,)), ((), ())), precision=HIGH,
         preferred_element_type=jnp.float32)
@@ -130,14 +161,15 @@
     e2_ref[...] = _ends(_scan(d2, cut_s, pwf_ref, seg, False), seg, False)
 
 
-def k_adjoint_in(seg, scale, d2_ref, start_ref, end_ref, c2_ref, cw_ref, ref_ref, pwf_ref, pwb_ref,
+def k_adjoint_in(seg, scale, d2_ref, start_ref, end_ref, c2_ref, ff_ref, cw_ref, ref_ref, pwf_ref, pwb_ref,
                  x_ref, w3_ref, e3_ref, cost_ref):
     shape = d2_ref.shape
     rows, width = shape
     scen = rows // seg
     cut_s = jnp.broadcast_to(start_ref[...], shape)
     cut_e = jnp.broadcast_to(end_ref[...], shape)
-    states = _scan(d2_ref[...], cut_s, pwf_ref, seg, False, c2_ref[...])
+    c2 = _carry(c2_ref, ff_ref, pwf_ref, scen, False)
+    states = _scan(d2_ref[...], cut_s, pwf_ref, seg, False, c2)
     x_ref[...] = states
     offset = states - ref_ref[...]
     cw = cw_ref[...]
@@ -152,22 +184,24 @@
     e3_ref[...] = _ends(_scan(w3, cut_e, pwb_ref, seg, True), seg, True)
 
 
-def k_value_adjoint_in(seg, w3_ref, end_ref, start_ref, c3_ref, imap_ref, gain_ref, pwb_ref,
+def k_value_adjoint_in(seg, w3_ref, end_ref, start_ref, c3_ref, fb_ref, imap_ref, gain_ref, pwb_ref,
                        pwf_ref, s4_ref, e4_ref):
     shape = w3_ref.shape
     cut_e = jnp.broadcast_to(end_ref[...], shape)
     cut_s = jnp.broadcast_to(start_ref[...], shape)
-    adjoint = _scan(w3_ref[...], cut_e, pwb_ref, seg, True, c3_ref[...])
+    c3 = _carry(c3_ref, fb_ref, pwb_ref, w3_ref.shape[0] // seg, True)
+    adjoint = _scan(w3_ref[...], cut_e, pwb_ref, seg, True, c3)
     pulled = _dot(adjoint, imap_ref[...])
     source = -_dot(pulled, gain_ref[...])
     s4_ref[...] = source
     e4_ref[...] = _ends(_scan(source, cut_s, pwf_ref, seg, False), seg, False)
 
 
-def k_last(seg, s4_ref, start_ref, c4_ref, x_ref, ref_ref, pwf_ref, g_ref):
+def k_last(seg, s4_ref, start_ref, c4_ref, ff_ref, x_ref, ref_ref, pwf_ref, g_ref):
     shape = s4_ref.shape
     cut_s = jnp.broadcast_to(start_ref[...], shape)
-    va = _scan(s4_ref[...], cut_s, pwf_ref, seg, False, c4_ref[...])
+    c4 = _carry(c4_ref, ff_ref, pwf_ref, s4_ref.shape[0] // seg, False)
+    va = _scan(s4_ref[...], cut_s, pwf_ref, seg, False, c4)
     ref = ref_ref[...]
     offset = x_ref[...] - ref
     g_ref[...] = 0.5 * offset * offset + ref * va
@@ -241,25 +275,32 @@
     ends = jax.ShapeDtypeStruct((scen_count, width), f32)
     seg = seg_steps
 
+    seg_lo = jnp.arange(devices, dtype=jnp.int32)[:, None, None] * seg_steps
+    in_fwd = (starts[None] >= seg_lo) & (starts[None] < seg_lo + seg_steps)
+    in_bwd = (ends_incl[None] > seg_lo) & (ends_incl[None] <= seg_lo + seg_steps)
+    flat = (devices * scen_count, 1)
+    ff = 1.0 - jnp.any(in_fwd, axis=-1).astype(f32).reshape(flat)
+    fb = 1.0 - jnp.any(in_bwd, axis=-1).astype(f32).reshape(flat)
+
+    def gather(end_values):
+        every = lax.all_gather(end_values[None], "tm", axis=0, tiled=True)
+        return every.reshape(devices * scen_count, end_values.shape[1])
+
     w1, e1 = _call(functools.partial(k_first, seg), (full, ends), cw, ref, end_col, pwb)
-    c1, _ = combine(e1, mirrored, squares, True, seg, local_levels, device_levels)
     d2, e2 = _call(
         functools.partial(k_states_in, seg), (full, ends),
-        w1, end_col, start_col, c1, init_image, ff_gain, input_map, pwb, pwf)
-    c2, _ = combine(e2, starts, forward_powers, False, seg, local_levels, device_levels)
+        w1, end_col, start_col, gather(e1), fb, init_image, ff_gain, input_map, pwb, pwf)
     cost_shape = jax.ShapeDtypeStruct((scen_count, 128), f32)
     states, w3, e3, cost_part = _call(
         functools.partial(k_adjoint_in, seg, 0.5 / total), (full, full, ends, cost_shape),
-        d2, start_col, end_col, c2, cw, ref, pwf, pwb)
-    c3, all_costs = combine(
-        e3, mirrored, squares, True, seg, local_levels, device_levels, cost_part[:, 0])
-    cost = jnp.sum(all_costs, axis=0)
+        d2, start_col, end_col, gather(e2), ff, cw, ref, pwf, pwb)
+    g3 = gather(jnp.concatenate([e3, cost_part], axis=1))
+    cost = jnp.sum(g3[:, width].reshape(devices, scen_count), axis=0)
     s4, e4 = _call(
         functools.partial(k_value_adjoint_in, seg), (full, ends),
-        w3, end_col, start_col, c3, input_map, ff_gain, pwb, pwf)
-    c4, _ = combine(e4, starts, forward_powers, False, seg, local_levels, device_levels)
+        w3, end_col, start_col, g3, fb, input_map, ff_gain, pwb, pwf)
     (grad,) = _call(
-        functools.partial(k_last, seg), (full,), s4, start_col, c4, states, ref, pwf)
+        functools.partial(k_last, seg), (full,), s4, start_col, gather(e4), ff, states, ref, pwf)
     shape3 = (scen_count, seg_steps, width)
     return (states.reshape(shape3), grad.reshape(shape3), cost)
 

time: 166 us -> 153 us (0.922)
  matrix products: 25.2 us -> 3.09 us
  Pallas kernels: 50.8 us -> 57.4 us
  local copies, waits for them, and re-layouts: 4.63 us -> 8.24 us
    dot_general x16 -> x0, matrix products: 22.1 us -> none  [row_times(): jnp.dot(values.reshape(-1, width), matrix, precision=lax.Precision.HIGHEST)]
    pallas_call x6, Pallas kernels: 50.8 us -> 57.4 us  [_call(): pl.pallas_call(kernel, out_shape=outs, in_specs=_vmem(len(args)), out_spe...]
    unnamed x5 -> x9, local copies, waits for them, and re-layouts: 1.61 us -> 4.2 us
where the time goes in v4:
time: 153 us; the launch traced here: 152 us
  blocking collectives  78.8 us (52%)
  Pallas kernels  57.4 us (38%)
  local copies, waits for them, and re-layouts  8.24 us (5%)
  other arithmetic  3.93 us (3%)
  matrix products  3.09 us (2%)
    all_gather x4, blocking collectives, gather(): every = lax.all_gather(end_values[None], 'tm', axis=0, tiled=True)  78.8 us
    pallas_call x6, Pallas kernels, _call(): pl.pallas_call(kernel, out_shape=outs, in_specs=_vmem(len(args)), out_spe...  57.4 us
    unnamed x9, local copies, waits for them, and re-layouts  4.2 us

profile of v4, /device:TPU:0, one launch (start us, length us, event | category | flops | bytes accessed | tf_op | source)
XLA Modules:
  0.0 152.2 jit_solution(17101964083122049711)
XLA Ops:
  0.6 0.0 copy-start
  0.7 0.8 multiply_bitcast_fusion
  1.4 0.9 reduce_window_sum.11
  2.3 0.1 compare_reduce_fusion.1
  2.4 0.7 sub.13
  3.1 0.1 and_reduce_fusion
  3.2 0.1 compare_reduce_fusion
  3.3 0.1 iota_add_fusion
  3.4 0.1 copy.54
  3.5 0.1 copy.49
  3.5 0.7 sub.18.fb_ref
  4.2 0.7 sub.19.ff_ref
  4.9 0.8 reshape.207.start_ref
  5.7 0.8 reshape.206.end_ref
  6.5 1.6 %copy.53.imap_ref = f32[256,64]{1,0:T(8,128)} copy(f32[256,64]{0,1:T(8,128)} %param.15) | data formatting | bytes 131072 | tf_op args[6]
  8.0 0.0 copy-done
  8.1 0.3 convolution_bitcast_fusion.1
  8.4 1.2 fusion.f_ref
  9.5 0.0 copy-start.1
  9.6 1.6 %convolution_bitcast_fusion.2.init_ref = f32[4,256]{1,0:T(4,128)} fusion(f32[256,256]{1,0:T(8,128)S(1)} %fusion.f_ref, f32[4,256]{1,0:T(4,128)} %param.11), kind=kOutput, calls=%fused_computation.3 | convolution fusion | flops 3145728 | bytes 270336 | tf_op jit(solution)/shard_map/dot_general | solution.py:270
  11.2 0.0 copy-done.1
  11.2 7.1 %shard_map.112.pwb_ref.pwf_ref = f32[10,256,256]{2,1,0:T(8,128)} custom-call(f32[256,256]{1,0:T(8,128)} %copy-done.1), custom_call_target="tpu_custom_call" | custom-call | tf_op jit(solution)/shard_map/pallas_call | solution.py:127
  18.2 5.7 %shard_map.113 = (f32[256,256]{1,0:T(8,128)}, f32[4,256]{1,0:T(4,128)}) custom-call(f32[256,256]{1,0:T(8,128)} %bitcast.28, f32[256,256]{1,0:T(8,128)} %bitcast.25, f32[256,1]{1,0:T(8,128)} %reshape.206.end_ref, f32[10,256,256]{2,1,0:T(8,128)} %shard_map.112.pwb_ref.pwf_ref), custom_call_target="tpu_custom_call" | custom-call | tf_op jit(solution)/shard_map/pallas_call | solution.py:127
  23.9 23.6 %all-gather.4 = f32[16,4,256]{2,1,0:T(4,128)S(1)} all-gather(f32[1,4,256]{2,1,0:T(4,128)} %bitcast.34), channel_id=2, replica_groups=mesh['groups'=2,'tm'=16] {'tm'}, dimensions={0}, use_global_device_ids=true | all-gather | bytes 69632 | tf_op jit(solution)/shard_map/all_gather | solution.py:286
  47.6 0.7 reshape.198.c1_ref
  48.2 12.2 %shard_map.114 = (f32[256,256]{1,0:T(8,128)}, f32[4,256]{1,0:T(4,128)}) custom-call(f32[256,256]{1,0:T(8,128)} %get-tuple-element.13.w1_ref, f32[256,1]{1,0:T(8,128)} %reshape.206.end_ref, f32[256,1]{1,0:T(8,128)} %reshape.207.start_ref, f32[64,256]{1,0:T(8,128)} %reshape.198.c1_ref, f32[64,1]{1,0:T(8,128)} %sub.18.fb_ref, ...), custom_call_target="tpu_custom_call" | custom-call | tf_op jit(solution)/shard_map/pallas_call | solution.py:127
  60.4 18.1 %all-gather.5 = f32[16,4,256]{2,1,0:T(4,128)S(1)} all-gather(f32[1,4,256]{2,1,0:T(4,128)} %bitcast.33), channel_id=3, replica_groups=mesh['groups'=2,'tm'=16] {'tm'}, dimensions={0}, use_global_device_ids=true | all-gather | bytes 69632 | tf_op jit(solution)/shard_map/all_gather | solution.py:286
  78.5 0.6 reshape.200.c2_ref
  79.1 12.3 %shard_map.115 = (f32[256,256]{1,0:T(8,128)}, f32[256,256]{1,0:T(8,128)}, f32[4,256]{1,0:T(4,128)}, f32[4,128]{1,0:T(4,128)}) custom-call(f32[256,256]{1,0:T(8,128)} %get-tuple-element.15.d2_ref, f32[256,1]{1,0:T(8,128)} %reshape.207.start_ref, f32[256,1]{1,0:T(8,128)} %reshape.206.end_ref, f32[64,256]{1,0:T(8,128)} %reshape.200.c2_ref, ...), custom_call_target="tpu_custom_call" | custom-call | tf_op jit(solution)/shard_map/pallas_call | solution.py:127
  91.4 0.7 maximum_bitcast_fusion
  92.1 19.2 %all-gather.6 = f32[16,4,384]{2,1,0:T(4,128)S(1)} all-gather(f32[1,4,384]{2,1,0:T(4,128)S(1)} %maximum_bitcast_fusion), channel_id=4, replica_groups=mesh['groups'=2,'tm'=16] {'tm'}, dimensions={0}, use_global_device_ids=true | all-gather | bytes 104448 | tf_op jit(solution)/shard_map/all_gather | solution.py:286
  111.3 0.7 reshape.202.c3_ref
  111.9 12.2 %shard_map.116 = (f32[256,256]{1,0:T(8,128)}, f32[4,256]{1,0:T(4,128)}) custom-call(f32[256,256]{1,0:T(8,128)} %get-tuple-element.18.w3_ref, f32[256,1]{1,0:T(8,128)} %reshape.206.end_ref, f32[256,1]{1,0:T(8,128)} %reshape.207.start_ref, f32[64,384]{1,0:T(8,128)} %reshape.202.c3_ref, f32[64,1]{1,0:T(8,128)} %sub.18.fb_ref, f32[256,64]{1,0:T(8,128)} %copy.53.imap_ref, ...), custom_call_target="tpu_custom_call" | custom-call | tf_op jit(solution)/shard_map/pallas_call | solution.py:127
  124.1 0.9 slice_reduce_fusion
  125.0 0.1 reshape_squeeze.3
  125.1 0.6 reduce_sum.9
  125.6 17.9 %all-gather.7 = f32[16,4,256]{2,1,0:T(4,128)S(1)} all-gather(f32[1,4,256]{2,1,0:T(4,128)} %bitcast.32), channel_id=5, replica_groups=mesh['groups'=2,'tm'=16] {'tm'}, dimensions={0}, use_global_device_ids=true | all-gather | bytes 69632 | tf_op jit(solution)/shard_map/all_gather | solution.py:286
  143.5 0.6 reshape.204.c4_ref
  144.2 8.0 %shard_map.117 = f32[256,256]{1,0:T(8,128)} custom-call(f32[256,256]{1,0:T(8,128)} %get-tuple-element.21.s4_ref, f32[256,1]{1,0:T(8,128)} %reshape.207.start_ref, f32[64,256]{1,0:T(8,128)} %reshape.204.c4_ref, f32[64,1]{1,0:T(8,128)} %sub.19.ff_ref, f32[256,256]{1,0:T(8,128)} %get-tuple-element.17.x_ref, f32[256,256]{1,0:T(8,128)} %bitcast.27, ...), custom_call_target="tpu_custom_call" | custom-call | tf_op jit(solution)/shard_map/pallas_call | solution.py:127
  (6 shorter events, 0.0 us)
Async XLA Ops:
  0.6 7.4 %copy-start = (f32[3,64,64]{2,1,0:T(8,128)S(1)}, f32[3,64,64]{2,1,0:T(8,128)}, u32[]{:S(2)}) copy-start(f32[3,64,64]{2,1,0:T(8,128)} %param.13) | copy-start | bytes 147460
  9.5 1.6 %copy-start.1 = (f32[256,256]{1,0:T(8,128)}, f32[256,256]{1,0:T(8,128)S(1)}, u32[]{:S(2)}) copy-start(f32[256,256]{1,0:T(8,128)S(1)} %fusion.f_ref) | copy-start | bytes 786436

commit v5 on v4

--- a/solution.py
+++ b/solution.py
@@ -42,6 +42,21 @@
         a, b, (((1,), (1,)), ((), ())), precision=HIGH, preferred_element_type=jnp.float32)
 
 
+def _split(x):
+    hi = x.astype(jnp.bfloat16)
+    lo = (x - hi.astype(jnp.float32)).astype(jnp.bfloat16)
+    return hi, lo
+
+
+def _mm(a, b, nt=False):
+    dims = (((1,), (1 if nt else 0,)), ((), ()))
+    a_hi, a_lo = _split(a)
+    b_hi, b_lo = _split(b)
+    part = functools.partial(lax.dot_general, dimension_numbers=dims,
+                             preferred_element_type=jnp.float32)
+    return part(a_lo, b_hi) + part(a_hi, b_lo) + part(a_hi, b_hi)
+
+
 def k_powers(f_ref, out_ref):
     power = f_ref[...]
     out_ref[0] = power
@@ -57,7 +72,7 @@
     flags = 1.0 - cut
     if levels is None:
         levels = seg.bit_length() - 1
-    step = _dot if backward else _dot_nt
+    step = functools.partial(_mm, nt=not backward)
     if carry is not None:
         pushed = step(carry, pw_ref[0])
         pushed = jnp.broadcast_to(pushed[:, None, :], (scen, seg, width)).reshape(rows, width)
@@ -88,7 +103,7 @@
     local_levels = pw_ref.shape[0] - max((devices - 1).bit_length(), 1)
     r = lax.broadcasted_iota(jnp.int32, (rows, width), 0)
     flags = jnp.broadcast_to(fl_ref[...], (rows, width))
-    step = _dot if backward else _dot_nt
+    step = functools.partial(_mm, nt=not backward)
     for level in range((devices - 1).bit_length()):
         stride = scen * 2**level
         if backward:
@@ -147,12 +162,8 @@
     cut_s = jnp.broadcast_to(start_ref[...], shape)
     c1 = _carry(c1_ref, fb_ref, pwb_ref, w1_ref.shape[0] // seg, True)
     vt = _scan(w1_ref[...], cut_e, pwb_ref, seg, True, c1)
-    controls = lax.dot_general(
-        vt, gain_ref[...], (((1,), (1,)), ((), ())), precision=HIGH,
-        preferred_element_type=jnp.float32)
-    forcing = -lax.dot_general(
-        controls, imap_ref[...], (((1,), (1,)), ((), ())), precision=HIGH,
-        preferred_element_type=jnp.float32)
+    controls = _mm(vt, gain_ref[...], nt=True)
+    forcing = -_mm(controls, imap_ref[...], nt=True)
     rows, width = shape
     scen = rows // seg
     init = jnp.broadcast_to(init_ref[...][:, None, :], (scen, seg, width)).reshape(rows, width)
@@ -191,8 +202,8 @@
     cut_s = jnp.broadcast_to(start_ref[...], shape)
     c3 = _carry(c3_ref, fb_ref, pwb_ref, w3_ref.shape[0] // seg, True)
     adjoint = _scan(w3_ref[...], cut_e, pwb_ref, seg, True, c3)
-    pulled = _dot(adjoint, imap_ref[...])
-    source = -_dot(pulled, gain_ref[...])
+    pulled = _mm(adjoint, imap_ref[...])
+    source = -_mm(pulled, gain_ref[...])
     s4_ref[...] = source
     e4_ref[...] = _ends(_scan(source, cut_s, pwf_ref, seg, False), seg, False)
 

time: 153 us -> 138 us (0.902)
  Pallas kernels: 57.4 us -> 43.6 us
    pallas_call x6, Pallas kernels: 57.4 us -> 43.6 us  [_call(): pl.pallas_call(kernel, out_shape=outs, in_specs=_vmem(len(args)), out_spe...]
where the time goes in v5:
time: 138 us
  blocking collectives  78.4 us (57%)
  Pallas kernels  43.6 us (32%)
  local copies, waits for them, and re-layouts  8.24 us (6%)
  other arithmetic  3.93 us (3%)
  matrix products  3.09 us (2%)
    all_gather x4, blocking collectives, gather(): every = lax.all_gather(end_values[None], 'tm', axis=0, tiled=True)  78.4 us
    pallas_call x6, Pallas kernels, _call(): pl.pallas_call(kernel, out_shape=outs, in_specs=_vmem(len(args)), out_spe...  43.6 us
    unnamed x9, local copies, waits for them, and re-layouts  4.2 us

profile of v5, /device:TPU:0, one launch (start us, length us, event | category | flops | bytes accessed | tf_op | source)
XLA Modules:
  0.0 137.9 jit_solution(13816062790826549345)
XLA Ops:
  0.6 0.0 copy-start
  0.7 0.8 multiply_bitcast_fusion
  1.4 0.9 reduce_window_sum.11
  2.3 0.1 compare_reduce_fusion.1
  2.4 0.7 sub.13
  3.1 0.1 and_reduce_fusion
  3.2 0.1 compare_reduce_fusion
  3.3 0.1 iota_add_fusion
  3.4 0.1 copy.54
  3.5 0.1 copy.49
  3.5 0.7 sub.18.fb_ref
  4.2 0.7 sub.19.ff_ref
  4.9 0.8 reshape.207.start_ref
  5.7 0.8 reshape.206.end_ref
  6.5 1.6 %copy.53.imap_ref = f32[256,64]{1,0:T(8,128)} copy(f32[256,64]{0,1:T(8,128)} %param.15) | data formatting | bytes 131072 | tf_op args[6]
  8.0 0.0 copy-done
  8.1 0.3 convolution_bitcast_fusion.1
  8.4 1.2 fusion.f_ref
  9.5 0.0 copy-start.1
  9.6 1.6 %convolution_bitcast_fusion.2.init_ref = f32[4,256]{1,0:T(4,128)} fusion(f32[256,256]{1,0:T(8,128)S(1)} %fusion.f_ref, f32[4,256]{1,0:T(4,128)} %param.11), kind=kOutput, calls=%fused_computation.3 | convolution fusion | flops 3145728 | bytes 270336 | tf_op jit(solution)/shard_map/dot_general | solution.py:281
  11.2 0.0 copy-done.1
  11.2 7.1 %shard_map.112.pwb_ref.pwf_ref = f32[10,256,256]{2,1,0:T(8,128)} custom-call(f32[256,256]{1,0:T(8,128)} %copy-done.1), custom_call_target="tpu_custom_call" | custom-call | tf_op jit(solution)/shard_map/pallas_call | solution.py:142
  18.2 4.4 %shard_map.113 = (f32[256,256]{1,0:T(8,128)}, f32[4,256]{1,0:T(4,128)}) custom-call(f32[256,256]{1,0:T(8,128)} %bitcast.28, f32[256,256]{1,0:T(8,128)} %bitcast.25, f32[256,1]{1,0:T(8,128)} %reshape.206.end_ref, f32[10,256,256]{2,1,0:T(8,128)} %shard_map.112.pwb_ref.pwf_ref), custom_call_target="tpu_custom_call" | custom-call | tf_op jit(solution)/shard_map/pallas_call | solution.py:142
  22.7 23.5 %all-gather.4 = f32[16,4,256]{2,1,0:T(4,128)S(1)} all-gather(f32[1,4,256]{2,1,0:T(4,128)} %bitcast.34), channel_id=2, replica_groups=mesh['groups'=2,'tm'=16] {'tm'}, dimensions={0}, use_global_device_ids=true | all-gather | bytes 69632 | tf_op jit(solution)/shard_map/all_gather | solution.py:297
  46.1 0.7 reshape.198.c1_ref
  46.8 8.8 %shard_map.114 = (f32[256,256]{1,0:T(8,128)}, f32[4,256]{1,0:T(4,128)}) custom-call(f32[256,256]{1,0:T(8,128)} %get-tuple-element.13.w1_ref, f32[256,1]{1,0:T(8,128)} %reshape.206.end_ref, f32[256,1]{1,0:T(8,128)} %reshape.207.start_ref, f32[64,256]{1,0:T(8,128)} %reshape.198.c1_ref, f32[64,1]{1,0:T(8,128)} %sub.18.fb_ref, ...), custom_call_target="tpu_custom_call" | custom-call | tf_op jit(solution)/shard_map/pallas_call | solution.py:142
  55.5 18.0 %all-gather.5 = f32[16,4,256]{2,1,0:T(4,128)S(1)} all-gather(f32[1,4,256]{2,1,0:T(4,128)} %bitcast.33), channel_id=3, replica_groups=mesh['groups'=2,'tm'=16] {'tm'}, dimensions={0}, use_global_device_ids=true | all-gather | bytes 69632 | tf_op jit(solution)/shard_map/all_gather | solution.py:297
  73.6 0.6 reshape.200.c2_ref
  74.2 8.7 %shard_map.115 = (f32[256,256]{1,0:T(8,128)}, f32[256,256]{1,0:T(8,128)}, f32[4,256]{1,0:T(4,128)}, f32[4,128]{1,0:T(4,128)}) custom-call(f32[256,256]{1,0:T(8,128)} %get-tuple-element.15.d2_ref, f32[256,1]{1,0:T(8,128)} %reshape.207.start_ref, f32[256,1]{1,0:T(8,128)} %reshape.206.end_ref, f32[64,256]{1,0:T(8,128)} %reshape.200.c2_ref, ...), custom_call_target="tpu_custom_call" | custom-call | tf_op jit(solution)/shard_map/pallas_call | solution.py:142
  82.9 0.7 maximum_bitcast_fusion
  83.6 18.9 %all-gather.6 = f32[16,4,384]{2,1,0:T(4,128)S(1)} all-gather(f32[1,4,384]{2,1,0:T(4,128)S(1)} %maximum_bitcast_fusion), channel_id=4, replica_groups=mesh['groups'=2,'tm'=16] {'tm'}, dimensions={0}, use_global_device_ids=true | all-gather | bytes 104448 | tf_op jit(solution)/shard_map/all_gather | solution.py:297
  102.6 0.7 reshape.202.c3_ref
  103.2 8.8 %shard_map.116 = (f32[256,256]{1,0:T(8,128)}, f32[4,256]{1,0:T(4,128)}) custom-call(f32[256,256]{1,0:T(8,128)} %get-tuple-element.18.w3_ref, f32[256,1]{1,0:T(8,128)} %reshape.206.end_ref, f32[256,1]{1,0:T(8,128)} %reshape.207.start_ref, f32[64,384]{1,0:T(8,128)} %reshape.202.c3_ref, f32[64,1]{1,0:T(8,128)} %sub.18.fb_ref, f32[256,64]{1,0:T(8,128)} %copy.53.imap_ref, ...), custom_call_target="tpu_custom_call" | custom-call | tf_op jit(solution)/shard_map/pallas_call | solution.py:142
  112.0 0.9 slice_reduce_fusion
  112.9 0.1 reshape_squeeze.3
  112.9 0.6 reduce_sum.9
  113.5 17.9 %all-gather.7 = f32[16,4,256]{2,1,0:T(4,128)S(1)} all-gather(f32[1,4,256]{2,1,0:T(4,128)} %bitcast.32), channel_id=5, replica_groups=mesh['groups'=2,'tm'=16] {'tm'}, dimensions={0}, use_global_device_ids=true | all-gather | bytes 69632 | tf_op jit(solution)/shard_map/all_gather | solution.py:297
  131.4 0.6 reshape.204.c4_ref
  132.0 5.9 %shard_map.117 = f32[256,256]{1,0:T(8,128)} custom-call(f32[256,256]{1,0:T(8,128)} %get-tuple-element.21.s4_ref, f32[256,1]{1,0:T(8,128)} %reshape.207.start_ref, f32[64,256]{1,0:T(8,128)} %reshape.204.c4_ref, f32[64,1]{1,0:T(8,128)} %sub.19.ff_ref, f32[256,256]{1,0:T(8,128)} %get-tuple-element.17.x_ref, f32[256,256]{1,0:T(8,128)} %bitcast.27, ...), custom_call_target="tpu_custom_call" | custom-call | tf_op jit(solution)/shard_map/pallas_call | solution.py:142
  (6 shorter events, 0.0 us)
Async XLA Ops:
  0.6 7.4 %copy-start = (f32[3,64,64]{2,1,0:T(8,128)S(1)}, f32[3,64,64]{2,1,0:T(8,128)}, u32[]{:S(2)}) copy-start(f32[3,64,64]{2,1,0:T(8,128)} %param.13) | copy-start | bytes 147460
  9.5 1.6 %copy-start.1 = (f32[256,256]{1,0:T(8,128)}, f32[256,256]{1,0:T(8,128)S(1)}, u32[]{:S(2)}) copy-start(f32[256,256]{1,0:T(8,128)S(1)} %fusion.f_ref) | copy-start | bytes 786436

commit v6 on v5

--- a/solution.py
+++ b/solution.py
@@ -294,7 +294,8 @@
     fb = 1.0 - jnp.any(in_bwd, axis=-1).astype(f32).reshape(flat)
 
     def gather(end_values):
-        every = lax.all_gather(end_values[None], "tm", axis=0, tiled=True)
+        copies = jnp.broadcast_to(end_values[None], (devices,) + end_values.shape)
+        every = lax.all_to_all(copies, "tm", 0, 0, tiled=True)
         return every.reshape(devices * scen_count, end_values.shape[1])
 
     w1, e1 = _call(functools.partial(k_first, seg), (full, ends), cw, ref, end_col, pwb)

time: 138 us -> 102 us (0.74)
  blocking collectives: 78.4 us -> 9.99 us
  waiting for transfers between devices: 0 us -> 14.7 us
  starting transfers between devices: 0 us -> 14.5 us
  local copies, waits for them, and re-layouts: 8.24 us -> 11.3 us
    all_gather x4 -> x0, blocking collectives: 78.4 us -> none  [gather(): every = lax.all_gather(end_values[None], 'tm', axis=0, tiled=True)]
    all_to_all x0 -> x3, waiting for transfers between devices: none -> 14.7 us  [gather(): every = lax.all_to_all(copies, 'tm', 0, 0, tiled=True)]
    all_to_all x0 -> x3, starting transfers between devices: none -> 14.5 us  [gather(): every = lax.all_to_all(copies, 'tm', 0, 0, tiled=True)]
    all_to_all x0 -> x1, blocking collectives: none -> 9.99 us  [gather(): every = lax.all_to_all(copies, 'tm', 0, 0, tiled=True)]
    broadcast_in_dim x0 -> x4, local copies, waits for them, and re-layouts: none -> 3.92 us  [gather(): copies = jnp.broadcast_to(end_values[None], (devices,) + end_values.shape)]
    unnamed x9 -> x11, local copies, waits for them, and re-layouts: 4.2 us -> 0.78 us
    reshape x0 -> x4, local copies, waits for them, and re-layouts: none -> 2.58 us  [gather(): return every.reshape(devices * scen_count, end_values.shape[1])]
  transfers between devices with their start and end apart: 0 -> 3, of which waited for: 0 -> 3; matrix products, arithmetic and copies ran while one was open for 0% -> 6% of each run, Pallas kernels for 0% -> 0%
where the time goes in v6:
time: 102 us; the launch traced here: 101 us
  Pallas kernels  43.7 us (43%)
  waiting for transfers between devices  14.7 us (14%)
  starting transfers between devices  14.5 us (14%)
  local copies, waits for them, and re-layouts  11.3 us (11%)
  blocking collectives  9.99 us (10%)
  other arithmetic  3.25 us (3%)
  matrix products  3.1 us (3%)
    pallas_call x6, Pallas kernels, _call(): pl.pallas_call(kernel, out_shape=outs, in_specs=_vmem(len(args)), out_spe...  43.7 us
    all_to_all x3, waiting for transfers between devices, gather(): every = lax.all_to_all(copies, 'tm', 0, 0, tiled=True)  14.7 us
    all_to_all x3, starting transfers between devices, gather(): every = lax.all_to_all(copies, 'tm', 0, 0, tiled=True)  14.5 us
    all_to_all x1, blocking collectives, gather(): every = lax.all_to_all(copies, 'tm', 0, 0, tiled=True)  9.99 us
    broadcast_in_dim x4, local copies, waits for them, and re-layouts, gather(): copies = jnp.broadcast_to(end_values[None], (devices,) + end_values.shape)  3.92 us
    reshape x4, local copies, waits for them, and re-layouts, gather(): return every.reshape(devices * scen_count, end_values.shape[1])  2.58 us
    dot_general x2, matrix products, build_dynamics(): jnp.einsum('lia,lab,ljb->ij', row_hot, coupling, col_hot, precision=lax.P...  2.18 us
  transfers between devices with their start and end apart: 3, of which 3 were waited for; matrix products, arithmetic and copies ran while one was open for 6% of the time, Pallas kernels for 0%

profile of v6, /device:TPU:0, one launch (start us, length us, event | category | flops | bytes accessed | tf_op | source)
XLA Modules:
  0.0 101.3 jit_solution(16802899976468751136)
XLA Ops:
  0.6 0.0 copy-start
  0.7 0.8 multiply_bitcast_fusion
  1.4 0.9 reduce_window_sum.11
  2.3 0.1 compare_reduce_fusion.1
  2.4 0.8 reshape.194.end_ref
  3.2 0.1 iota_add_fusion
  3.2 0.0 copy-done
  3.2 0.3 convolution_bitcast_fusion.1
  3.6 1.9 %fusion.f_ref = f32[256,256]{1,0:T(8,128)} fusion(f32[3,64,256]{2,1,0:T(8,128)S(1)} %convolution_bitcast_fusion.1, f32[256]{0:T(256)} %param.12, s32[3,64]{1,0:T(4,128)S(1)} %get-tuple-element.29), kind=kOutput, calls=%fused_computation.1 | convolution fusion | flops 151240704 | bytes 460544 | tf_op jit(solution)/shard_map/lia,lab,ljb->ij/dot_general | solution.py:24
  5.4 0.0 copy-start.3
  5.4 0.0 copy-start.2
  5.4 7.1 %shard_map.112.pwb_ref.pwf_ref = f32[10,256,256]{2,1,0:T(8,128)} custom-call(f32[256,256]{1,0:T(8,128)} %fusion.f_ref), custom_call_target="tpu_custom_call" | custom-call | tf_op jit(solution)/shard_map/pallas_call | solution.py:142
  12.5 4.4 %shard_map.113 = (f32[256,256]{1,0:T(8,128)}, f32[4,256]{1,0:T(4,128)}) custom-call(f32[256,256]{1,0:T(8,128)} %bitcast.23, f32[256,256]{1,0:T(8,128)} %bitcast.20, f32[256,1]{1,0:T(8,128)} %reshape.194.end_ref, f32[10,256,256]{2,1,0:T(8,128)} %shard_map.112.pwb_ref.pwf_ref), custom_call_target="tpu_custom_call" | custom-call | tf_op jit(solution)/shard_map/pallas_call | solution.py:142
  17.0 1.3 %broadcast_in_dim.28 = f32[16,4,256]{2,1,0:T(4,128)} broadcast(f32[4,256]{1,0:T(4,128)} %get-tuple-element.14), dimensions={1,2} | broadcast | bytes 69632 | tf_op jit(solution)/shard_map/broadcast_in_dim | solution.py:297
  18.3 7.4 %all-to-all-start = ((f32[16,4,256]{2,1,0:T(4,128)}), f32[16,4,256]{2,1,0:T(4,128)S(1)}, u32[]{:S(2)}, u32[]{:S(2)}) async-start(f32[16,4,256]{2,1,0:T(4,128)} %broadcast_in_dim.28), calls=%async_computation | async-start | bytes 131072 | tf_op jit(solution)/shard_map/all_to_all | solution.py:298
  25.7 0.0 copy-done.3
  25.7 0.1 compare_reduce_fusion
  25.8 0.1 and_reduce_fusion
  25.9 0.1 copy.34
  26.0 0.7 sub.18.fb_ref
  26.7 0.8 reshape.195.start_ref
  27.4 0.0 copy-done.2
  27.4 0.8 copy.38.imap_ref
  28.2 0.0 copy-done.1
  28.2 0.0 copy-done.4
  28.2 0.9 convolution_bitcast_fusion.2.init_ref
  29.1 3.4 %all-to-all-done = f32[16,4,256]{2,1,0:T(4,128)S(1)} async-done(((f32[16,4,256]{2,1,0:T(4,128)}), f32[16,4,256]{2,1,0:T(4,128)S(1)}, u32[]{:S(2)}, u32[]{:S(2)}) %all-to-all-start) | async-done | bytes 65568 | tf_op jit(solution)/shard_map/all_to_all | solution.py:298
  32.5 0.6 reshape.185.c1_ref
  33.2 8.8 %shard_map.114 = (f32[256,256]{1,0:T(8,128)}, f32[4,256]{1,0:T(4,128)}) custom-call(f32[256,256]{1,0:T(8,128)} %get-tuple-element.13.w1_ref, f32[256,1]{1,0:T(8,128)} %reshape.194.end_ref, f32[256,1]{1,0:T(8,128)} %reshape.195.start_ref, f32[64,256]{1,0:T(8,128)} %reshape.185.c1_ref, f32[64,1]{1,0:T(8,128)} %sub.18.fb_ref, ...), custom_call_target="tpu_custom_call" | custom-call | tf_op jit(solution)/shard_map/pallas_call | solution.py:142
  41.9 1.3 %broadcast_in_dim.29 = f32[16,4,256]{2,1,0:T(4,128)} broadcast(f32[4,256]{1,0:T(4,128)} %get-tuple-element.16), dimensions={1,2} | broadcast | bytes 69632 | tf_op jit(solution)/shard_map/broadcast_in_dim | solution.py:297
  43.3 3.7 %all-to-all-start.1 = ((f32[16,4,256]{2,1,0:T(4,128)}), f32[16,4,256]{2,1,0:T(4,128)S(1)}, u32[]{:S(2)}, u32[]{:S(2)}) async-start(f32[16,4,256]{2,1,0:T(4,128)} %broadcast_in_dim.29), calls=%async_computation.1 | async-start | bytes 131072 | tf_op jit(solution)/shard_map/all_to_all | solution.py:298
  47.0 0.1 copy.39
  47.0 0.7 sub.19.ff_ref
  47.7 5.9 %all-to-all-done.1 = f32[16,4,256]{2,1,0:T(4,128)S(1)} async-done(((f32[16,4,256]{2,1,0:T(4,128)}), f32[16,4,256]{2,1,0:T(4,128)S(1)}, u32[]{:S(2)}, u32[]{:S(2)}) %all-to-all-start.1) | async-done | bytes 65568 | tf_op jit(solution)/shard_map/all_to_all | solution.py:298
  53.6 0.6 reshape.186.c2_ref
  54.3 8.7 %shard_map.115 = (f32[256,256]{1,0:T(8,128)}, f32[256,256]{1,0:T(8,128)}, f32[4,256]{1,0:T(4,128)}, f32[4,128]{1,0:T(4,128)}) custom-call(f32[256,256]{1,0:T(8,128)} %get-tuple-element.15.d2_ref, f32[256,1]{1,0:T(8,128)} %reshape.195.start_ref, f32[256,1]{1,0:T(8,128)} %reshape.194.end_ref, f32[64,256]{1,0:T(8,128)} %reshape.186.c2_ref, ...), custom_call_target="tpu_custom_call" | custom-call | tf_op jit(solution)/shard_map/pallas_call | solution.py:142
  63.0 0.7 pad_maximum_fusion
  63.7 10.0 %all_to_all.20 = f32[16,4,384]{2,1,0:T(4,128)S(1)} all-to-all(f32[16,4,384]{2,1,0:T(4,128)S(1)} %broadcast_in_dim.30), channel_id=1, replica_groups=mesh['groups'=2,'tm'=16] {'tm'}, dimensions={0} | all-to-all | bytes 196608 | tf_op jit(solution)/shard_map/all_to_all | solution.py:298
  73.7 0.7 reshape.188.c3_ref
  74.4 8.8 %shard_map.116 = (f32[256,256]{1,0:T(8,128)}, f32[4,256]{1,0:T(4,128)}) custom-call(f32[256,256]{1,0:T(8,128)} %get-tuple-element.18.w3_ref, f32[256,1]{1,0:T(8,128)} %reshape.194.end_ref, f32[256,1]{1,0:T(8,128)} %reshape.195.start_ref, f32[64,384]{1,0:T(8,128)} %reshape.188.c3_ref, f32[64,1]{1,0:T(8,128)} %sub.18.fb_ref, f32[256,64]{1,0:T(8,128)} %copy.38.imap_ref, ...), custom_call_target="tpu_custom_call" | custom-call | tf_op jit(solution)/shard_map/pallas_call | solution.py:142
  83.1 1.3 %broadcast_in_dim.31 = f32[16,4,256]{2,1,0:T(4,128)} broadcast(f32[4,256]{1,0:T(4,128)} %get-tuple-element.22), dimensions={1,2} | broadcast | bytes 69632 | tf_op jit(solution)/shard_map/broadcast_in_dim | solution.py:297
  84.4 3.5 %all-to-all-start.3 = ((f32[16,4,256]{2,1,0:T(4,128)}), f32[16,4,256]{2,1,0:T(4,128)S(1)}, u32[]{:S(2)}, u32[]{:S(2)}) async-start(f32[16,4,256]{2,1,0:T(4,128)} %broadcast_in_dim.31), calls=%async_computation.3 | async-start | bytes 131072 | tf_op jit(solution)/shard_map/all_to_all | solution.py:298
  87.9 0.9 slice_reduce_fusion
  88.8 0.1 reshape_squeeze.3
  88.9 0.6 reduce_sum.9
  89.4 5.4 %all-to-all-done.3 = f32[16,4,256]{2,1,0:T(4,128)S(1)} async-done(((f32[16,4,256]{2,1,0:T(4,128)}), f32[16,4,256]{2,1,0:T(4,128)S(1)}, u32[]{:S(2)}, u32[]{:S(2)}) %all-to-all-start.3) | async-done | bytes 65568 | tf_op jit(solution)/shard_map/all_to_all | solution.py:298
  94.8 0.6 reshape.189.c4_ref
  95.4 5.9 %shard_map.117 = f32[256,256]{1,0:T(8,128)} custom-call(f32[256,256]{1,0:T(8,128)} %get-tuple-element.21.s4_ref, f32[256,1]{1,0:T(8,128)} %reshape.195.start_ref, f32[64,256]{1,0:T(8,128)} %reshape.189.c4_ref, f32[64,1]{1,0:T(8,128)} %sub.19.ff_ref, f32[256,256]{1,0:T(8,128)} %get-tuple-element.17.x_ref, f32[256,256]{1,0:T(8,128)} %bitcast.22, ...), custom_call_target="tpu_custom_call" | custom-call | tf_op jit(solution)/shard_map/pallas_call | solution.py:142
  (10 shorter events, 0.1 us)
Async XLA Ops:
  0.6 2.6 %copy-start = (f32[3,64,64]{2,1,0:T(8,128)S(1)}, f32[3,64,64]{2,1,0:T(8,128)}, u32[]{:S(2)}) copy-start(f32[3,64,64]{2,1,0:T(8,128)} %param.13) | copy-start | bytes 147460
  5.4 20.2 %copy-start.3 = (s32[4,4]{1,0:T(4,128)S(1)}, s32[4,4]{1,0:T(4,128)}, u32[]{:S(2)}) copy-start(s32[4,4]{1,0:T(4,128)} %param.17) | copy-start | bytes 196
  5.4 22.0 %copy-start.2 = (f32[256,64]{0,1:T(8,128)S(1)}, f32[256,64]{0,1:T(8,128)}, u32[]{:S(2)}) copy-start(f32[256,64]{0,1:T(8,128)} %param.15) | copy-start | bytes 196612
  12.5 15.7 %copy-start.1 = (f32[256,256]{1,0:T(8,128)S(1)}, f32[256,256]{1,0:T(8,128)}, u32[]{:S(2)}) copy-start(f32[256,256]{1,0:T(8,128)} %fusion.f_ref) | copy-start | bytes 786436
  12.5 15.7 %copy-start.4 = (f32[4,256]{1,0:T(4,128)S(1)}, f32[4,256]{1,0:T(4,128)}, u32[]{:S(2)}) copy-start(f32[4,256]{1,0:T(4,128)} %param.11) | copy-start | bytes 12292
  18.3 14.3 %all-to-all-start = ((f32[16,4,256]{2,1,0:T(4,128)}), f32[16,4,256]{2,1,0:T(4,128)S(1)}, u32[]{:S(2)}, u32[]{:S(2)}) async-start(f32[16,4,256]{2,1,0:T(4,128)} %broadcast_in_dim.28), calls=%async_computation | async-start | bytes 131072 | tf_op jit(solution)/shard_map/all_to_all | solution.py:298
  43.3 10.4 %all-to-all-start.1 = ((f32[16,4,256]{2,1,0:T(4,128)}), f32[16,4,256]{2,1,0:T(4,128)S(1)}, u32[]{:S(2)}, u32[]{:S(2)}) async-start(f32[16,4,256]{2,1,0:T(4,128)} %broadcast_in_dim.29), calls=%async_computation.1 | async-start | bytes 131072 | tf_op jit(solution)/shard_map/all_to_all | solution.py:298
  84.4 10.4 %all-to-all-start.3 = ((f32[16,4,256]{2,1,0:T(4,128)}), f32[16,4,256]{2,1,0:T(4,128)S(1)}, u32[]{:S(2)}, u32[]{:S(2)}) async-start(f32[16,4,256]{2,1,0:T(4,128)} %broadcast_in_dim.31), calls=%async_computation.3 | async-start | bytes 131072 | tf_op jit(solution)/shard_map/all_to_all | solution.py:298

commit v7 on v5

--- a/solution.py
+++ b/solution.py
@@ -125,13 +125,13 @@
     return _dot((pick == want).astype(jnp.float32), g)
 
 
-def _ends(v, seg, backward):
+def _ends(v, seg, backward, out_rows):
     rows, width = v.shape
     scen = rows // seg
-    pick = lax.broadcasted_iota(jnp.int32, (scen, rows), 1)
-    want = lax.broadcasted_iota(jnp.int32, (scen, rows), 0) * seg + (0 if backward else seg - 1)
-    sel = (pick == want).astype(jnp.float32)
-    return _dot(sel, v)
+    pick = lax.broadcasted_iota(jnp.int32, (out_rows, rows), 1)
+    want = lax.broadcasted_iota(jnp.int32, (out_rows, rows), 0) % scen * seg
+    want = want + (0 if backward else seg - 1)
+    return _dot((pick == want).astype(jnp.float32), v)
 
 
 def _vmem(count):
@@ -152,7 +152,7 @@
     cut = jnp.broadcast_to(end_ref[...], cw_ref.shape)
     w1 = cw_ref[...] * ref_ref[...]
     w1_ref[...] = w1
-    e1_ref[...] = _ends(_scan(w1, cut, pwb_ref, seg, True), seg, True)
+    e1_ref[...] = _ends(_scan(w1, cut, pwb_ref, seg, True), seg, True, e1_ref.shape[0])
 
 
 def k_states_in(seg, w1_ref, end_ref, start_ref, c1_ref, fb_ref, init_ref, gain_ref, imap_ref, pwb_ref,
@@ -169,11 +169,11 @@
     init = jnp.broadcast_to(init_ref[...][:, None, :], (scen, seg, width)).reshape(rows, width)
     d2 = forcing + cut_s * init
     d2_ref[...] = d2
-    e2_ref[...] = _ends(_scan(d2, cut_s, pwf_ref, seg, False), seg, False)
+    e2_ref[...] = _ends(_scan(d2, cut_s, pwf_ref, seg, False), seg, False, e2_ref.shape[0])
 
 
 def k_adjoint_in(seg, scale, d2_ref, start_ref, end_ref, c2_ref, ff_ref, cw_ref, ref_ref, pwf_ref, pwb_ref,
-                 x_ref, w3_ref, e3_ref, cost_ref):
+                 x_ref, w3_ref, e3_ref):
     shape = d2_ref.shape
     rows, width = shape
     scen = rows // seg
@@ -187,12 +187,13 @@
     w3 = cw * offset
     w3_ref[...] = w3
     per_row = jnp.sum(w3 * offset, axis=1, keepdims=True)
-    pick = lax.broadcasted_iota(jnp.int32, (scen, rows), 1) // seg
-    want = lax.broadcasted_iota(jnp.int32, (scen, rows), 0)
+    out_rows = e3_ref.shape[0]
+    pick = lax.broadcasted_iota(jnp.int32, (out_rows, rows), 1) // seg
+    want = lax.broadcasted_iota(jnp.int32, (out_rows, rows), 0) % scen
     sel = (pick == want).astype(jnp.float32)
     per_scen = _dot(sel, jnp.broadcast_to(per_row, (rows, 128)))
-    cost_ref[...] = per_scen * scale
-    e3_ref[...] = _ends(_scan(w3, cut_e, pwb_ref, seg, True), seg, True)
+    e3_ref[:, width:] = per_scen * scale
+    e3_ref[:, :width] = _ends(_scan(w3, cut_e, pwb_ref, seg, True), seg, True, out_rows)
 
 
 def k_value_adjoint_in(seg, w3_ref, end_ref, start_ref, c3_ref, fb_ref, imap_ref, gain_ref, pwb_ref,
@@ -205,7 +206,7 @@
     pulled = _mm(adjoint, imap_ref[...])
     source = -_mm(pulled, gain_ref[...])
     s4_ref[...] = source
-    e4_ref[...] = _ends(_scan(source, cut_s, pwf_ref, seg, False), seg, False)
+    e4_ref[...] = _ends(_scan(source, cut_s, pwf_ref, seg, False), seg, False, e4_ref.shape[0])
 
 
 def k_last(seg, s4_ref, start_ref, c4_ref, ff_ref, x_ref, ref_ref, pwf_ref, g_ref):
@@ -283,7 +284,7 @@
     ref = ref_traj.reshape(rows, width)
     f32 = jnp.float32
     full = jax.ShapeDtypeStruct((rows, width), f32)
-    ends = jax.ShapeDtypeStruct((scen_count, width), f32)
+    ends = jax.ShapeDtypeStruct((devices * scen_count, width), f32)
     seg = seg_steps
 
     seg_lo = jnp.arange(devices, dtype=jnp.int32)[:, None, None] * seg_steps
@@ -293,19 +294,18 @@
     ff = 1.0 - jnp.any(in_fwd, axis=-1).astype(f32).reshape(flat)
     fb = 1.0 - jnp.any(in_bwd, axis=-1).astype(f32).reshape(flat)
 
-    def gather(end_values):
-        every = lax.all_gather(end_values[None], "tm", axis=0, tiled=True)
-        return every.reshape(devices * scen_count, end_values.shape[1])
+    def gather(copies):
+        return lax.all_to_all(copies, "tm", 0, 0, tiled=True)
 
     w1, e1 = _call(functools.partial(k_first, seg), (full, ends), cw, ref, end_col, pwb)
     d2, e2 = _call(
         functools.partial(k_states_in, seg), (full, ends),
         w1, end_col, start_col, gather(e1), fb, init_image, ff_gain, input_map, pwb, pwf)
-    cost_shape = jax.ShapeDtypeStruct((scen_count, 128), f32)
-    states, w3, e3, cost_part = _call(
-        functools.partial(k_adjoint_in, seg, 0.5 / total), (full, full, ends, cost_shape),
+    packed = jax.ShapeDtypeStruct((devices * scen_count, width + 128), f32)
+    states, w3, e3 = _call(
+        functools.partial(k_adjoint_in, seg, 0.5 / total), (full, full, packed),
         d2, start_col, end_col, gather(e2), ff, cw, ref, pwf, pwb)
-    g3 = gather(jnp.concatenate([e3, cost_part], axis=1))
+    g3 = gather(e3)
     cost = jnp.sum(g3[:, width].reshape(devices, scen_count), axis=0)
     s4, e4 = _call(
         functools.partial(k_value_adjoint_in, seg), (full, ends),

time: 138 us -> 103 us (0.75)
  blocking collectives: 78.4 us -> 9.99 us
  waiting for transfers between devices: 0 us -> 14.7 us
  starting transfers between devices: 0 us -> 14.5 us
  local copies, waits for them, and re-layouts: 8.24 us -> 12.8 us
    all_gather x4 -> x0, blocking collectives: 78.4 us -> none  [gather(): every = lax.all_gather(end_values[None], 'tm', axis=0, tiled=True)]
    all_to_all x0 -> x3, waiting for transfers between devices: none -> 14.7 us  [gather(): return lax.all_to_all(copies, 'tm', 0, 0, tiled=True)]
    all_to_all x0 -> x3, starting transfers between devices: none -> 14.5 us  [gather(): return lax.all_to_all(copies, 'tm', 0, 0, tiled=True)]
    all_to_all x0 -> x1, blocking collectives: none -> 9.99 us  [gather(): return lax.all_to_all(copies, 'tm', 0, 0, tiled=True)]
    all_to_all x0 -> x8, local copies, waits for them, and re-layouts: none -> 7.93 us  [gather(): return lax.all_to_all(copies, 'tm', 0, 0, tiled=True)]
    unnamed x9 -> x11, local copies, waits for them, and re-layouts: 4.2 us -> 0.78 us
  transfers between devices with their start and end apart: 0 -> 3, of which waited for: 0 -> 3; matrix products, arithmetic and copies ran while one was open for 0% -> 6% of each run, Pallas kernels for 0% -> 0%
where the time goes in v7:
time: 103 us; the launch traced here: 102 us
  Pallas kernels  43.9 us (43%)
  waiting for transfers between devices  14.7 us (14%)
  starting transfers between devices  14.5 us (14%)
  local copies, waits for them, and re-layouts  12.8 us (12%)
  blocking collectives  9.99 us (10%)
  matrix products  3.1 us (3%)
  other arithmetic  2.56 us (2%)
    pallas_call x6, Pallas kernels, _call(): pl.pallas_call(kernel, out_shape=outs, in_specs=_vmem(len(args)), out_spe...  43.9 us
    all_to_all x3, waiting for transfers between devices, gather(): return lax.all_to_all(copies, 'tm', 0, 0, tiled=True)  14.7 us
    all_to_all x3, starting transfers between devices, gather(): return lax.all_to_all(copies, 'tm', 0, 0, tiled=True)  14.5 us
    all_to_all x1, blocking collectives, gather(): return lax.all_to_all(copies, 'tm', 0, 0, tiled=True)  9.99 us
    all_to_all x8, local copies, waits for them, and re-layouts, gather(): return lax.all_to_all(copies, 'tm', 0, 0, tiled=True)  7.93 us
    dot_general x2, matrix products, build_dynamics(): jnp.einsum('lia,lab,ljb->ij', row_hot, coupling, col_hot, precision=lax.P...  2.18 us
  transfers between devices with their start and end apart: 3, of which 3 were waited for; matrix products, arithmetic and copies ran while one was open for 6% of the time, Pallas kernels for 0%

profile of v7, /device:TPU:0, one launch (start us, length us, event | category | flops | bytes accessed | tf_op | source)
XLA Modules:
  0.0 102.3 jit_solution(4704699466149020820)
XLA Ops:
  0.6 0.0 copy-start
  0.7 0.8 multiply_bitcast_fusion
  1.4 0.9 reduce_window_sum.11
  2.3 0.1 compare_reduce_fusion.1
  2.4 0.8 reshape.182.end_ref
  3.2 0.1 iota_add_fusion
  3.2 0.0 copy-done
  3.2 0.3 convolution_bitcast_fusion.1
  3.6 1.9 %fusion.f_ref = f32[256,256]{1,0:T(8,128)} fusion(f32[3,64,256]{2,1,0:T(8,128)S(1)} %convolution_bitcast_fusion.1, f32[256]{0:T(256)} %param.12, s32[3,64]{1,0:T(4,128)S(1)} %get-tuple-element.27), kind=kOutput, calls=%fused_computation.1 | convolution fusion | flops 151240704 | bytes 460544 | tf_op jit(solution)/shard_map/lia,lab,ljb->ij/dot_general | solution.py:24
  5.4 0.0 copy-start.3
  5.4 0.0 copy-start.2
  5.4 7.1 %shard_map.112.pwb_ref.pwf_ref = f32[10,256,256]{2,1,0:T(8,128)} custom-call(f32[256,256]{1,0:T(8,128)} %fusion.f_ref), custom_call_target="tpu_custom_call" | custom-call | tf_op jit(solution)/shard_map/pallas_call | solution.py:142
  12.5 4.5 %shard_map.113 = (f32[256,256]{1,0:T(8,128)}, f32[64,256]{1,0:T(8,128)}) custom-call(f32[256,256]{1,0:T(8,128)} %bitcast.23, f32[256,256]{1,0:T(8,128)} %bitcast.20, f32[256,1]{1,0:T(8,128)} %reshape.182.end_ref, f32[10,256,256]{2,1,0:T(8,128)} %shard_map.112.pwb_ref.pwf_ref), custom_call_target="tpu_custom_call" | custom-call | tf_op jit(solution)/shard_map/pallas_call | solution.py:142
  17.0 1.5 %all_to_all.28 = f32[16,4,256]{2,1,0:T(4,128)} reshape(f32[64,256]{1,0:T(8,128)} %get-tuple-element.13) | data formatting | bytes 131072 | tf_op jit(solution)/shard_map/all_to_all | solution.py:298
  18.5 7.4 %all-to-all-start = ((f32[16,4,256]{2,1,0:T(4,128)}), f32[16,4,256]{2,1,0:T(4,128)S(1)}, u32[]{:S(2)}, u32[]{:S(2)}) async-start(f32[16,4,256]{2,1,0:T(4,128)} %all_to_all.28), calls=%async_computation | async-start | bytes 131072 | tf_op jit(solution)/shard_map/all_to_all | solution.py:298
  25.9 0.0 copy-done.3
  25.9 0.1 compare_reduce_fusion
  26.0 0.1 and_reduce_fusion
  26.1 0.1 copy.34
  26.2 0.7 sub.18.fb_ref
  26.9 0.8 reshape.183.start_ref
  27.7 0.0 copy-done.2
  27.7 0.8 copy.38.imap_ref
  28.4 0.0 copy-done.1
  28.4 0.0 copy-done.4
  28.4 0.9 convolution_bitcast_fusion.2.init_ref
  29.4 3.4 %all-to-all-done = f32[16,4,256]{2,1,0:T(4,128)S(1)} async-done(((f32[16,4,256]{2,1,0:T(4,128)}), f32[16,4,256]{2,1,0:T(4,128)S(1)}, u32[]{:S(2)}, u32[]{:S(2)}) %all-to-all-start) | async-done | bytes 65568 | tf_op jit(solution)/shard_map/all_to_all | solution.py:298
  32.8 0.6 all_to_all.30.c1_ref
  33.4 8.8 %shard_map.114 = (f32[256,256]{1,0:T(8,128)}, f32[64,256]{1,0:T(8,128)}) custom-call(f32[256,256]{1,0:T(8,128)} %get-tuple-element.12.w1_ref, f32[256,1]{1,0:T(8,128)} %reshape.182.end_ref, f32[256,1]{1,0:T(8,128)} %reshape.183.start_ref, f32[64,256]{1,0:T(8,128)} %all_to_all.30.c1_ref, f32[64,1]{1,0:T(8,128)} %sub.18.fb_ref, ...), custom_call_target="tpu_custom_call" | custom-call | tf_op jit(solution)/shard_map/pallas_call | solution.py:142
  42.2 1.5 %all_to_all.31 = f32[16,4,256]{2,1,0:T(4,128)} reshape(f32[64,256]{1,0:T(8,128)} %get-tuple-element.15) | data formatting | bytes 131072 | tf_op jit(solution)/shard_map/all_to_all | solution.py:298
  43.7 3.7 %all-to-all-start.1 = ((f32[16,4,256]{2,1,0:T(4,128)}), f32[16,4,256]{2,1,0:T(4,128)S(1)}, u32[]{:S(2)}, u32[]{:S(2)}) async-start(f32[16,4,256]{2,1,0:T(4,128)} %all_to_all.31), calls=%async_computation.1 | async-start | bytes 131072 | tf_op jit(solution)/shard_map/all_to_all | solution.py:298
  47.4 0.1 copy.39
  47.5 0.7 sub.19.ff_ref
  48.2 5.9 %all-to-all-done.1 = f32[16,4,256]{2,1,0:T(4,128)S(1)} async-done(((f32[16,4,256]{2,1,0:T(4,128)}), f32[16,4,256]{2,1,0:T(4,128)S(1)}, u32[]{:S(2)}, u32[]{:S(2)}) %all-to-all-start.1) | async-done | bytes 65568 | tf_op jit(solution)/shard_map/all_to_all | solution.py:298
  54.1 0.6 all_to_all.33.c2_ref
  54.7 8.8 %shard_map.115 = (f32[256,256]{1,0:T(8,128)}, f32[256,256]{1,0:T(8,128)}, f32[64,384]{1,0:T(8,128)}) custom-call(f32[256,256]{1,0:T(8,128)} %get-tuple-element.14.d2_ref, f32[256,1]{1,0:T(8,128)} %reshape.183.start_ref, f32[256,1]{1,0:T(8,128)} %reshape.182.end_ref, f32[64,256]{1,0:T(8,128)} %all_to_all.33.c2_ref, f32[64,1]{1,0:T(8,128)} %sub.19.ff_ref, ...), custom_call_target="tpu_custom_call" | custom-call | tf_op jit(solution)/shard_map/pallas_call | solution.py:142
  63.5 0.9 all_to_all.34
  64.4 10.0 %all_to_all.44 = f32[16,4,384]{2,1,0:T(4,128)S(1)} all-to-all(f32[16,4,384]{2,1,0:T(4,128)S(1)} %all_to_all.34), channel_id=1, replica_groups=mesh['groups'=2,'tm'=16] {'tm'}, dimensions={0} | all-to-all | bytes 196608 | tf_op jit(solution)/shard_map/all_to_all | solution.py:298
  74.4 0.7 all_to_all.36.c3_ref
  75.1 8.8 %shard_map.116 = (f32[256,256]{1,0:T(8,128)}, f32[64,256]{1,0:T(8,128)}) custom-call(f32[256,256]{1,0:T(8,128)} %get-tuple-element.17.w3_ref, f32[256,1]{1,0:T(8,128)} %reshape.182.end_ref, f32[256,1]{1,0:T(8,128)} %reshape.183.start_ref, f32[64,384]{1,0:T(8,128)} %all_to_all.36.c3_ref, f32[64,1]{1,0:T(8,128)} %sub.18.fb_ref, f32[256,64]{1,0:T(8,128)} %copy.38.imap_ref, ...), custom_call_target="tpu_custom_call" | custom-call | tf_op jit(solution)/shard_map/pallas_call | solution.py:142
  83.9 1.5 %all_to_all.37 = f32[16,4,256]{2,1,0:T(4,128)} reshape(f32[64,256]{1,0:T(8,128)} %get-tuple-element.20) | data formatting | bytes 131072 | tf_op jit(solution)/shard_map/all_to_all | solution.py:298
  85.4 3.5 %all-to-all-start.3 = ((f32[16,4,256]{2,1,0:T(4,128)}), f32[16,4,256]{2,1,0:T(4,128)S(1)}, u32[]{:S(2)}, u32[]{:S(2)}) async-start(f32[16,4,256]{2,1,0:T(4,128)} %all_to_all.37), calls=%async_computation.3 | async-start | bytes 131072 | tf_op jit(solution)/shard_map/all_to_all | solution.py:298
  88.9 0.9 slice_reduce_fusion
  89.7 0.1 reshape_squeeze.3
  89.8 0.6 reduce_sum.9
  90.4 5.4 %all-to-all-done.3 = f32[16,4,256]{2,1,0:T(4,128)S(1)} async-done(((f32[16,4,256]{2,1,0:T(4,128)}), f32[16,4,256]{2,1,0:T(4,128)S(1)}, u32[]{:S(2)}, u32[]{:S(2)}) %all-to-all-start.3) | async-done | bytes 65568 | tf_op jit(solution)/shard_map/all_to_all | solution.py:298
  95.7 0.6 all_to_all.39.c4_ref
  96.4 5.9 %shard_map.117 = f32[256,256]{1,0:T(8,128)} custom-call(f32[256,256]{1,0:T(8,128)} %get-tuple-element.19.s4_ref, f32[256,1]{1,0:T(8,128)} %reshape.183.start_ref, f32[64,256]{1,0:T(8,128)} %all_to_all.39.c4_ref, f32[64,1]{1,0:T(8,128)} %sub.19.ff_ref, f32[256,256]{1,0:T(8,128)} %get-tuple-element.16.x_ref, f32[256,256]{1,0:T(8,128)} %bitcast.22, ...), custom_call_target="tpu_custom_call" | custom-call | tf_op jit(solution)/shard_map/pallas_call | solution.py:142
  (9 shorter events, 0.0 us)
Async XLA Ops:
  0.6 2.6 %copy-start = (f32[3,64,64]{2,1,0:T(8,128)S(1)}, f32[3,64,64]{2,1,0:T(8,128)}, u32[]{:S(2)}) copy-start(f32[3,64,64]{2,1,0:T(8,128)} %param.13) | copy-start | bytes 147460
  5.4 20.5 %copy-start.3 = (s32[4,4]{1,0:T(4,128)S(1)}, s32[4,4]{1,0:T(4,128)}, u32[]{:S(2)}) copy-start(s32[4,4]{1,0:T(4,128)} %param.17) | copy-start | bytes 196
  5.4 22.2 %copy-start.2 = (f32[256,64]{0,1:T(8,128)S(1)}, f32[256,64]{0,1:T(8,128)}, u32[]{:S(2)}) copy-start(f32[256,64]{0,1:T(8,128)} %param.15) | copy-start | bytes 196612
  12.5 15.9 %copy-start.1 = (f32[256,256]{1,0:T(8,128)S(1)}, f32[256,256]{1,0:T(8,128)}, u32[]{:S(2)}) copy-start(f32[256,256]{1,0:T(8,128)} %fusion.f_ref) | copy-start | bytes 786436
  12.5 15.9 %copy-start.4 = (f32[4,256]{1,0:T(4,128)S(1)}, f32[4,256]{1,0:T(4,128)}, u32[]{:S(2)}) copy-start(f32[4,256]{1,0:T(4,128)} %param.11) | copy-start | bytes 12292
  18.5 14.3 %all-to-all-start = ((f32[16,4,256]{2,1,0:T(4,128)}), f32[16,4,256]{2,1,0:T(4,128)S(1)}, u32[]{:S(2)}, u32[]{:S(2)}) async-start(f32[16,4,256]{2,1,0:T(4,128)} %all_to_all.28), calls=%async_computation | async-start | bytes 131072 | tf_op jit(solution)/shard_map/all_to_all | solution.py:298
  43.7 10.4 %all-to-all-start.1 = ((f32[16,4,256]{2,1,0:T(4,128)}), f32[16,4,256]{2,1,0:T(4,128)S(1)}, u32[]{:S(2)}, u32[]{:S(2)}) async-start(f32[16,4,256]{2,1,0:T(4,128)} %all_to_all.31), calls=%async_computation.1 | async-start | bytes 131072 | tf_op jit(solution)/shard_map/all_to_all | solution.py:298
  85.4 10.4 %all-to-all-start.3 = ((f32[16,4,256]{2,1,0:T(4,128)}), f32[16,4,256]{2,1,0:T(4,128)S(1)}, u32[]{:S(2)}, u32[]{:S(2)}) async-start(f32[16,4,256]{2,1,0:T(4,128)} %all_to_all.37), calls=%async_computation.3 | async-start | bytes 131072 | tf_op jit(solution)/shard_map/all_to_all | solution.py:298

commit v8 on v7

--- a/solution.py
+++ b/solution.py
@@ -128,10 +128,10 @@
 def _ends(v, seg, backward, out_rows):
     rows, width = v.shape
     scen = rows // seg
-    pick = lax.broadcasted_iota(jnp.int32, (out_rows, rows), 1)
-    want = lax.broadcasted_iota(jnp.int32, (out_rows, rows), 0) % scen * seg
-    want = want + (0 if backward else seg - 1)
-    return _dot((pick == want).astype(jnp.float32), v)
+    pick = lax.broadcasted_iota(jnp.int32, (scen, rows), 1)
+    want = lax.broadcasted_iota(jnp.int32, (scen, rows), 0) * seg + (0 if backward else seg - 1)
+    ends = _dot((pick == want).astype(jnp.float32), v)
+    return jnp.broadcast_to(ends[None], (out_rows,) + ends.shape)
 
 
 def _vmem(count):
@@ -187,13 +187,13 @@
     w3 = cw * offset
     w3_ref[...] = w3
     per_row = jnp.sum(w3 * offset, axis=1, keepdims=True)
-    out_rows = e3_ref.shape[0]
-    pick = lax.broadcasted_iota(jnp.int32, (out_rows, rows), 1) // seg
-    want = lax.broadcasted_iota(jnp.int32, (out_rows, rows), 0) % scen
+    copies = e3_ref.shape[0]
+    pick = lax.broadcasted_iota(jnp.int32, (scen, rows), 1) // seg
+    want = lax.broadcasted_iota(jnp.int32, (scen, rows), 0)
     sel = (pick == want).astype(jnp.float32)
-    per_scen = _dot(sel, jnp.broadcast_to(per_row, (rows, 128)))
-    e3_ref[:, width:] = per_scen * scale
-    e3_ref[:, :width] = _ends(_scan(w3, cut_e, pwb_ref, seg, True), seg, True, out_rows)
+    per_scen = _dot(sel, jnp.broadcast_to(per_row, (rows, 128))) * scale
+    e3_ref[:, :, width:] = jnp.broadcast_to(per_scen[None], (copies, scen, 128))
+    e3_ref[:, :, :width] = _ends(_scan(w3, cut_e, pwb_ref, seg, True), seg, True, copies)
 
 
 def k_value_adjoint_in(seg, w3_ref, end_ref, start_ref, c3_ref, fb_ref, imap_ref, gain_ref, pwb_ref,
@@ -284,7 +284,7 @@
     ref = ref_traj.reshape(rows, width)
     f32 = jnp.float32
     full = jax.ShapeDtypeStruct((rows, width), f32)
-    ends = jax.ShapeDtypeStruct((devices * scen_count, width), f32)
+    ends = jax.ShapeDtypeStruct((devices, scen_count, width), f32)
     seg = seg_steps
 
     seg_lo = jnp.arange(devices, dtype=jnp.int32)[:, None, None] * seg_steps
@@ -295,13 +295,14 @@
     fb = 1.0 - jnp.any(in_bwd, axis=-1).astype(f32).reshape(flat)
 
     def gather(copies):
-        return lax.all_to_all(copies, "tm", 0, 0, tiled=True)
+        every = lax.all_to_all(copies, "tm", 0, 0, tiled=True)
+        return every.reshape(devices * scen_count, copies.shape[2])
 
     w1, e1 = _call(functools.partial(k_first, seg), (full, ends), cw, ref, end_col, pwb)
     d2, e2 = _call(
         functools.partial(k_states_in, seg), (full, ends),
         w1, end_col, start_col, gather(e1), fb, init_image, ff_gain, input_map, pwb, pwf)
-    packed = jax.ShapeDtypeStruct((devices * scen_count, width + 128), f32)
+    packed = jax.ShapeDtypeStruct((devices, scen_count, width + 128), f32)
     states, w3, e3 = _call(
         functools.partial(k_adjoint_in, seg, 0.5 / total), (full, full, packed),
         d2, start_col, end_col, gather(e2), ff, cw, ref, pwf, pwb)

time: 103 us -> 98.3 us (0.954)
  local copies, waits for them, and re-layouts: 12.8 us -> 7.41 us
    all_to_all x8 -> x0, local copies, waits for them, and re-layouts: 7.93 us -> none  [gather(): return lax.all_to_all(copies, 'tm', 0, 0, tiled=True)]
    reshape x0 -> x4, local copies, waits for them, and re-layouts: none -> 2.59 us  [gather(): return every.reshape(devices * scen_count, copies.shape[2])]
where the time goes in v8:
time: 98.3 us; the launch traced here: 97.7 us
  Pallas kernels  43.8 us (45%)
  waiting for transfers between devices  14.7 us (15%)
  starting transfers between devices  14.5 us (15%)
  blocking collectives  10.9 us (11%)
  local copies, waits for them, and re-layouts  7.41 us (8%)
  matrix products  3.1 us (3%)
  other arithmetic  2.56 us (3%)
    pallas_call x6, Pallas kernels, _call(): pl.pallas_call(kernel, out_shape=outs, in_specs=_vmem(len(args)), out_spe...  43.8 us
    all_to_all x3, waiting for transfers between devices, gather(): every = lax.all_to_all(copies, 'tm', 0, 0, tiled=True)  14.7 us
    all_to_all x3, starting transfers between devices, gather(): every = lax.all_to_all(copies, 'tm', 0, 0, tiled=True)  14.5 us
    all_to_all x1, blocking collectives, gather(): every = lax.all_to_all(copies, 'tm', 0, 0, tiled=True)  10.9 us
    reshape x4, local copies, waits for them, and re-layouts, gather(): return every.reshape(devices * scen_count, copies.shape[2])  2.59 us
    dot_general x2, matrix products, build_dynamics(): jnp.einsum('lia,lab,ljb->ij', row_hot, coupling, col_hot, precision=lax.P...  2.18 us
  transfers between devices with their start and end apart: 3, of which 3 were waited for; matrix products, arithmetic and copies ran while one was open for 6% of the time, Pallas kernels for 0%

profile of v8, /device:TPU:0, one launch (start us, length us, event | category | flops | bytes accessed | tf_op | source)
XLA Modules:
  0.0 97.7 jit_solution(3765737297015229231)
XLA Ops:
  0.6 0.0 copy-start
  0.7 0.8 multiply_bitcast_fusion
  1.4 0.9 reduce_window_sum.11
  2.3 0.1 compare_reduce_fusion.1
  2.4 0.8 reshape.190.end_ref
  3.2 0.1 iota_add_fusion
  3.2 0.0 copy-done
  3.2 0.3 convolution_bitcast_fusion.1
  3.6 1.9 %fusion.f_ref = f32[256,256]{1,0:T(8,128)} fusion(f32[3,64,256]{2,1,0:T(8,128)S(1)} %convolution_bitcast_fusion.1, f32[256]{0:T(256)} %param.12, s32[3,64]{1,0:T(4,128)S(1)} %get-tuple-element.27), kind=kOutput, calls=%fused_computation.1 | convolution fusion | flops 151240704 | bytes 460544 | tf_op jit(solution)/shard_map/lia,lab,ljb->ij/dot_general | solution.py:24
  5.4 0.0 copy-start.3
  5.4 0.0 copy-start.2
  5.4 7.1 %shard_map.112.pwb_ref.pwf_ref = f32[10,256,256]{2,1,0:T(8,128)} custom-call(f32[256,256]{1,0:T(8,128)} %fusion.f_ref), custom_call_target="tpu_custom_call" | custom-call | tf_op jit(solution)/shard_map/pallas_call | solution.py:142
  12.5 0.0 copy-start.1
  12.5 0.0 copy-start.4
  12.5 4.5 %shard_map.113 = (f32[256,256]{1,0:T(8,128)}, f32[16,4,256]{2,1,0:T(4,128)}) custom-call(f32[256,256]{1,0:T(8,128)} %bitcast.23, f32[256,256]{1,0:T(8,128)} %bitcast.20, f32[256,1]{1,0:T(8,128)} %reshape.190.end_ref, f32[10,256,256]{2,1,0:T(8,128)} %shard_map.112.pwb_ref.pwf_ref), custom_call_target="tpu_custom_call" | custom-call | tf_op jit(solution)/shard_map/pallas_call | solution.py:142
  17.0 7.4 %all-to-all-start = ((f32[16,4,256]{2,1,0:T(4,128)}), f32[16,4,256]{2,1,0:T(4,128)S(1)}, u32[]{:S(2)}, u32[]{:S(2)}) async-start(f32[16,4,256]{2,1,0:T(4,128)} %get-tuple-element.13), calls=%async_computation | async-start | bytes 131072 | tf_op jit(solution)/shard_map/all_to_all | solution.py:298
  24.4 0.0 copy-done.3
  24.4 0.1 compare_reduce_fusion
  24.5 0.1 and_reduce_fusion
  24.6 0.1 copy.34
  24.7 0.7 sub.18.fb_ref
  25.4 0.8 reshape.191.start_ref
  26.2 0.0 copy-done.2
  26.2 0.8 copy.38.imap_ref
  26.9 0.0 copy-done.1
  26.9 0.0 copy-done.4
  26.9 0.9 convolution_bitcast_fusion.2.init_ref
  27.9 3.4 %all-to-all-done = f32[16,4,256]{2,1,0:T(4,128)S(1)} async-done(((f32[16,4,256]{2,1,0:T(4,128)}), f32[16,4,256]{2,1,0:T(4,128)S(1)}, u32[]{:S(2)}, u32[]{:S(2)}) %all-to-all-start) | async-done | bytes 65568 | tf_op jit(solution)/shard_map/all_to_all | solution.py:298
  31.3 0.6 reshape.181.c1_ref
  31.9 8.8 %shard_map.114 = (f32[256,256]{1,0:T(8,128)}, f32[16,4,256]{2,1,0:T(4,128)}) custom-call(f32[256,256]{1,0:T(8,128)} %get-tuple-element.12.w1_ref, f32[256,1]{1,0:T(8,128)} %reshape.190.end_ref, f32[256,1]{1,0:T(8,128)} %reshape.191.start_ref, f32[64,256]{1,0:T(8,128)} %reshape.181.c1_ref, f32[64,1]{1,0:T(8,128)} %sub.18.fb_ref, ...), custom_call_target="tpu_custom_call" | custom-call | tf_op jit(solution)/shard_map/pallas_call | solution.py:142
  40.7 3.7 %all-to-all-start.1 = ((f32[16,4,256]{2,1,0:T(4,128)}), f32[16,4,256]{2,1,0:T(4,128)S(1)}, u32[]{:S(2)}, u32[]{:S(2)}) async-start(f32[16,4,256]{2,1,0:T(4,128)} %get-tuple-element.15), calls=%async_computation.1 | async-start | bytes 131072 | tf_op jit(solution)/shard_map/all_to_all | solution.py:298
  44.4 0.1 copy.39
  44.5 0.7 sub.19.ff_ref
  45.1 5.9 %all-to-all-done.1 = f32[16,4,256]{2,1,0:T(4,128)S(1)} async-done(((f32[16,4,256]{2,1,0:T(4,128)}), f32[16,4,256]{2,1,0:T(4,128)S(1)}, u32[]{:S(2)}, u32[]{:S(2)}) %all-to-all-start.1) | async-done | bytes 65568 | tf_op jit(solution)/shard_map/all_to_all | solution.py:298
  51.1 0.6 reshape.182.c2_ref
  51.7 8.8 %shard_map.115 = (f32[256,256]{1,0:T(8,128)}, f32[256,256]{1,0:T(8,128)}, f32[16,4,384]{2,1,0:T(4,128)}) custom-call(f32[256,256]{1,0:T(8,128)} %get-tuple-element.14.d2_ref, f32[256,1]{1,0:T(8,128)} %reshape.191.start_ref, f32[256,1]{1,0:T(8,128)} %reshape.190.end_ref, f32[64,256]{1,0:T(8,128)} %reshape.182.c2_ref, f32[64,1]{1,0:T(8,128)} %sub.19.ff_ref, ...), custom_call_target="tpu_custom_call" | custom-call | tf_op jit(solution)/shard_map/pallas_call | solution.py:142
  60.4 10.9 %all_to_all.20 = f32[16,4,384]{2,1,0:T(4,128)S(1)} all-to-all(f32[16,4,384]{2,1,0:T(4,128)} %get-tuple-element.18), channel_id=1, replica_groups=mesh['groups'=2,'tm'=16] {'tm'}, dimensions={0} | all-to-all | bytes 196608 | tf_op jit(solution)/shard_map/all_to_all | solution.py:298
  71.3 0.7 reshape.184.c3_ref
  72.0 8.8 %shard_map.116 = (f32[256,256]{1,0:T(8,128)}, f32[16,4,256]{2,1,0:T(4,128)}) custom-call(f32[256,256]{1,0:T(8,128)} %get-tuple-element.17.w3_ref, f32[256,1]{1,0:T(8,128)} %reshape.190.end_ref, f32[256,1]{1,0:T(8,128)} %reshape.191.start_ref, f32[64,384]{1,0:T(8,128)} %reshape.184.c3_ref, f32[64,1]{1,0:T(8,128)} %sub.18.fb_ref, f32[256,64]{1,0:T(8,128)} %copy.38.imap_ref, ...), custom_call_target="tpu_custom_call" | custom-call | tf_op jit(solution)/shard_map/pallas_call | solution.py:142
  80.8 3.5 %all-to-all-start.3 = ((f32[16,4,256]{2,1,0:T(4,128)}), f32[16,4,256]{2,1,0:T(4,128)S(1)}, u32[]{:S(2)}, u32[]{:S(2)}) async-start(f32[16,4,256]{2,1,0:T(4,128)} %get-tuple-element.20), calls=%async_computation.3 | async-start | bytes 131072 | tf_op jit(solution)/shard_map/all_to_all | solution.py:298
  84.3 0.9 slice_reduce_fusion
  85.2 0.1 reshape_squeeze.3
  85.2 0.6 reduce_sum.9
  85.8 5.4 %all-to-all-done.3 = f32[16,4,256]{2,1,0:T(4,128)S(1)} async-done(((f32[16,4,256]{2,1,0:T(4,128)}), f32[16,4,256]{2,1,0:T(4,128)S(1)}, u32[]{:S(2)}, u32[]{:S(2)}) %all-to-all-start.3) | async-done | bytes 65568 | tf_op jit(solution)/shard_map/all_to_all | solution.py:298
  91.2 0.6 reshape.185.c4_ref
  91.8 5.9 %shard_map.117 = f32[256,256]{1,0:T(8,128)} custom-call(f32[256,256]{1,0:T(8,128)} %get-tuple-element.19.s4_ref, f32[256,1]{1,0:T(8,128)} %reshape.191.start_ref, f32[64,256]{1,0:T(8,128)} %reshape.185.c4_ref, f32[64,1]{1,0:T(8,128)} %sub.19.ff_ref, f32[256,256]{1,0:T(8,128)} %get-tuple-element.16.x_ref, f32[256,256]{1,0:T(8,128)} %bitcast.22, ...), custom_call_target="tpu_custom_call" | custom-call | tf_op jit(solution)/shard_map/pallas_call | solution.py:142
  (7 shorter events, 0.0 us)
Async XLA Ops:
  0.6 2.6 %copy-start = (f32[3,64,64]{2,1,0:T(8,128)S(1)}, f32[3,64,64]{2,1,0:T(8,128)}, u32[]{:S(2)}) copy-start(f32[3,64,64]{2,1,0:T(8,128)} %param.13) | copy-start | bytes 147460
  5.4 19.0 %copy-start.3 = (s32[4,4]{1,0:T(4,128)S(1)}, s32[4,4]{1,0:T(4,128)}, u32[]{:S(2)}) copy-start(s32[4,4]{1,0:T(4,128)} %param.17) | copy-start | bytes 196
  5.4 20.7 %copy-start.2 = (f32[256,64]{0,1:T(8,128)S(1)}, f32[256,64]{0,1:T(8,128)}, u32[]{:S(2)}) copy-start(f32[256,64]{0,1:T(8,128)} %param.15) | copy-start | bytes 196612
  12.5 14.4 %copy-start.1 = (f32[256,256]{1,0:T(8,128)S(1)}, f32[256,256]{1,0:T(8,128)}, u32[]{:S(2)}) copy-start(f32[256,256]{1,0:T(8,128)} %fusion.f_ref) | copy-start | bytes 786436
  12.5 14.4 %copy-start.4 = (f32[4,256]{1,0:T(4,128)S(1)}, f32[4,256]{1,0:T(4,128)}, u32[]{:S(2)}) copy-start(f32[4,256]{1,0:T(4,128)} %param.11) | copy-start | bytes 12292
  17.0 14.3 %all-to-all-start = ((f32[16,4,256]{2,1,0:T(4,128)}), f32[16,4,256]{2,1,0:T(4,128)S(1)}, u32[]{:S(2)}, u32[]{:S(2)}) async-start(f32[16,4,256]{2,1,0:T(4,128)} %get-tuple-element.13), calls=%async_computation | async-start | bytes 131072 | tf_op jit(solution)/shard_map/all_to_all | solution.py:298
  40.7 10.4 %all-to-all-start.1 = ((f32[16,4,256]{2,1,0:T(4,128)}), f32[16,4,256]{2,1,0:T(4,128)S(1)}, u32[]{:S(2)}, u32[]{:S(2)}) async-start(f32[16,4,256]{2,1,0:T(4,128)} %get-tuple-element.15), calls=%async_computation.1 | async-start | bytes 131072 | tf_op jit(solution)/shard_map/all_to_all | solution.py:298
  80.8 10.4 %all-to-all-start.3 = ((f32[16,4,256]{2,1,0:T(4,128)}), f32[16,4,256]{2,1,0:T(4,128)S(1)}, u32[]{:S(2)}, u32[]{:S(2)}) async-start(f32[16,4,256]{2,1,0:T(4,128)} %get-tuple-element.20), calls=%async_computation.3 | async-start | bytes 131072 | tf_op jit(solution)/shard_map/all_to_all | solution.py:298

commit v9 on v8

--- a/solution.py
+++ b/solution.py
@@ -57,8 +57,10 @@
     return part(a_lo, b_hi) + part(a_hi, b_lo) + part(a_hi, b_hi)
 
 
-def k_powers(f_ref, out_ref):
+def k_powers(square_first, f_ref, out_ref):
     power = f_ref[...]
+    if square_first:
+        power = _dot(power, power)
     out_ref[0] = power
     for level in range(1, out_ref.shape[0]):
         power = _dot(power, power)
@@ -95,34 +97,34 @@
     return v
 
 
-def _carry(g_ref, fl_ref, pw_ref, scen, backward):
-    width = pw_ref.shape[1]
-    g = g_ref[...][:, :width]
+def _carry(g_ref, fl_ref, pd_ref, backward):
+    devices, scen = g_ref.shape[0], g_ref.shape[1]
+    width = pd_ref.shape[1]
+    g = jnp.concatenate([g_ref[:, s, :width] for s in range(scen)], axis=0)
     rows = g.shape[0]
-    devices = rows // scen
-    local_levels = pw_ref.shape[0] - max((devices - 1).bit_length(), 1)
-    r = lax.broadcasted_iota(jnp.int32, (rows, width), 0)
+    j = lax.broadcasted_iota(jnp.int32, (rows, width), 0) % devices
     flags = jnp.broadcast_to(fl_ref[...], (rows, width))
     step = functools.partial(_mm, nt=not backward)
     for level in range((devices - 1).bit_length()):
-        stride = scen * 2**level
+        stride = 2**level
         if backward:
             prior_g = pltpu.roll(g, rows - stride, 0)
             prior_f = pltpu.roll(flags, rows - stride, 0)
-            valid = r < rows - stride
+            valid = j < devices - stride
         else:
             prior_g = pltpu.roll(g, stride, 0)
             prior_f = pltpu.roll(flags, stride, 0)
-            valid = r >= stride
+            valid = j >= stride
         prior_g = jnp.where(valid, prior_g, 0.0)
         prior_f = jnp.where(valid, prior_f, 1.0)
-        g = g + flags * step(prior_g, pw_ref[local_levels + level])
+        g = g + flags * step(prior_g, pd_ref[level])
         flags = flags * prior_f
     me = lax.axis_index("tm")
     target = me + 1 if backward else me - 1
     pick = lax.broadcasted_iota(jnp.int32, (scen, rows), 1)
-    want = lax.broadcasted_iota(jnp.int32, (scen, rows), 0) + target * scen
-    return _dot((pick == want).astype(jnp.float32), g)
+    want = lax.broadcasted_iota(jnp.int32, (scen, rows), 0) * devices + target
+    hit = (pick == want) & (target >= 0) & (target < devices)
+    return _dot(hit.astype(jnp.float32), g)
 
 
 def _ends(v, seg, backward, out_rows):
@@ -156,11 +158,11 @@
 
 
 def k_states_in(seg, w1_ref, end_ref, start_ref, c1_ref, fb_ref, init_ref, gain_ref, imap_ref, pwb_ref,
-                pwf_ref, d2_ref, e2_ref):
+                pwf_ref, pd_ref, d2_ref, e2_ref):
     shape = w1_ref.shape
     cut_e = jnp.broadcast_to(end_ref[...], shape)
     cut_s = jnp.broadcast_to(start_ref[...], shape)
-    c1 = _carry(c1_ref, fb_ref, pwb_ref, w1_ref.shape[0] // seg, True)
+    c1 = _carry(c1_ref, fb_ref, pd_ref, True)
     vt = _scan(w1_ref[...], cut_e, pwb_ref, seg, True, c1)
     controls = _mm(vt, gain_ref[...], nt=True)
     forcing = -_mm(controls, imap_ref[...], nt=True)
@@ -173,13 +175,13 @@
 
 
 def k_adjoint_in(seg, scale, d2_ref, start_ref, end_ref, c2_ref, ff_ref, cw_ref, ref_ref, pwf_ref, pwb_ref,
-                 x_ref, w3_ref, e3_ref):
+                 pd_ref, x_ref, w3_ref, e3_ref):
     shape = d2_ref.shape
     rows, width = shape
     scen = rows // seg
     cut_s = jnp.broadcast_to(start_ref[...], shape)
     cut_e = jnp.broadcast_to(end_ref[...], shape)
-    c2 = _carry(c2_ref, ff_ref, pwf_ref, scen, False)
+    c2 = _carry(c2_ref, ff_ref, pd_ref, False)
     states = _scan(d2_ref[...], cut_s, pwf_ref, seg, False, c2)
     x_ref[...] = states
     offset = states - ref_ref[...]
@@ -197,11 +199,11 @@
 
 
 def k_value_adjoint_in(seg, w3_ref, end_ref, start_ref, c3_ref, fb_ref, imap_ref, gain_ref, pwb_ref,
-                       pwf_ref, s4_ref, e4_ref):
+                       pwf_ref, pd_ref, s4_ref, e4_ref):
     shape = w3_ref.shape
     cut_e = jnp.broadcast_to(end_ref[...], shape)
     cut_s = jnp.broadcast_to(start_ref[...], shape)
-    c3 = _carry(c3_ref, fb_ref, pwb_ref, w3_ref.shape[0] // seg, True)
+    c3 = _carry(c3_ref, fb_ref, pd_ref, True)
     adjoint = _scan(w3_ref[...], cut_e, pwb_ref, seg, True, c3)
     pulled = _mm(adjoint, imap_ref[...])
     source = -_mm(pulled, gain_ref[...])
@@ -209,10 +211,10 @@
     e4_ref[...] = _ends(_scan(source, cut_s, pwf_ref, seg, False), seg, False, e4_ref.shape[0])
 
 
-def k_last(seg, s4_ref, start_ref, c4_ref, ff_ref, x_ref, ref_ref, pwf_ref, g_ref):
+def k_last(seg, s4_ref, start_ref, c4_ref, ff_ref, x_ref, ref_ref, pwf_ref, pd_ref, g_ref):
     shape = s4_ref.shape
     cut_s = jnp.broadcast_to(start_ref[...], shape)
-    c4 = _carry(c4_ref, ff_ref, pwf_ref, s4_ref.shape[0] // seg, False)
+    c4 = _carry(c4_ref, ff_ref, pd_ref, False)
     va = _scan(s4_ref[...], cut_s, pwf_ref, seg, False, c4)
     ref = ref_ref[...]
     offset = x_ref[...] - ref
@@ -267,7 +269,12 @@
     device_levels = (devices - 1).bit_length()
     power_count = local_levels + max(device_levels, 1)
     (squares,) = _call(
-        k_powers, (jax.ShapeDtypeStruct((power_count, width, width), jnp.float32),), dynamics)
+        functools.partial(k_powers, False),
+        (jax.ShapeDtypeStruct((local_levels, width, width), jnp.float32),), dynamics)
+    (dev_powers,) = _call(
+        functools.partial(k_powers, True),
+        (jax.ShapeDtypeStruct((max(device_levels, 1), width, width), jnp.float32),),
+        squares[local_levels - 1])
     forward_powers = squares
     pwb = squares
     pwf = squares
@@ -291,28 +298,27 @@
     in_fwd = (starts[None] >= seg_lo) & (starts[None] < seg_lo + seg_steps)
     in_bwd = (ends_incl[None] > seg_lo) & (ends_incl[None] <= seg_lo + seg_steps)
     flat = (devices * scen_count, 1)
-    ff = 1.0 - jnp.any(in_fwd, axis=-1).astype(f32).reshape(flat)
-    fb = 1.0 - jnp.any(in_bwd, axis=-1).astype(f32).reshape(flat)
+    ff = 1.0 - jnp.any(in_fwd, axis=-1).astype(f32).T.reshape(flat)
+    fb = 1.0 - jnp.any(in_bwd, axis=-1).astype(f32).T.reshape(flat)
 
     def gather(copies):
-        every = lax.all_to_all(copies, "tm", 0, 0, tiled=True)
-        return every.reshape(devices * scen_count, copies.shape[2])
+        return lax.all_to_all(copies, "tm", 0, 0, tiled=True)
 
     w1, e1 = _call(functools.partial(k_first, seg), (full, ends), cw, ref, end_col, pwb)
     d2, e2 = _call(
         functools.partial(k_states_in, seg), (full, ends),
-        w1, end_col, start_col, gather(e1), fb, init_image, ff_gain, input_map, pwb, pwf)
+        w1, end_col, start_col, gather(e1), fb, init_image, ff_gain, input_map, pwb, pwf, dev_powers)
     packed = jax.ShapeDtypeStruct((devices, scen_count, width + 128), f32)
     states, w3, e3 = _call(
         functools.partial(k_adjoint_in, seg, 0.5 / total), (full, full, packed),
-        d2, start_col, end_col, gather(e2), ff, cw, ref, pwf, pwb)
+        d2, start_col, end_col, gather(e2), ff, cw, ref, pwf, pwb, dev_powers)
     g3 = gather(e3)
-    cost = jnp.sum(g3[:, width].reshape(devices, scen_count), axis=0)
+    cost = jnp.sum(g3[:, :, width], axis=0)
     s4, e4 = _call(
         functools.partial(k_value_adjoint_in, seg), (full, ends),
-        w3, end_col, start_col, g3, fb, input_map, ff_gain, pwb, pwf)
+        w3, end_col, start_col, g3, fb, input_map, ff_gain, pwb, pwf, dev_powers)
     (grad,) = _call(
-        functools.partial(k_last, seg), (full,), s4, start_col, gather(e4), ff, states, ref, pwf)
+        functools.partial(k_last, seg), (full,), s4, start_col, gather(e4), ff, states, ref, pwf, dev_powers)
     shape3 = (scen_count, seg_steps, width)
     return (states.reshape(shape3), grad.reshape(shape3), cost)
 

time: 98.3 us -> 99.6 us (1.013)
  waiting for transfers between devices: 14.7 us -> 11.6 us
  starting transfers between devices: 14.5 us -> 17 us
    all_to_all x3, waiting for transfers between devices: 14.7 us -> 11.6 us  [gather(): return lax.all_to_all(copies, 'tm', 0, 0, tiled=True)]
    reshape x4 -> x0, local copies, waits for them, and re-layouts: 2.59 us -> none  [gather(): return every.reshape(devices * scen_count, copies.shape[2])]
    all_to_all x3, starting transfers between devices: 14.5 us -> 17 us  [gather(): return lax.all_to_all(copies, 'tm', 0, 0, tiled=True)]
    unnamed x11 -> x17, local copies, waits for them, and re-layouts: 0.78 us -> 2.64 us
    squeeze x0 -> x1, local copies, waits for them, and re-layouts: none -> 1.67 us  [per_device(): squares[local_levels - 1]]
    pallas_call x6 -> x7, Pallas kernels: 43.8 us -> 44.2 us  [_call(): pl.pallas_call(kernel, out_shape=outs, in_specs=_vmem(len(args)), out_spe...]
  transfers between devices with their start and end apart: 3 -> 3, of which waited for: 3 -> 2; matrix products, arithmetic and copies ran while one was open for 6% -> 7% of each run, Pallas kernels for 0% -> 4%
where the time goes in v9:
time: 99.6 us; the launch traced here: 98.9 us
  Pallas kernels  44.2 us (44%)
  starting transfers between devices  17 us (17%)
  waiting for transfers between devices  11.6 us (12%)
  blocking collectives  11.6 us (12%)
  local copies, waits for them, and re-layouts  7.27 us (7%)
  other arithmetic  3.4 us (3%)
  matrix products  3.1 us (3%)
    pallas_call x7, Pallas kernels, _call(): pl.pallas_call(kernel, out_shape=outs, in_specs=_vmem(len(args)), out_spe...  44.2 us
    all_to_all x3, starting transfers between devices, gather(): return lax.all_to_all(copies, 'tm', 0, 0, tiled=True)  17 us
    all_to_all x3, waiting for transfers between devices, gather(): return lax.all_to_all(copies, 'tm', 0, 0, tiled=True)  11.6 us
    all_to_all x1, blocking collectives, gather(): return lax.all_to_all(copies, 'tm', 0, 0, tiled=True)  11.6 us
    unnamed x17, local copies, waits for them, and re-layouts  2.64 us
    dot_general x2, matrix products, build_dynamics(): jnp.einsum('lia,lab,ljb->ij', row_hot, coupling, col_hot, precision=lax.P...  2.18 us
  transfers between devices with their start and end apart: 3, of which 2 were waited for; matrix products, arithmetic and copies ran while one was open for 7% of the time, Pallas kernels for 4%

profile of v9, /device:TPU:0, one launch (start us, length us, event | category | flops | bytes accessed | tf_op | source)
XLA Modules:
  0.0 98.9 jit_solution(1478577894391776390)
XLA Ops:
  0.6 0.0 copy-start
  0.7 0.8 multiply_bitcast_fusion
  1.4 0.9 reduce_window_sum.11
  2.3 0.1 compare_reduce_fusion.1
  2.4 0.8 reshape.164.end_ref
  3.2 0.1 iota_add_fusion
  3.2 0.0 copy-done
  3.2 0.3 convolution_bitcast_fusion.1
  3.6 1.9 %fusion.f_ref = f32[256,256]{1,0:T(8,128)} fusion(f32[3,64,256]{2,1,0:T(8,128)S(1)} %convolution_bitcast_fusion.1, f32[256]{0:T(256)} %param.12, s32[3,64]{1,0:T(4,128)S(1)} %get-tuple-element.27), kind=kOutput, calls=%fused_computation.1 | convolution fusion | flops 151240704 | bytes 460544 | tf_op jit(solution)/shard_map/lia,lab,ljb->ij/dot_general | solution.py:24
  5.4 4.6 %shard_map.112.pwb_ref.pwf_ref = f32[6,256,256]{2,1,0:T(8,128)} custom-call(f32[256,256]{1,0:T(8,128)} %fusion.f_ref), custom_call_target="tpu_custom_call" | custom-call | tf_op jit(solution)/shard_map/pallas_call | solution.py:144
  10.0 0.0 copy-start.6
  10.0 0.0 copy-start.5
  10.0 4.1 %shard_map.113 = (f32[256,256]{1,0:T(8,128)}, f32[16,4,256]{2,1,0:T(4,128)}) custom-call(f32[256,256]{1,0:T(8,128)} %bitcast.29, f32[256,256]{1,0:T(8,128)} %bitcast.26, f32[256,1]{1,0:T(8,128)} %reshape.164.end_ref, f32[6,256,256]{2,1,0:T(8,128)} %shard_map.112.pwb_ref.pwf_ref), custom_call_target="tpu_custom_call" | custom-call | tf_op jit(solution)/shard_map/pallas_call | solution.py:144
  14.2 0.0 copy-start.1
  14.2 0.0 copy-start.7
  14.2 7.5 %all-to-all-start = ((f32[16,4,256]{2,1,0:T(4,128)}), f32[16,4,256]{2,1,0:T(4,128)S(1)}, u32[]{:S(2)}, u32[]{:S(2)}) async-start(f32[16,4,256]{2,1,0:T(4,128)} %get-tuple-element.13), calls=%async_computation | async-start | bytes 131072 | tf_op jit(solution)/shard_map/all_to_all | solution.py:305
  21.7 0.0 copy-done.6
  21.7 1.7 %slice_bitcast_fusion.f_ref = f32[256,256]{1,0:T(8,128)} fusion(f32[6,256,256]{2,1,0:T(8,128)} %shard_map.112.pwb_ref.pwf_ref), kind=kLoop, calls=%fused_computation.4 | loop fusion | bytes 524288 | tf_op jit(solution)/shard_map/squeeze | solution.py:277
  23.4 0.1 compare_reduce_fusion
  23.5 0.1 and_reduce_fusion
  23.6 0.7 sub.24.fb_ref
  24.3 0.8 reshape.165.start_ref
  25.1 0.0 copy-done.5
  25.1 0.7 copy.37.imap_ref
  25.8 4.1 %shard_map.114.pd_ref = f32[4,256,256]{2,1,0:T(8,128)} custom-call(f32[256,256]{1,0:T(8,128)} %slice_bitcast_fusion.f_ref), custom_call_target="tpu_custom_call" | custom-call | tf_op jit(solution)/shard_map/pallas_call | solution.py:144
  29.9 0.0 copy-done.1
  29.9 0.0 copy-done.7
  29.9 0.9 convolution_bitcast_fusion.2.init_ref
  30.8 0.0 all-to-all-done.c1_ref
  30.8 0.0 copy-start.2
  30.8 0.6 copy-done.2
  31.4 8.4 %shard_map.115 = (f32[256,256]{1,0:T(8,128)}, f32[16,4,256]{2,1,0:T(4,128)}) custom-call(f32[256,256]{1,0:T(8,128)} %get-tuple-element.12.w1_ref, f32[256,1]{1,0:T(8,128)} %reshape.164.end_ref, f32[256,1]{1,0:T(8,128)} %reshape.165.start_ref, f32[16,4,256]{2,1,0:T(4,128)} %copy-done.2, f32[64,1]{1,0:T(8,128)} %sub.24.fb_ref, ...), custom_call_target="tpu_custom_call" | custom-call | tf_op jit(solution)/shard_map/pallas_call | solution.py:144
  39.8 6.0 %all-to-all-start.1 = ((f32[16,4,256]{2,1,0:T(4,128)}), f32[16,4,256]{2,1,0:T(4,128)S(1)}, u32[]{:S(2)}, u32[]{:S(2)}) async-start(f32[16,4,256]{2,1,0:T(4,128)} %get-tuple-element.15), calls=%async_computation.1 | async-start | bytes 131072 | tf_op jit(solution)/shard_map/all_to_all | solution.py:305
  45.9 0.7 sub.25.ff_ref
  46.6 6.2 %all-to-all-done.1.c2_ref = f32[16,4,256]{2,1,0:T(4,128)S(1)} async-done(((f32[16,4,256]{2,1,0:T(4,128)}), f32[16,4,256]{2,1,0:T(4,128)S(1)}, u32[]{:S(2)}, u32[]{:S(2)}) %all-to-all-start.1) | async-done | bytes 65568 | tf_op jit(solution)/shard_map/all_to_all | solution.py:305
  52.8 0.0 copy-start.4
  52.8 0.6 copy-done.4
  53.4 8.5 %shard_map.116 = (f32[256,256]{1,0:T(8,128)}, f32[256,256]{1,0:T(8,128)}, f32[16,4,384]{2,1,0:T(4,128)}) custom-call(f32[256,256]{1,0:T(8,128)} %get-tuple-element.14.d2_ref, f32[256,1]{1,0:T(8,128)} %reshape.165.start_ref, f32[256,1]{1,0:T(8,128)} %reshape.164.end_ref, f32[16,4,256]{2,1,0:T(4,128)} %copy-done.4, f32[64,1]{1,0:T(8,128)} %sub.25.ff_ref, ...), custom_call_target="tpu_custom_call" | custom-call | tf_op jit(solution)/shard_map/pallas_call | solution.py:144
  61.9 11.6 %all_to_all.20.c3_ref = f32[16,4,384]{2,1,0:T(4,128)} all-to-all(f32[16,4,384]{2,1,0:T(4,128)} %get-tuple-element.18), channel_id=1, replica_groups=mesh['groups'=2,'tm'=16] {'tm'}, dimensions={0} | all-to-all | bytes 196608 | tf_op jit(solution)/shard_map/all_to_all | solution.py:305
  73.5 8.4 %shard_map.117 = (f32[256,256]{1,0:T(8,128)}, f32[16,4,256]{2,1,0:T(4,128)}) custom-call(f32[256,256]{1,0:T(8,128)} %get-tuple-element.17.w3_ref, f32[256,1]{1,0:T(8,128)} %reshape.164.end_ref, f32[256,1]{1,0:T(8,128)} %reshape.165.start_ref, f32[16,4,384]{2,1,0:T(4,128)} %all_to_all.20.c3_ref, f32[64,1]{1,0:T(8,128)} %sub.24.fb_ref, ...), custom_call_target="tpu_custom_call" | custom-call | tf_op jit(solution)/shard_map/pallas_call | solution.py:144
  81.9 3.5 %all-to-all-start.3 = ((f32[16,4,256]{2,1,0:T(4,128)}), f32[16,4,256]{2,1,0:T(4,128)S(1)}, u32[]{:S(2)}, u32[]{:S(2)}) async-start(f32[16,4,256]{2,1,0:T(4,128)} %get-tuple-element.20), calls=%async_computation.3 | async-start | bytes 131072 | tf_op jit(solution)/shard_map/all_to_all | solution.py:305
  85.4 1.4 %slice_reduce_fusion = f32[4]{0:T(128)} fusion(f32[16,4,384]{2,1,0:T(4,128)} %all_to_all.20.c3_ref), kind=kLoop, calls=%fused_computation.10 | loop fusion | flops 60 | bytes 272 | tf_op jit(solution)/shard_map/reduce_sum | solution.py:316
  86.8 5.5 %all-to-all-done.3.c4_ref = f32[16,4,256]{2,1,0:T(4,128)S(1)} async-done(((f32[16,4,256]{2,1,0:T(4,128)}), f32[16,4,256]{2,1,0:T(4,128)S(1)}, u32[]{:S(2)}, u32[]{:S(2)}) %all-to-all-start.3) | async-done | bytes 65568 | tf_op jit(solution)/shard_map/all_to_all | solution.py:305
  92.3 0.0 copy-start.3
  92.3 0.6 copy-done.3
  92.9 6.0 %shard_map.118 = f32[256,256]{1,0:T(8,128)} custom-call(f32[256,256]{1,0:T(8,128)} %get-tuple-element.19.s4_ref, f32[256,1]{1,0:T(8,128)} %reshape.165.start_ref, f32[16,4,256]{2,1,0:T(4,128)} %copy-done.3, f32[64,1]{1,0:T(8,128)} %sub.25.ff_ref, f32[256,256]{1,0:T(8,128)} %get-tuple-element.16.x_ref, f32[256,256]{1,0:T(8,128)} %bitcast.28, ...), custom_call_target="tpu_custom_call" | custom-call | tf_op jit(solution)/shard_map/pallas_call | solution.py:144
  (7 shorter events, 0.0 us)
Async XLA Ops:
  0.6 2.6 %copy-start = (f32[3,64,64]{2,1,0:T(8,128)S(1)}, f32[3,64,64]{2,1,0:T(8,128)}, u32[]{:S(2)}) copy-start(f32[3,64,64]{2,1,0:T(8,128)} %param.13) | copy-start | bytes 147460
  10.0 11.7 %copy-start.6 = (s32[4,4]{1,0:T(4,128)S(1)}, s32[4,4]{1,0:T(4,128)}, u32[]{:S(2)}) copy-start(s32[4,4]{1,0:T(4,128)} %param.17) | copy-start | bytes 196
  10.0 15.0 %copy-start.5 = (f32[256,64]{0,1:T(8,128)S(1)}, f32[256,64]{0,1:T(8,128)}, u32[]{:S(2)}) copy-start(f32[256,64]{0,1:T(8,128)} %param.15) | copy-start | bytes 196612
  14.2 15.7 %copy-start.1 = (f32[256,256]{1,0:T(8,128)S(1)}, f32[256,256]{1,0:T(8,128)}, u32[]{:S(2)}) copy-start(f32[256,256]{1,0:T(8,128)} %fusion.f_ref) | copy-start | bytes 786436
  14.2 15.7 %copy-start.7 = (f32[4,256]{1,0:T(4,128)S(1)}, f32[4,256]{1,0:T(4,128)}, u32[]{:S(2)}) copy-start(f32[4,256]{1,0:T(4,128)} %param.11) | copy-start | bytes 12292
  14.2 16.6 %all-to-all-start = ((f32[16,4,256]{2,1,0:T(4,128)}), f32[16,4,256]{2,1,0:T(4,128)S(1)}, u32[]{:S(2)}, u32[]{:S(2)}) async-start(f32[16,4,256]{2,1,0:T(4,128)} %get-tuple-element.13), calls=%async_computation | async-start | bytes 131072 | tf_op jit(solution)/shard_map/all_to_all | solution.py:305
  30.8 0.6 copy-start.2
  39.8 12.9 %all-to-all-start.1 = ((f32[16,4,256]{2,1,0:T(4,128)}), f32[16,4,256]{2,1,0:T(4,128)S(1)}, u32[]{:S(2)}, u32[]{:S(2)}) async-start(f32[16,4,256]{2,1,0:T(4,128)} %get-tuple-element.15), calls=%async_computation.1 | async-start | bytes 131072 | tf_op jit(solution)/shard_map/all_to_all | solution.py:305
  52.8 0.6 copy-start.4
  81.9 10.4 %all-to-all-start.3 = ((f32[16,4,256]{2,1,0:T(4,128)}), f32[16,4,256]{2,1,0:T(4,128)S(1)}, u32[]{:S(2)}, u32[]{:S(2)}) async-start(f32[16,4,256]{2,1,0:T(4,128)} %get-tuple-element.20), calls=%async_computation.3 | async-start | bytes 131072 | tf_op jit(solution)/shard_map/all_to_all | solution.py:305
  92.3 0.6 copy-start.3

commit v10 on v8

v10 whole, which is shorter than its diff:
```python
import functools

import jax
import jax.numpy as jnp
from jax import lax
from jax.experimental import pallas as pl
from jax.experimental.pallas import tpu as pltpu
from jax.sharding import PartitionSpec as P

HIGH = lax.Precision.HIGHEST


def build_dynamics(decay, coupling, links):
    size = decay.shape[0]
    width = coupling.shape[1]
    lanes = jnp.arange(size, dtype=jnp.int32)
    offsets = jnp.arange(width, dtype=jnp.int32)
    row_hot = (lanes[None, :, None] == links[:, 0:1, None] * width + offsets[None, None, :]).astype(
        jnp.float32
    )
    col_hot = (lanes[None, :, None] == links[:, 1:2, None] * width + offsets[None, None, :]).astype(
        jnp.float32
    )
    placed = jnp.einsum(
        "lia,lab,ljb->ij", row_hot, coupling, col_hot, precision=lax.Precision.HIGHEST
    )
    return jnp.diag(decay) + placed


def row_times(values, matrix):
    width = values.shape[-1]
    flat = jnp.dot(values.reshape(-1, width), matrix, precision=lax.Precision.HIGHEST)
    return flat.reshape(values.shape)


def _dot(a, b):
    return jnp.dot(a, b, precision=HIGH, preferred_element_type=jnp.float32)


def _dot_nt(a, b):
    return lax.dot_general(
        a, b, (((1,), (1,)), ((), ())), precision=HIGH, preferred_element_type=jnp.float32)


def _split(x):
    hi = x.astype(jnp.bfloat16)
    lo = (x - hi.astype(jnp.float32)).astype(jnp.bfloat16)
    return hi, lo


def _mm(a, b, nt=False):
    dims = (((1,), (1 if nt else 0,)), ((), ()))
    a_hi, a_lo = _split(a)
    b_hi, b_lo = _split(b)
    part = functools.partial(lax.dot_general, dimension_numbers=dims,
                             preferred_element_type=jnp.float32)
    return part(a_lo, b_hi) + part(a_hi, b_lo) + part(a_hi, b_hi)


def k_powers(decay_ref, coupling_ref, links_ref, out_ref):
    size = decay_ref.shape[1]
    width = coupling_ref.shape[1]
    r = lax.broadcasted_iota(jnp.int32, (size, size), 0)
    c = lax.broadcasted_iota(jnp.int32, (size, size), 1)
    power = jnp.where(r == c, jnp.broadcast_to(decay_ref[...], (size, size)), 0.0)
    lane = lax.broadcasted_iota(jnp.int32, (size, width), 0)
    off = lax.broadcasted_iota(jnp.int32, (size, width), 1)
    for link in range(coupling_ref.shape[0]):
        row_hot = (lane == links_ref[link, 0] * width + off).astype(jnp.float32)
        col_hot = (lane == links_ref[link, 1] * width + off).astype(jnp.float32)
        power = power + _dot_nt(_dot(row_hot, coupling_ref[link]), col_hot)
    out_ref[0] = power
    for level in range(1, out_ref.shape[0]):
        power = _dot(power, power)
        out_ref[level] = power


def _scan(v, cut, pw_ref, seg, backward, carry=None, levels=None):
    rows, width = v.shape
    scen = rows // seg
    t = lax.broadcasted_iota(jnp.int32, (rows, width), 0) % seg
    flags = 1.0 - cut
    if levels is None:
        levels = seg.bit_length() - 1
    step = functools.partial(_mm, nt=not backward)
    if carry is not None:
        pushed = step(carry, pw_ref[0])
        pushed = jnp.broadcast_to(pushed[:, None, :], (scen, seg, width)).reshape(rows, width)
        first = t == (seg - 1 if backward else 0)
        v = v + jnp.where(first, flags * pushed, 0.0)
    for level in range(levels):
        stride = 2**level
        if backward:
            prior_v = pltpu.roll(v, rows - stride, 0)
            prior_f = pltpu.roll(flags, rows - stride, 0)
            valid = t < seg - stride
        else:
            prior_v = pltpu.roll(v, stride, 0)
            prior_f = pltpu.roll(flags, stride, 0)
            valid = t >= stride
        prior_v = jnp.where(valid, prior_v, 0.0)
        prior_f = jnp.where(valid, prior_f, 1.0)
        v = v + flags * step(prior_v, pw_ref[level])
        flags = flags * prior_f
    return v


def _carry(g_ref, len_ref, pw_ref, scen, backward, seg):
    width = pw_ref.shape[1]
    g = g_ref[...][:, :width]
    rows = g.shape[0]
    devices = rows // scen
    local_levels = pw_ref.shape[0] - max((devices - 1).bit_length(), 1)
    r = lax.broadcasted_iota(jnp.int32, (rows, width), 0)
    flags = jnp.broadcast_to(_seg_flags(len_ref, devices, seg, not backward), (rows, width))
    step = functools.partial(_mm, nt=not backward)
    for level in range((devices - 1).bit_length()):
        stride = scen * 2**level
        if backward:
            prior_g = pltpu.roll(g, rows - stride, 0)
            prior_f = pltpu.roll(flags, rows - stride, 0)
            valid = r < rows - stride
        else:
            prior_g = pltpu.roll(g, stride, 0)
            prior_f = pltpu.roll(flags, stride, 0)
            valid = r >= stride
        prior_g = jnp.where(valid, prior_g, 0.0)
        prior_f = jnp.where(valid, prior_f, 1.0)
        g = g + flags * step(prior_g, pw_ref[local_levels + level])
        flags = flags * prior_f
    me = lax.axis_index("tm")
    target = me + 1 if backward else me - 1
    pick = lax.broadcasted_iota(jnp.int32, (scen, rows), 1)
    want = lax.broadcasted_iota(jnp.int32, (scen, rows), 0) + target * scen
    return _dot((pick == want).astype(jnp.float32), g)


def _ends(v, seg, backward, out_rows):
    rows, width = v.shape
    scen = rows // seg
    pick = lax.broadcasted_iota(jnp.int32, (scen, rows), 1)
    want = lax.broadcasted_iota(jnp.int32, (scen, rows), 0) * seg + (0 if backward else seg - 1)
    ends = _dot((pick == want).astype(jnp.float32), v)
    return jnp.broadcast_to(ends[None], (out_rows,) + ends.shape)


def _cut_rows(len_ref, shape, seg, start):
    rows, width = shape
    scen, episodes = len_ref.shape
    r = lax.broadcasted_iota(jnp.int32, (rows, 1), 0)
    which = r // seg
    pos = lax.axis_index("tm") * seg + r % seg
    hit = jnp.zeros((rows, 1), jnp.bool_)
    for s in range(scen):
        edge = 0
        for k in range(episodes):
            first = edge
            edge = edge + len_ref[s, k]
            hit = hit | ((which == s) & (pos == first if start else pos + 1 == edge))
    return jnp.broadcast_to(hit.astype(jnp.float32), shape)


def _seg_flags(len_ref, devices, seg, start):
    scen, episodes = len_ref.shape
    rows = devices * scen
    r = lax.broadcasted_iota(jnp.int32, (rows, 1), 0)
    which = r % scen
    lo = r // scen * seg
    hit = jnp.zeros((rows, 1), jnp.bool_)
    for s in range(scen):
        edge = 0
        for k in range(episodes):
            first = edge
            edge = edge + len_ref[s, k]
            if start:
                inside = (first >= lo) & (first < lo + seg)
            else:
                inside = (edge > lo) & (edge <= lo + seg)
            hit = hit | ((which == s) & inside)
    return 1.0 - hit.astype(jnp.float32)


def _vmem(count):
    return [pl.BlockSpec(memory_space=pltpu.VMEM)] * count


def _call(kernel, outs, *args, smem=()):
    specs = _vmem(len(args))
    for index in smem:
        specs[index] = pl.BlockSpec(memory_space=pltpu.SMEM)
    return pl.pallas_call(
        kernel,
        out_shape=outs,
        in_specs=specs,
        out_specs=tuple(_vmem(len(outs))),
    )(*args)


def k_first(seg, cw_ref, ref_ref, len_ref, pwb_ref, w1_ref, e1_ref):
    cut = _cut_rows(len_ref, cw_ref.shape, seg, False)
    w1 = cw_ref[...] * ref_ref[...]
    w1_ref[...] = w1
    e1_ref[...] = _ends(_scan(w1, cut, pwb_ref, seg, True), seg, True, e1_ref.shape[0])


def k_states_in(seg, w1_ref, len_ref, c1_ref, xi_ref, gain_ref, imap_ref, pwb_ref,
                pwf_ref, d2_ref, e2_ref):
    shape = w1_ref.shape
    cut_e = _cut_rows(len_ref, shape, seg, False)
    cut_s = _cut_rows(len_ref, shape, seg, True)
    c1 = _carry(c1_ref, len_ref, pwb_ref, w1_ref.shape[0] // seg, True, seg)
    vt = _scan(w1_ref[...], cut_e, pwb_ref, seg, True, c1)
    controls = _mm(vt, gain_ref[...], nt=True)
    forcing = -_mm(controls, imap_ref[...], nt=True)
    rows, width = shape
    scen = rows // seg
    image = _dot_nt(xi_ref[...], pwf_ref[0])
    init = jnp.broadcast_to(image[:, None, :], (scen, seg, width)).reshape(rows, width)
    d2 = forcing + cut_s * init
    d2_ref[...] = d2
    e2_ref[...] = _ends(_scan(d2, cut_s, pwf_ref, seg, False), seg, False, e2_ref.shape[0])


def k_adjoint_in(seg, scale, d2_ref, len_ref, c2_ref, cw_ref, ref_ref, pwf_ref, pwb_ref,
                 x_ref, w3_ref, e3_ref):
    shape = d2_ref.shape
    rows, width = shape
    scen = rows // seg
    cut_s = _cut_rows(len_ref, shape, seg, True)
    cut_e = _cut_rows(len_ref, shape, seg, False)
    c2 = _carry(c2_ref, len_ref, pwf_ref, scen, False, seg)
    states = _scan(d2_ref[...], cut_s, pwf_ref, seg, False, c2)
    x_ref[...] = states
    offset = states - ref_ref[...]
    cw = cw_ref[...]
    w3 = cw * offset
    w3_ref[...] = w3
    per_row = jnp.sum(w3 * offset, axis=1, keepdims=True)
    copies = e3_ref.shape[0]
    pick = lax.broadcasted_iota(jnp.int32, (scen, rows), 1) // seg
    want = lax.broadcasted_iota(jnp.int32, (scen, rows), 0)
    sel = (pick == want).astype(jnp.float32)
    per_scen = _dot(sel, jnp.broadcast_to(per_row, (rows, 128))) * scale
    e3_ref[:, :, width:] = jnp.broadcast_to(per_scen[None], (copies, scen, 128))
    e3_ref[:, :, :width] = _ends(_scan(w3, cut_e, pwb_ref, seg, True), seg, True, copies)


def k_value_adjoint_in(seg, w3_ref, len_ref, c3_ref, imap_ref, gain_ref, pwb_ref,
                       pwf_ref, s4_ref, e4_ref):
    shape = w3_ref.shape
    cut_e = _cut_rows(len_ref, shape, seg, False)
    cut_s = _cut_rows(len_ref, shape, seg, True)
    c3 = _carry(c3_ref, len_ref, pwb_ref, w3_ref.shape[0] // seg, True, seg)
    adjoint = _scan(w3_ref[...], cut_e, pwb_ref, seg, True, c3)
    pulled = _mm(adjoint, imap_ref[...])
    source = -_mm(pulled, gain_ref[...])
    s4_ref[...] = source
    e4_ref[...] = _ends(_scan(source, cut_s, pwf_ref, seg, False), seg, False, e4_ref.shape[0])


def k_last(seg, s4_ref, len_ref, c4_ref, x_ref, ref_ref, pwf_ref, g_ref):
    shape = s4_ref.shape
    cut_s = _cut_rows(len_ref, shape, seg, True)
    c4 = _carry(c4_ref, len_ref, pwf_ref, s4_ref.shape[0] // seg, False, seg)
    va = _scan(s4_ref[...], cut_s, pwf_ref, seg, False, c4)
    ref = ref_ref[...]
    offset = x_ref[...] - ref
    g_ref[...] = 0.5 * offset * offset + ref * va


def per_device(ref_traj, cost_weights, x_init, decay, coupling, links, input_map, ff_gain, lengths):
    scen_count, seg_steps, width = ref_traj.shape
    rows = scen_count * seg_steps
    devices = lax.axis_size("tm")
    device = lax.axis_index("tm")
    total = seg_steps * devices
    local_levels = seg_steps.bit_length() - 1
    device_levels = (devices - 1).bit_length()
    power_count = local_levels + max(device_levels, 1)
    (squares,) = _call(
        k_powers, (jax.ShapeDtypeStruct((power_count, width, width), jnp.float32),),
        decay.reshape(1, width), coupling, links, smem=(2,))
    forward_powers = squares
    pwb = squares
    pwf = squares
    cw = cost_weights.reshape(rows, width)
    ref = ref_traj.reshape(rows, width)
    f32 = jnp.float32
    full = jax.ShapeDtypeStruct((rows, width), f32)
    ends = jax.ShapeDtypeStruct((devices, scen_count, width), f32)
    seg = seg_steps

    def gather(copies):
        every = lax.all_to_all(copies, "tm", 0, 0, tiled=True)
        return every.reshape(devices * scen_count, copies.shape[2])

    w1, e1 = _call(functools.partial(k_first, seg), (full, ends), cw, ref, lengths, pwb, smem=(2,))
    d2, e2 = _call(
        functools.partial(k_states_in, seg), (full, ends),
        w1, lengths, gather(e1), x_init, ff_gain, input_map, pwb, pwf, smem=(1,))
    packed = jax.ShapeDtypeStruct((devices, scen_count, width + 128), f32)
    states, w3, e3 = _call(
        functools.partial(k_adjoint_in, seg, 0.5 / total), (full, full, packed),
        d2, lengths, gather(e2), cw, ref, pwf, pwb, smem=(1,))
    g3 = gather(e3)
    cost = jnp.sum(g3[:, width].reshape(devices, scen_count), axis=0)
    s4, e4 = _call(
        functools.partial(k_value_adjoint_in, seg), (full, ends),
        w3, lengths, g3, input_map, ff_gain, pwb, pwf, smem=(1,))
    (grad,) = _call(
        functools.partial(k_last, seg), (full,), s4, lengths, gather(e4), states, ref, pwf,
        smem=(1,))
    shape3 = (scen_count, seg_steps, width)
    return (states.reshape(shape3), grad.reshape(shape3), cost)


def solution(mesh):
    placed = (
        P("groups", "tm", None),
        P("groups", "tm", None),
        P("groups", None),
        P(),
        P(),
        P(),
        P(),
        P(),
        P("groups", None),
    )
    return jax.shard_map(
        per_device,
        mesh=mesh,
        in_specs=placed,
        out_specs=(P("groups", "tm", None), P("groups", "tm", None), P("groups")),
        check_vma=False,
    )
```

time: 98.3 us -> 96.3 us (0.980)
  blocking collectives: 10.9 us -> 21.2 us
  starting transfers between devices: 14.5 us -> 10.9 us
  waiting for transfers between devices: 14.7 us -> 11.5 us
  matrix products: 3.1 us -> 0 us
  other arithmetic: 2.56 us -> 0.56 us
  local copies, waits for them, and re-layouts: 7.41 us -> 5.64 us
  Pallas kernels: 43.8 us -> 45.3 us
    all_to_all x1 -> x2, blocking collectives: 10.9 us -> 21.2 us  [gather(): every = lax.all_to_all(copies, 'tm', 0, 0, tiled=True)]
    all_to_all x3 -> x2, starting transfers between devices: 14.5 us -> 10.9 us  [gather(): every = lax.all_to_all(copies, 'tm', 0, 0, tiled=True)]
    all_to_all x3 -> x2, waiting for transfers between devices: 14.7 us -> 11.5 us  [gather(): every = lax.all_to_all(copies, 'tm', 0, 0, tiled=True)]
    dot_general x3 -> x0, matrix products: 3.1 us -> none  [the longest x2 2.18 us: build_dynamics(): jnp.einsum('lia,lab,ljb->ij', row_hot, coupling, col_hot, precision=lax.P...]
    convert_element_type x2 -> x0, local copies, waits for them, and re-layouts: 1.58 us -> none  [the longest x1 0.79 us: per_device(): end_col = end_flag.astype(jnp.float32).reshape(rows, 1)]
    pallas_call x6, Pallas kernels: 43.8 us -> 45.3 us  [_call(): pl.pallas_call(kernel, out_shape=outs, in_specs=specs, out_specs=tuple(_v...]
    sub x4 -> x0, local copies, waits for them, and re-layouts: 1.52 us -> none  [the longest x2 0.76 us: per_device(): ff = 1.0 - jnp.any(in_fwd, axis=-1).astype(f32).reshape(flat)]
    unnamed x11 -> x4, local copies, waits for them, and re-layouts: 0.78 us -> 2.09 us
  transfers between devices with their start and end apart: 3 -> 2, of which waited for: 3 -> 2; matrix products, arithmetic and copies ran while one was open for 6% -> 2% of each run, Pallas kernels for 0% -> 0%
where the time goes in v10:
time: 96.3 us; the launch traced here: 95.7 us
  Pallas kernels  45.3 us (47%)
  blocking collectives  21.2 us (22%)
  waiting for transfers between devices  11.5 us (12%)
  starting transfers between devices  10.9 us (11%)
  local copies, waits for them, and re-layouts  5.64 us (6%)
    pallas_call x6, Pallas kernels, _call(): pl.pallas_call(kernel, out_shape=outs, in_specs=specs, out_specs=tuple(_v...  45.3 us
    all_to_all x2, blocking collectives, gather(): every = lax.all_to_all(copies, 'tm', 0, 0, tiled=True)  21.2 us
    all_to_all x2, waiting for transfers between devices, gather(): every = lax.all_to_all(copies, 'tm', 0, 0, tiled=True)  11.5 us
    all_to_all x2, starting transfers between devices, gather(): every = lax.all_to_all(copies, 'tm', 0, 0, tiled=True)  10.9 us
    reshape x4, local copies, waits for them, and re-layouts, gather(): return every.reshape(devices * scen_count, copies.shape[2])  2.6 us
    unnamed x4, local copies, waits for them, and re-layouts  2.09 us
  transfers between devices with their start and end apart: 2, of which 2 were waited for; matrix products, arithmetic and copies ran while one was open for 2% of the time, Pallas kernels for 0%

profile of v10, /device:TPU:0, one launch (start us, length us, event | category | flops | bytes accessed | tf_op | source)
XLA Modules:
  0.0 95.7 jit_solution(9034867473727408539)
XLA Ops:
  0.6 1.3 %copy.15.links_ref = s32[3,2]{1,0:T(4,128)} copy(s32[3,2]{0,1:T(2,128)} %param.14) | data formatting | bytes 48 | tf_op args[5]
  2.0 0.0 copy-start
  2.0 8.7 %shard_map.112.pwb_ref.pwf_ref = f32[10,256,256]{2,1,0:T(8,128)} custom-call(f32[1,256]{1,0:T(1,128)} %bitcast.12, f32[3,64,64]{2,1,0:T(8,128)} %coupling_ref.1, s32[3,2]{1,0:T(4,128)} %copy.15.links_ref), custom_call_target="tpu_custom_call" | custom-call | tf_op jit(solution)/shard_map/pallas_call | solution.py:191
  10.7 4.4 %shard_map.113 = (f32[256,256]{1,0:T(8,128)}, f32[16,4,256]{2,1,0:T(4,128)}) custom-call(f32[256,256]{1,0:T(8,128)} %bitcast.8, f32[256,256]{1,0:T(8,128)} %bitcast.5, s32[4,4]{1,0:T(4,128)} %len_ref.9, f32[10,256,256]{2,1,0:T(8,128)} %shard_map.112.pwb_ref.pwf_ref), custom_call_target="tpu_custom_call" | custom-call | tf_op jit(solution)/shard_map/pallas_call | solution.py:191
  15.2 7.4 %all-to-all-start = ((f32[16,4,256]{2,1,0:T(4,128)}), f32[16,4,256]{2,1,0:T(4,128)S(1)}, u32[]{:S(2)}, u32[]{:S(2)}) async-start(f32[16,4,256]{2,1,0:T(4,128)} %get-tuple-element.13), calls=%async_computation | async-start | bytes 131072 | tf_op jit(solution)/shard_map/all_to_all | solution.py:294
  22.5 0.0 copy-done
  22.5 0.8 copy.16.imap_ref
  23.3 6.1 %all-to-all-done = f32[16,4,256]{2,1,0:T(4,128)S(1)} async-done(((f32[16,4,256]{2,1,0:T(4,128)}), f32[16,4,256]{2,1,0:T(4,128)S(1)}, u32[]{:S(2)}, u32[]{:S(2)}) %all-to-all-start) | async-done | bytes 65568 | tf_op jit(solution)/shard_map/all_to_all | solution.py:294
  29.4 0.7 reshape.36.c1_ref
  30.1 8.9 %shard_map.114 = (f32[256,256]{1,0:T(8,128)}, f32[16,4,256]{2,1,0:T(4,128)}) custom-call(f32[256,256]{1,0:T(8,128)} %get-tuple-element.12.w1_ref, s32[4,4]{1,0:T(4,128)} %len_ref.9, f32[64,256]{1,0:T(8,128)} %reshape.36.c1_ref, f32[4,256]{1,0:T(4,128)} %xi_ref.1, f32[64,256]{1,0:T(8,128)} %gain_ref.3, f32[256,64]{1,0:T(8,128)} %copy.16.imap_ref, ...), custom_call_target="tpu_custom_call" | custom-call | tf_op jit(solution)/shard_map/pallas_call | solution.py:191
  38.9 10.3 %all_to_all.20 = f32[16,4,256]{2,1,0:T(4,128)S(1)} all-to-all(f32[16,4,256]{2,1,0:T(4,128)} %get-tuple-element.15), channel_id=1, replica_groups=mesh['groups'=2,'tm'=16] {'tm'}, dimensions={0} | all-to-all | bytes 131072 | tf_op jit(solution)/shard_map/all_to_all | solution.py:294
  49.3 0.6 reshape.37.c2_ref
  49.9 8.7 %shard_map.115 = (f32[256,256]{1,0:T(8,128)}, f32[256,256]{1,0:T(8,128)}, f32[16,4,384]{2,1,0:T(4,128)}) custom-call(f32[256,256]{1,0:T(8,128)} %get-tuple-element.14.d2_ref, s32[4,4]{1,0:T(4,128)} %len_ref.9, f32[64,256]{1,0:T(8,128)} %reshape.37.c2_ref, f32[256,256]{1,0:T(8,128)} %bitcast.9, f32[256,256]{1,0:T(8,128)} %bitcast.6, ...), custom_call_target="tpu_custom_call" | custom-call | tf_op jit(solution)/shard_map/pallas_call | solution.py:191
  58.6 10.9 %all_to_all.21 = f32[16,4,384]{2,1,0:T(4,128)S(1)} all-to-all(f32[16,4,384]{2,1,0:T(4,128)} %get-tuple-element.18), channel_id=1, replica_groups=mesh['groups'=2,'tm'=16] {'tm'}, dimensions={0} | all-to-all | bytes 196608 | tf_op jit(solution)/shard_map/all_to_all | solution.py:294
  69.4 0.7 reshape.39.c3_ref
  70.1 8.8 %shard_map.116 = (f32[256,256]{1,0:T(8,128)}, f32[16,4,256]{2,1,0:T(4,128)}) custom-call(f32[256,256]{1,0:T(8,128)} %get-tuple-element.17.w3_ref, s32[4,4]{1,0:T(4,128)} %len_ref.9, f32[64,384]{1,0:T(8,128)} %reshape.39.c3_ref, f32[256,64]{1,0:T(8,128)} %copy.16.imap_ref, f32[64,256]{1,0:T(8,128)} %gain_ref.3, f32[10,256,256]{2,1,0:T(8,128)} %shard_map.112.pwb_ref.pwf_ref, ...), custom_call_target="tpu_custom_call" | custom-call | tf_op jit(solution)/shard_map/pallas_call | solution.py:191
  78.9 3.5 %all-to-all-start.3 = ((f32[16,4,256]{2,1,0:T(4,128)}), f32[16,4,256]{2,1,0:T(4,128)S(1)}, u32[]{:S(2)}, u32[]{:S(2)}) async-start(f32[16,4,256]{2,1,0:T(4,128)} %get-tuple-element.20), calls=%async_computation.3 | async-start | bytes 131072 | tf_op jit(solution)/shard_map/all_to_all | solution.py:294
  82.4 0.9 slice_reduce_fusion
  83.2 0.1 reshape_squeeze.3
  83.3 0.6 reduce_sum.9
  83.9 5.4 %all-to-all-done.3 = f32[16,4,256]{2,1,0:T(4,128)S(1)} async-done(((f32[16,4,256]{2,1,0:T(4,128)}), f32[16,4,256]{2,1,0:T(4,128)S(1)}, u32[]{:S(2)}, u32[]{:S(2)}) %all-to-all-start.3) | async-done | bytes 65568 | tf_op jit(solution)/shard_map/all_to_all | solution.py:294
  89.2 0.6 reshape.40.c4_ref
  89.9 5.8 %shard_map.117 = f32[256,256]{1,0:T(8,128)} custom-call(f32[256,256]{1,0:T(8,128)} %get-tuple-element.19.s4_ref, s32[4,4]{1,0:T(4,128)} %len_ref.9, f32[64,256]{1,0:T(8,128)} %reshape.40.c4_ref, f32[256,256]{1,0:T(8,128)} %get-tuple-element.16.x_ref, f32[256,256]{1,0:T(8,128)} %bitcast.7, f32[10,256,256]{2,1,0:T(8,128)} %shard_map.112.pwb_ref.pwf_ref), custom_call_target="tpu_custom_call" | custom-call | tf_op jit(solution)/shard_map/pallas_call | solution.py:191
Async XLA Ops:
  2.0 20.6 %copy-start = (f32[256,64]{0,1:T(8,128)S(1)}, f32[256,64]{0,1:T(8,128)}, u32[]{:S(2)}) copy-start(f32[256,64]{0,1:T(8,128)} %param.15) | copy-start | bytes 196612
  15.2 14.3 %all-to-all-start = ((f32[16,4,256]{2,1,0:T(4,128)}), f32[16,4,256]{2,1,0:T(4,128)S(1)}, u32[]{:S(2)}, u32[]{:S(2)}) async-start(f32[16,4,256]{2,1,0:T(4,128)} %get-tuple-element.13), calls=%async_computation | async-start | bytes 131072 | tf_op jit(solution)/shard_map/all_to_all | solution.py:294
  78.9 10.4 %all-to-all-start.3 = ((f32[16,4,256]{2,1,0:T(4,128)}), f32[16,4,256]{2,1,0:T(4,128)S(1)}, u32[]{:S(2)}, u32[]{:S(2)}) async-start(f32[16,4,256]{2,1,0:T(4,128)} %get-tuple-element.20), calls=%async_computation.3 | async-start | bytes 131072 | tf_op jit(solution)/shard_map/all_to_all | solution.py:294

commit v11 on v10

--- a/solution.py
+++ b/solution.py
@@ -57,7 +57,7 @@
     return part(a_lo, b_hi) + part(a_hi, b_lo) + part(a_hi, b_hi)
 
 
-def k_powers(decay_ref, coupling_ref, links_ref, out_ref):
+def _build(decay_ref, coupling_ref, links_ref):
     size = decay_ref.shape[1]
     width = coupling_ref.shape[1]
     r = lax.broadcasted_iota(jnp.int32, (size, size), 0)
@@ -66,13 +66,10 @@
     lane = lax.broadcasted_iota(jnp.int32, (size, width), 0)
     off = lax.broadcasted_iota(jnp.int32, (size, width), 1)
     for link in range(coupling_ref.shape[0]):
-        row_hot = (lane == links_ref[link, 0] * width + off).astype(jnp.float32)
-        col_hot = (lane == links_ref[link, 1] * width + off).astype(jnp.float32)
+        row_hot = (lane == links_ref[0, link] * width + off).astype(jnp.float32)
+        col_hot = (lane == links_ref[1, link] * width + off).astype(jnp.float32)
         power = power + _dot_nt(_dot(row_hot, coupling_ref[link]), col_hot)
-    out_ref[0] = power
-    for level in range(1, out_ref.shape[0]):
-        power = _dot(power, power)
-        out_ref[level] = power
+    return power
 
 
 def _scan(v, cut, pw_ref, seg, backward, carry=None, levels=None):
@@ -196,11 +193,19 @@
     )(*args)
 
 
-def k_first(seg, cw_ref, ref_ref, len_ref, pwb_ref, w1_ref, e1_ref):
-    cut = _cut_rows(len_ref, cw_ref.shape, seg, False)
-    w1 = cw_ref[...] * ref_ref[...]
-    w1_ref[...] = w1
-    e1_ref[...] = _ends(_scan(w1, cut, pwb_ref, seg, True), seg, True, e1_ref.shape[0])
+def k_first(seg, decay_ref, coupling_ref, links_ref, cw_ref, ref_ref, len_ref, pwb_ref, w1_ref,
+            e1_ref):
+    local_levels = seg.bit_length() - 1
+    power = _build(decay_ref, coupling_ref, links_ref)
+    pwb_ref[0] = power
+    for level in range(1, pwb_ref.shape[0]):
+        if level == local_levels:
+            cut = _cut_rows(len_ref, cw_ref.shape, seg, False)
+            w1 = cw_ref[...] * ref_ref[...]
+            w1_ref[...] = w1
+            e1_ref[...] = _ends(_scan(w1, cut, pwb_ref, seg, True), seg, True, e1_ref.shape[0])
+        power = _dot(power, power)
+        pwb_ref[level] = power
 
 
 def k_states_in(seg, w1_ref, len_ref, c1_ref, xi_ref, gain_ref, imap_ref, pwb_ref,
@@ -277,12 +282,6 @@
     local_levels = seg_steps.bit_length() - 1
     device_levels = (devices - 1).bit_length()
     power_count = local_levels + max(device_levels, 1)
-    (squares,) = _call(
-        k_powers, (jax.ShapeDtypeStruct((power_count, width, width), jnp.float32),),
-        decay.reshape(1, width), coupling, links, smem=(2,))
-    forward_powers = squares
-    pwb = squares
-    pwf = squares
     cw = cost_weights.reshape(rows, width)
     ref = ref_traj.reshape(rows, width)
     f32 = jnp.float32
@@ -294,7 +293,11 @@
         every = lax.all_to_all(copies, "tm", 0, 0, tiled=True)
         return every.reshape(devices * scen_count, copies.shape[2])
 
-    w1, e1 = _call(functools.partial(k_first, seg), (full, ends), cw, ref, lengths, pwb, smem=(2,))
+    powers = jax.ShapeDtypeStruct((power_count, width, width), f32)
+    pwb, w1, e1 = _call(
+        functools.partial(k_first, seg), (powers, full, ends),
+        decay.reshape(1, width), coupling, links.T, cw, ref, lengths, smem=(2, 5))
+    pwf = pwb
     d2, e2 = _call(
         functools.partial(k_states_in, seg), (full, ends),
         w1, lengths, gather(e1), x_init, ff_gain, input_map, pwb, pwf, smem=(1,))

time: 96.3 us -> 91.8 us (0.953)
  Pallas kernels: 45.3 us -> 42.2 us
    pallas_call x6 -> x5, Pallas kernels: 45.3 us -> 42.2 us  [_call(): pl.pallas_call(kernel, out_shape=outs, in_specs=specs, out_specs=tuple(_v...]
    unnamed x4 -> x1, local copies, waits for them, and re-layouts: 2.09 us -> 1.59 us
  transfers between devices with their start and end apart: 2 -> 2, of which waited for: 2 -> 2; matrix products, arithmetic and copies ran while one was open for 2% -> 3% of each run, Pallas kernels for 0% -> 0%
where the time goes in v11:
time: 91.8 us; the launch traced here: 91.3 us
  Pallas kernels  42.2 us (46%)
  blocking collectives  21.2 us (23%)
  starting transfers between devices  10.8 us (12%)
  waiting for transfers between devices  10.7 us (12%)
  local copies, waits for them, and re-layouts  5.16 us (6%)
    pallas_call x5, Pallas kernels, _call(): pl.pallas_call(kernel, out_shape=outs, in_specs=specs, out_specs=tuple(_v...  42.2 us
    all_to_all x2, blocking collectives, gather(): every = lax.all_to_all(copies, 'tm', 0, 0, tiled=True)  21.2 us
    all_to_all x2, starting transfers between devices, gather(): every = lax.all_to_all(copies, 'tm', 0, 0, tiled=True)  10.8 us
    all_to_all x2, waiting for transfers between devices, gather(): every = lax.all_to_all(copies, 'tm', 0, 0, tiled=True)  10.7 us
    reshape x4, local copies, waits for them, and re-layouts, gather(): return every.reshape(devices * scen_count, copies.shape[2])  2.63 us
  transfers between devices with their start and end apart: 2, of which 2 were waited for; matrix products, arithmetic and copies ran while one was open for 3% of the time, Pallas kernels for 0%

profile of v11, /device:TPU:0, one launch (start us, length us, event | category | flops | bytes accessed | tf_op | source)
XLA Modules:
  0.0 91.3 jit_solution(4279104724748654943)
XLA Ops:
  0.6 10.1 %shard_map.112 = (f32[10,256,256]{2,1,0:T(8,128)}, f32[256,256]{1,0:T(8,128)}, f32[16,4,256]{2,1,0:T(4,128)}) custom-call(f32[1,256]{1,0:T(1,128)} %bitcast.13, f32[3,64,64]{2,1,0:T(8,128)} %coupling_ref.1, s32[2,3]{1,0:T(2,128)} %bitcast.14, f32[256,256]{1,0:T(8,128)} %bitcast.9, f32[256,256]{1,0:T(8,128)} %bitcast.6, s32[4,4]{1,0:T(4,128)} %len_ref.9), custom_call_target="tpu_custom_call" | custom-call | tf_op jit(solution)/shard_map/pallas_call | solution.py:188
  10.7 7.4 %all-to-all-start = ((f32[16,4,256]{2,1,0:T(4,128)}), f32[16,4,256]{2,1,0:T(4,128)S(1)}, u32[]{:S(2)}, u32[]{:S(2)}) async-start(f32[16,4,256]{2,1,0:T(4,128)} %get-tuple-element.14), calls=%async_computation | async-start | bytes 131072 | tf_op jit(solution)/shard_map/all_to_all | solution.py:293
  18.1 1.6 %copy.14.imap_ref = f32[256,64]{1,0:T(8,128)} copy(f32[256,64]{0,1:T(8,128)} %param.15) | data formatting | bytes 131072 | tf_op args[6]
  19.6 5.3 %all-to-all-done = f32[16,4,256]{2,1,0:T(4,128)S(1)} async-done(((f32[16,4,256]{2,1,0:T(4,128)}), f32[16,4,256]{2,1,0:T(4,128)S(1)}, u32[]{:S(2)}, u32[]{:S(2)}) %all-to-all-start) | async-done | bytes 65568 | tf_op jit(solution)/shard_map/all_to_all | solution.py:293
  25.0 0.7 reshape.36.c1_ref
  25.6 8.9 %shard_map.113 = (f32[256,256]{1,0:T(8,128)}, f32[16,4,256]{2,1,0:T(4,128)}) custom-call(f32[256,256]{1,0:T(8,128)} %get-tuple-element.13.w1_ref, s32[4,4]{1,0:T(4,128)} %len_ref.9, f32[64,256]{1,0:T(8,128)} %reshape.36.c1_ref, f32[4,256]{1,0:T(4,128)} %xi_ref.1, f32[64,256]{1,0:T(8,128)} %gain_ref.3, f32[256,64]{1,0:T(8,128)} %copy.14.imap_ref, ...), custom_call_target="tpu_custom_call" | custom-call | tf_op jit(solution)/shard_map/pallas_call | solution.py:188
  34.5 10.3 %all_to_all.20 = f32[16,4,256]{2,1,0:T(4,128)S(1)} all-to-all(f32[16,4,256]{2,1,0:T(4,128)} %get-tuple-element.17), channel_id=1, replica_groups=mesh['groups'=2,'tm'=16] {'tm'}, dimensions={0} | all-to-all | bytes 131072 | tf_op jit(solution)/shard_map/all_to_all | solution.py:293
  44.8 0.6 reshape.37.c2_ref
  45.5 8.7 %shard_map.114 = (f32[256,256]{1,0:T(8,128)}, f32[256,256]{1,0:T(8,128)}, f32[16,4,384]{2,1,0:T(4,128)}) custom-call(f32[256,256]{1,0:T(8,128)} %get-tuple-element.16.d2_ref, s32[4,4]{1,0:T(4,128)} %len_ref.9, f32[64,256]{1,0:T(8,128)} %reshape.37.c2_ref, f32[256,256]{1,0:T(8,128)} %bitcast.10, f32[256,256]{1,0:T(8,128)} %bitcast.7, ...), custom_call_target="tpu_custom_call" | custom-call | tf_op jit(solution)/shard_map/pallas_call | solution.py:188
  54.1 10.9 %all_to_all.21 = f32[16,4,384]{2,1,0:T(4,128)S(1)} all-to-all(f32[16,4,384]{2,1,0:T(4,128)} %get-tuple-element.20), channel_id=1, replica_groups=mesh['groups'=2,'tm'=16] {'tm'}, dimensions={0} | all-to-all | bytes 196608 | tf_op jit(solution)/shard_map/all_to_all | solution.py:293
  65.0 0.7 reshape.39.c3_ref
  65.7 8.8 %shard_map.115 = (f32[256,256]{1,0:T(8,128)}, f32[16,4,256]{2,1,0:T(4,128)}) custom-call(f32[256,256]{1,0:T(8,128)} %get-tuple-element.19.w3_ref, s32[4,4]{1,0:T(4,128)} %len_ref.9, f32[64,384]{1,0:T(8,128)} %reshape.39.c3_ref, f32[256,64]{1,0:T(8,128)} %copy.14.imap_ref, f32[64,256]{1,0:T(8,128)} %gain_ref.3, ...), custom_call_target="tpu_custom_call" | custom-call | tf_op jit(solution)/shard_map/pallas_call | solution.py:188
  74.5 3.5 %all-to-all-start.3 = ((f32[16,4,256]{2,1,0:T(4,128)}), f32[16,4,256]{2,1,0:T(4,128)S(1)}, u32[]{:S(2)}, u32[]{:S(2)}) async-start(f32[16,4,256]{2,1,0:T(4,128)} %get-tuple-element.22), calls=%async_computation.3 | async-start | bytes 131072 | tf_op jit(solution)/shard_map/all_to_all | solution.py:293
  77.9 0.9 slice_reduce_fusion
  78.8 0.1 reshape_squeeze.3
  78.9 0.6 reduce_sum.9
  79.5 5.4 %all-to-all-done.3 = f32[16,4,256]{2,1,0:T(4,128)S(1)} async-done(((f32[16,4,256]{2,1,0:T(4,128)}), f32[16,4,256]{2,1,0:T(4,128)S(1)}, u32[]{:S(2)}, u32[]{:S(2)}) %all-to-all-start.3) | async-done | bytes 65568 | tf_op jit(solution)/shard_map/all_to_all | solution.py:293
  84.8 0.6 reshape.40.c4_ref
  85.5 5.8 %shard_map.116 = f32[256,256]{1,0:T(8,128)} custom-call(f32[256,256]{1,0:T(8,128)} %get-tuple-element.21.s4_ref, s32[4,4]{1,0:T(4,128)} %len_ref.9, f32[64,256]{1,0:T(8,128)} %reshape.40.c4_ref, f32[256,256]{1,0:T(8,128)} %get-tuple-element.18.x_ref, f32[256,256]{1,0:T(8,128)} %bitcast.8, f32[10,256,256]{2,1,0:T(8,128)} %get-tuple-element.15.pwb_ref.pwf_ref), custom_call_target="tpu_custom_call" | custom-call | tf_op jit(solution)/shard_map/pallas_call | solution.py:188
Async XLA Ops:
  10.7 14.3 %all-to-all-start = ((f32[16,4,256]{2,1,0:T(4,128)}), f32[16,4,256]{2,1,0:T(4,128)S(1)}, u32[]{:S(2)}, u32[]{:S(2)}) async-start(f32[16,4,256]{2,1,0:T(4,128)} %get-tuple-element.14), calls=%async_computation | async-start | bytes 131072 | tf_op jit(solution)/shard_map/all_to_all | solution.py:293
  74.5 10.4 %all-to-all-start.3 = ((f32[16,4,256]{2,1,0:T(4,128)}), f32[16,4,256]{2,1,0:T(4,128)S(1)}, u32[]{:S(2)}, u32[]{:S(2)}) async-start(f32[16,4,256]{2,1,0:T(4,128)} %get-tuple-element.22), calls=%async_computation.3 | async-start | bytes 131072 | tf_op jit(solution)/shard_map/all_to_all | solution.py:293

commit v12 on v11

--- a/solution.py
+++ b/solution.py
@@ -54,7 +54,9 @@
     b_hi, b_lo = _split(b)
     part = functools.partial(lax.dot_general, dimension_numbers=dims,
                              preferred_element_type=jnp.float32)
-    return part(a_lo, b_hi) + part(a_hi, b_lo) + part(a_hi, b_hi)
+    rows = a.shape[0]
+    both = part(jnp.concatenate([a_hi, a_lo], axis=0), b_hi)
+    return both[:rows] + both[rows:] + part(a_hi, b_lo)
 
 
 def _build(decay_ref, coupling_ref, links_ref):

time: 91.8 us -> 90.9 us (level)
  no operation moved by 1% of the time
where the time goes in v12:
time: 90.9 us; the launch traced here: 90.4 us
  Pallas kernels  41.3 us (45%)
  blocking collectives  21.2 us (23%)
  starting transfers between devices  10.8 us (12%)
  waiting for transfers between devices  10.7 us (12%)
  local copies, waits for them, and re-layouts  5.16 us (6%)
    pallas_call x5, Pallas kernels, _call(): pl.pallas_call(kernel, out_shape=outs, in_specs=specs, out_specs=tuple(_v...  41.3 us
    all_to_all x2, blocking collectives, gather(): every = lax.all_to_all(copies, 'tm', 0, 0, tiled=True)  21.2 us
    all_to_all x2, starting transfers between devices, gather(): every = lax.all_to_all(copies, 'tm', 0, 0, tiled=True)  10.8 us
    all_to_all x2, waiting for transfers between devices, gather(): every = lax.all_to_all(copies, 'tm', 0, 0, tiled=True)  10.7 us
    reshape x4, local copies, waits for them, and re-layouts, gather(): return every.reshape(devices * scen_count, copies.shape[2])  2.63 us
  transfers between devices with their start and end apart: 2, of which 2 were waited for; matrix products, arithmetic and copies ran while one was open for 3% of the time, Pallas kernels for 0%

profile of v12, /device:TPU:0, one launch (start us, length us, event | category | flops | bytes accessed | tf_op | source)
XLA Modules:
  0.0 90.4 jit_solution(10858691093403007335)
XLA Ops:
  0.6 10.2 %shard_map.112 = (f32[10,256,256]{2,1,0:T(8,128)}, f32[256,256]{1,0:T(8,128)}, f32[16,4,256]{2,1,0:T(4,128)}) custom-call(f32[1,256]{1,0:T(1,128)} %bitcast.13, f32[3,64,64]{2,1,0:T(8,128)} %coupling_ref.1, s32[2,3]{1,0:T(2,128)} %bitcast.14, f32[256,256]{1,0:T(8,128)} %bitcast.9, f32[256,256]{1,0:T(8,128)} %bitcast.6, s32[4,4]{1,0:T(4,128)} %len_ref.9), custom_call_target="tpu_custom_call" | custom-call | tf_op jit(solution)/shard_map/pallas_call | solution.py:190
  10.8 7.4 %all-to-all-start = ((f32[16,4,256]{2,1,0:T(4,128)}), f32[16,4,256]{2,1,0:T(4,128)S(1)}, u32[]{:S(2)}, u32[]{:S(2)}) async-start(f32[16,4,256]{2,1,0:T(4,128)} %get-tuple-element.14), calls=%async_computation | async-start | bytes 131072 | tf_op jit(solution)/shard_map/all_to_all | solution.py:295
  18.2 1.6 %copy.14.imap_ref = f32[256,64]{1,0:T(8,128)} copy(f32[256,64]{0,1:T(8,128)} %param.15) | data formatting | bytes 131072 | tf_op args[6]
  19.8 5.3 %all-to-all-done = f32[16,4,256]{2,1,0:T(4,128)S(1)} async-done(((f32[16,4,256]{2,1,0:T(4,128)}), f32[16,4,256]{2,1,0:T(4,128)S(1)}, u32[]{:S(2)}, u32[]{:S(2)}) %all-to-all-start) | async-done | bytes 65568 | tf_op jit(solution)/shard_map/all_to_all | solution.py:295
  25.1 0.7 reshape.36.c1_ref
  25.8 8.7 %shard_map.113 = (f32[256,256]{1,0:T(8,128)}, f32[16,4,256]{2,1,0:T(4,128)}) custom-call(f32[256,256]{1,0:T(8,128)} %get-tuple-element.13.w1_ref, s32[4,4]{1,0:T(4,128)} %len_ref.9, f32[64,256]{1,0:T(8,128)} %reshape.36.c1_ref, f32[4,256]{1,0:T(4,128)} %xi_ref.1, f32[64,256]{1,0:T(8,128)} %gain_ref.3, f32[256,64]{1,0:T(8,128)} %copy.14.imap_ref, ...), custom_call_target="tpu_custom_call" | custom-call | tf_op jit(solution)/shard_map/pallas_call | solution.py:190
  34.4 10.3 %all_to_all.20 = f32[16,4,256]{2,1,0:T(4,128)S(1)} all-to-all(f32[16,4,256]{2,1,0:T(4,128)} %get-tuple-element.17), channel_id=1, replica_groups=mesh['groups'=2,'tm'=16] {'tm'}, dimensions={0} | all-to-all | bytes 131072 | tf_op jit(solution)/shard_map/all_to_all | solution.py:295
  44.8 0.6 reshape.37.c2_ref
  45.4 8.3 %shard_map.114 = (f32[256,256]{1,0:T(8,128)}, f32[256,256]{1,0:T(8,128)}, f32[16,4,384]{2,1,0:T(4,128)}) custom-call(f32[256,256]{1,0:T(8,128)} %get-tuple-element.16.d2_ref, s32[4,4]{1,0:T(4,128)} %len_ref.9, f32[64,256]{1,0:T(8,128)} %reshape.37.c2_ref, f32[256,256]{1,0:T(8,128)} %bitcast.10, f32[256,256]{1,0:T(8,128)} %bitcast.7, ...), custom_call_target="tpu_custom_call" | custom-call | tf_op jit(solution)/shard_map/pallas_call | solution.py:190
  53.7 10.9 %all_to_all.21 = f32[16,4,384]{2,1,0:T(4,128)S(1)} all-to-all(f32[16,4,384]{2,1,0:T(4,128)} %get-tuple-element.20), channel_id=1, replica_groups=mesh['groups'=2,'tm'=16] {'tm'}, dimensions={0} | all-to-all | bytes 196608 | tf_op jit(solution)/shard_map/all_to_all | solution.py:295
  64.6 0.7 reshape.39.c3_ref
  65.3 8.6 %shard_map.115 = (f32[256,256]{1,0:T(8,128)}, f32[16,4,256]{2,1,0:T(4,128)}) custom-call(f32[256,256]{1,0:T(8,128)} %get-tuple-element.19.w3_ref, s32[4,4]{1,0:T(4,128)} %len_ref.9, f32[64,384]{1,0:T(8,128)} %reshape.39.c3_ref, f32[256,64]{1,0:T(8,128)} %copy.14.imap_ref, f32[64,256]{1,0:T(8,128)} %gain_ref.3, ...), custom_call_target="tpu_custom_call" | custom-call | tf_op jit(solution)/shard_map/pallas_call | solution.py:190
  73.9 3.5 %all-to-all-start.3 = ((f32[16,4,256]{2,1,0:T(4,128)}), f32[16,4,256]{2,1,0:T(4,128)S(1)}, u32[]{:S(2)}, u32[]{:S(2)}) async-start(f32[16,4,256]{2,1,0:T(4,128)} %get-tuple-element.22), calls=%async_computation.3 | async-start | bytes 131072 | tf_op jit(solution)/shard_map/all_to_all | solution.py:295
  77.4 0.9 slice_reduce_fusion
  78.2 0.1 reshape_squeeze.3
  78.3 0.6 reduce_sum.9
  78.9 5.4 %all-to-all-done.3 = f32[16,4,256]{2,1,0:T(4,128)S(1)} async-done(((f32[16,4,256]{2,1,0:T(4,128)}), f32[16,4,256]{2,1,0:T(4,128)S(1)}, u32[]{:S(2)}, u32[]{:S(2)}) %all-to-all-start.3) | async-done | bytes 65568 | tf_op jit(solution)/shard_map/all_to_all | solution.py:295
  84.2 0.6 reshape.40.c4_ref
  84.9 5.5 %shard_map.116 = f32[256,256]{1,0:T(8,128)} custom-call(f32[256,256]{1,0:T(8,128)} %get-tuple-element.21.s4_ref, s32[4,4]{1,0:T(4,128)} %len_ref.9, f32[64,256]{1,0:T(8,128)} %reshape.40.c4_ref, f32[256,256]{1,0:T(8,128)} %get-tuple-element.18.x_ref, f32[256,256]{1,0:T(8,128)} %bitcast.8, f32[10,256,256]{2,1,0:T(8,128)} %get-tuple-element.15.pwb_ref.pwf_ref), custom_call_target="tpu_custom_call" | custom-call | tf_op jit(solution)/shard_map/pallas_call | solution.py:190
Async XLA Ops:
  10.8 14.3 %all-to-all-start = ((f32[16,4,256]{2,1,0:T(4,128)}), f32[16,4,256]{2,1,0:T(4,128)S(1)}, u32[]{:S(2)}, u32[]{:S(2)}) async-start(f32[16,4,256]{2,1,0:T(4,128)} %get-tuple-element.14), calls=%async_computation | async-start | bytes 131072 | tf_op jit(solution)/shard_map/all_to_all | solution.py:295
  73.9 10.4 %all-to-all-start.3 = ((f32[16,4,256]{2,1,0:T(4,128)}), f32[16,4,256]{2,1,0:T(4,128)S(1)}, u32[]{:S(2)}, u32[]{:S(2)}) async-start(f32[16,4,256]{2,1,0:T(4,128)} %get-tuple-element.22), calls=%async_computation.3 | async-start | bytes 131072 | tf_op jit(solution)/shard_map/all_to_all | solution.py:295

commit v13 on v12

--- a/solution.py
+++ b/solution.py
@@ -210,8 +210,8 @@
         pwb_ref[level] = power
 
 
-def k_states_in(seg, w1_ref, len_ref, c1_ref, xi_ref, gain_ref, imap_ref, pwb_ref,
-                pwf_ref, d2_ref, e2_ref):
+def k_states_in(seg, w1_ref, len_ref, c1_ref, xi_ref, gain_ref, imap_ref, pwb_ref, d2_ref, e2_ref):
+    pwf_ref = pwb_ref
     shape = w1_ref.shape
     cut_e = _cut_rows(len_ref, shape, seg, False)
     cut_s = _cut_rows(len_ref, shape, seg, True)
@@ -228,8 +228,9 @@
     e2_ref[...] = _ends(_scan(d2, cut_s, pwf_ref, seg, False), seg, False, e2_ref.shape[0])
 
 
-def k_adjoint_in(seg, scale, d2_ref, len_ref, c2_ref, cw_ref, ref_ref, pwf_ref, pwb_ref,
-                 x_ref, w3_ref, e3_ref):
+def k_adjoint_in(seg, scale, d2_ref, len_ref, c2_ref, cw_ref, ref_ref, pwf_ref, x_ref, w3_ref,
+                 e3_ref):
+    pwb_ref = pwf_ref
     shape = d2_ref.shape
     rows, width = shape
     scen = rows // seg
@@ -252,8 +253,8 @@
     e3_ref[:, :, :width] = _ends(_scan(w3, cut_e, pwb_ref, seg, True), seg, True, copies)
 
 
-def k_value_adjoint_in(seg, w3_ref, len_ref, c3_ref, imap_ref, gain_ref, pwb_ref,
-                       pwf_ref, s4_ref, e4_ref):
+def k_value_adjoint_in(seg, w3_ref, len_ref, c3_ref, imap_ref, gain_ref, pwb_ref, s4_ref, e4_ref):
+    pwf_ref = pwb_ref
     shape = w3_ref.shape
     cut_e = _cut_rows(len_ref, shape, seg, False)
     cut_s = _cut_rows(len_ref, shape, seg, True)
@@ -302,16 +303,16 @@
     pwf = pwb
     d2, e2 = _call(
         functools.partial(k_states_in, seg), (full, ends),
-        w1, lengths, gather(e1), x_init, ff_gain, input_map, pwb, pwf, smem=(1,))
+        w1, lengths, gather(e1), x_init, ff_gain, input_map, pwb, smem=(1,))
     packed = jax.ShapeDtypeStruct((devices, scen_count, width + 128), f32)
     states, w3, e3 = _call(
         functools.partial(k_adjoint_in, seg, 0.5 / total), (full, full, packed),
-        d2, lengths, gather(e2), cw, ref, pwf, pwb, smem=(1,))
+        d2, lengths, gather(e2), cw, ref, pwf, smem=(1,))
     g3 = gather(e3)
     cost = jnp.sum(g3[:, width].reshape(devices, scen_count), axis=0)
     s4, e4 = _call(
         functools.partial(k_value_adjoint_in, seg), (full, ends),
-        w3, lengths, g3, input_map, ff_gain, pwb, pwf, smem=(1,))
+        w3, lengths, g3, input_map, ff_gain, pwb, smem=(1,))
     (grad,) = _call(
         functools.partial(k_last, seg), (full,), s4, lengths, gather(e4), states, ref, pwf,
         smem=(1,))

time: 90.9 us -> 88.6 us (0.975)
  Pallas kernels: 41.3 us -> 38.9 us
    pallas_call x5, Pallas kernels: 41.3 us -> 38.9 us  [_call(): pl.pallas_call(kernel, out_shape=outs, in_specs=specs, out_specs=tuple(_v...]
  transfers between devices with their start and end apart: 2 -> 2, of which waited for: 2 -> 2; matrix products, arithmetic and copies ran while one was open for 3% -> 4% of each run, Pallas kernels for 0% -> 0%
where the time goes in v13:
time: 88.6 us; the launch traced here: 88 us
  Pallas kernels  38.9 us (44%)
  blocking collectives  21.2 us (24%)
  starting transfers between devices  10.8 us (12%)
  waiting for transfers between devices  10.7 us (12%)
  local copies, waits for them, and re-layouts  5.16 us (6%)
    pallas_call x5, Pallas kernels, _call(): pl.pallas_call(kernel, out_shape=outs, in_specs=specs, out_specs=tuple(_v...  38.9 us
    all_to_all x2, blocking collectives, gather(): every = lax.all_to_all(copies, 'tm', 0, 0, tiled=True)  21.2 us
    all_to_all x2, starting transfers between devices, gather(): every = lax.all_to_all(copies, 'tm', 0, 0, tiled=True)  10.8 us
    all_to_all x2, waiting for transfers between devices, gather(): every = lax.all_to_all(copies, 'tm', 0, 0, tiled=True)  10.7 us
    reshape x4, local copies, waits for them, and re-layouts, gather(): return every.reshape(devices * scen_count, copies.shape[2])  2.63 us
  transfers between devices with their start and end apart: 2, of which 2 were waited for; matrix products, arithmetic and copies ran while one was open for 4% of the time, Pallas kernels for 0%

profile of v13, /device:TPU:0, one launch (start us, length us, event | category | flops | bytes accessed | tf_op | source)
XLA Modules:
  0.0 88.0 jit_solution(8153160619112191634)
XLA Ops:
  0.6 10.2 %shard_map.112 = (f32[10,256,256]{2,1,0:T(8,128)}, f32[256,256]{1,0:T(8,128)}, f32[16,4,256]{2,1,0:T(4,128)}) custom-call(f32[1,256]{1,0:T(1,128)} %bitcast.13, f32[3,64,64]{2,1,0:T(8,128)} %coupling_ref.1, s32[2,3]{1,0:T(2,128)} %bitcast.14, f32[256,256]{1,0:T(8,128)} %bitcast.9, f32[256,256]{1,0:T(8,128)} %bitcast.6, s32[4,4]{1,0:T(4,128)} %len_ref.9), custom_call_target="tpu_custom_call" | custom-call | tf_op jit(solution)/shard_map/pallas_call | solution.py:190
  10.8 7.4 %all-to-all-start = ((f32[16,4,256]{2,1,0:T(4,128)}), f32[16,4,256]{2,1,0:T(4,128)S(1)}, u32[]{:S(2)}, u32[]{:S(2)}) async-start(f32[16,4,256]{2,1,0:T(4,128)} %get-tuple-element.14), calls=%async_computation | async-start | bytes 131072 | tf_op jit(solution)/shard_map/all_to_all | solution.py:296
  18.2 1.6 %copy.14.imap_ref = f32[256,64]{1,0:T(8,128)} copy(f32[256,64]{0,1:T(8,128)} %param.15) | data formatting | bytes 131072 | tf_op args[6]
  19.8 5.3 %all-to-all-done = f32[16,4,256]{2,1,0:T(4,128)S(1)} async-done(((f32[16,4,256]{2,1,0:T(4,128)}), f32[16,4,256]{2,1,0:T(4,128)S(1)}, u32[]{:S(2)}, u32[]{:S(2)}) %all-to-all-start) | async-done | bytes 65568 | tf_op jit(solution)/shard_map/all_to_all | solution.py:296
  25.1 0.7 reshape.36.c1_ref
  25.8 7.9 %shard_map.113 = (f32[256,256]{1,0:T(8,128)}, f32[16,4,256]{2,1,0:T(4,128)}) custom-call(f32[256,256]{1,0:T(8,128)} %get-tuple-element.13.w1_ref, s32[4,4]{1,0:T(4,128)} %len_ref.9, f32[64,256]{1,0:T(8,128)} %reshape.36.c1_ref, f32[4,256]{1,0:T(4,128)} %xi_ref.1, f32[64,256]{1,0:T(8,128)} %gain_ref.3, f32[256,64]{1,0:T(8,128)} %copy.14.imap_ref, ...), custom_call_target="tpu_custom_call" | custom-call | tf_op jit(solution)/shard_map/pallas_call | solution.py:190
  33.7 10.3 %all_to_all.20 = f32[16,4,256]{2,1,0:T(4,128)S(1)} all-to-all(f32[16,4,256]{2,1,0:T(4,128)} %get-tuple-element.17), channel_id=1, replica_groups=mesh['groups'=2,'tm'=16] {'tm'}, dimensions={0} | all-to-all | bytes 131072 | tf_op jit(solution)/shard_map/all_to_all | solution.py:296
  44.0 0.6 reshape.37.c2_ref
  44.7 7.5 %shard_map.114 = (f32[256,256]{1,0:T(8,128)}, f32[256,256]{1,0:T(8,128)}, f32[16,4,384]{2,1,0:T(4,128)}) custom-call(f32[256,256]{1,0:T(8,128)} %get-tuple-element.16.d2_ref, s32[4,4]{1,0:T(4,128)} %len_ref.9, f32[64,256]{1,0:T(8,128)} %reshape.37.c2_ref, f32[256,256]{1,0:T(8,128)} %bitcast.10, f32[256,256]{1,0:T(8,128)} %bitcast.7, ...), custom_call_target="tpu_custom_call" | custom-call | tf_op jit(solution)/shard_map/pallas_call | solution.py:190
  52.2 10.9 %all_to_all.21 = f32[16,4,384]{2,1,0:T(4,128)S(1)} all-to-all(f32[16,4,384]{2,1,0:T(4,128)} %get-tuple-element.20), channel_id=1, replica_groups=mesh['groups'=2,'tm'=16] {'tm'}, dimensions={0} | all-to-all | bytes 196608 | tf_op jit(solution)/shard_map/all_to_all | solution.py:296
  63.0 0.7 reshape.39.c3_ref
  63.7 7.8 %shard_map.115 = (f32[256,256]{1,0:T(8,128)}, f32[16,4,256]{2,1,0:T(4,128)}) custom-call(f32[256,256]{1,0:T(8,128)} %get-tuple-element.19.w3_ref, s32[4,4]{1,0:T(4,128)} %len_ref.9, f32[64,384]{1,0:T(8,128)} %reshape.39.c3_ref, f32[256,64]{1,0:T(8,128)} %copy.14.imap_ref, f32[64,256]{1,0:T(8,128)} %gain_ref.3, f32[10,256,256]{2,1,0:T(8,128)} %get-tuple-element.15.pwb_ref.pwf_ref), custom_call_target="tpu_custom_call" | custom-call | tf_op jit(solution)/shard_map/pallas_call | solution.py:190
  71.5 3.5 %all-to-all-start.3 = ((f32[16,4,256]{2,1,0:T(4,128)}), f32[16,4,256]{2,1,0:T(4,128)S(1)}, u32[]{:S(2)}, u32[]{:S(2)}) async-start(f32[16,4,256]{2,1,0:T(4,128)} %get-tuple-element.22), calls=%async_computation.3 | async-start | bytes 131072 | tf_op jit(solution)/shard_map/all_to_all | solution.py:296
  75.0 0.9 slice_reduce_fusion
  75.9 0.1 reshape_squeeze.3
  76.0 0.6 reduce_sum.9
  76.5 5.4 %all-to-all-done.3 = f32[16,4,256]{2,1,0:T(4,128)S(1)} async-done(((f32[16,4,256]{2,1,0:T(4,128)}), f32[16,4,256]{2,1,0:T(4,128)S(1)}, u32[]{:S(2)}, u32[]{:S(2)}) %all-to-all-start.3) | async-done | bytes 65568 | tf_op jit(solution)/shard_map/all_to_all | solution.py:296
  81.9 0.6 reshape.40.c4_ref
  82.5 5.5 %shard_map.116 = f32[256,256]{1,0:T(8,128)} custom-call(f32[256,256]{1,0:T(8,128)} %get-tuple-element.21.s4_ref, s32[4,4]{1,0:T(4,128)} %len_ref.9, f32[64,256]{1,0:T(8,128)} %reshape.40.c4_ref, f32[256,256]{1,0:T(8,128)} %get-tuple-element.18.x_ref, f32[256,256]{1,0:T(8,128)} %bitcast.8, f32[10,256,256]{2,1,0:T(8,128)} %get-tuple-element.15.pwb_ref.pwf_ref), custom_call_target="tpu_custom_call" | custom-call | tf_op jit(solution)/shard_map/pallas_call | solution.py:190
Async XLA Ops:
  10.8 14.3 %all-to-all-start = ((f32[16,4,256]{2,1,0:T(4,128)}), f32[16,4,256]{2,1,0:T(4,128)S(1)}, u32[]{:S(2)}, u32[]{:S(2)}) async-start(f32[16,4,256]{2,1,0:T(4,128)} %get-tuple-element.14), calls=%async_computation | async-start | bytes 131072 | tf_op jit(solution)/shard_map/all_to_all | solution.py:296
  71.5 10.4 %all-to-all-start.3 = ((f32[16,4,256]{2,1,0:T(4,128)}), f32[16,4,256]{2,1,0:T(4,128)S(1)}, u32[]{:S(2)}, u32[]{:S(2)}) async-start(f32[16,4,256]{2,1,0:T(4,128)} %get-tuple-element.22), calls=%async_computation.3 | async-start | bytes 131072 | tf_op jit(solution)/shard_map/all_to_all | solution.py:296

commit v14 on v12

--- a/solution.py
+++ b/solution.py
@@ -48,10 +48,19 @@
     return hi, lo
 
 
+class _Pair:
+    def __init__(self, hi, lo):
+        self.hi, self.lo = hi, lo
+        self.shape = hi.shape
+
+    def __getitem__(self, index):
+        return (self.hi[index], self.lo[index])
+
+
 def _mm(a, b, nt=False):
     dims = (((1,), (1 if nt else 0,)), ((), ()))
     a_hi, a_lo = _split(a)
-    b_hi, b_lo = _split(b)
+    b_hi, b_lo = b if isinstance(b, tuple) else _split(b)
     part = functools.partial(lax.dot_general, dimension_numbers=dims,
                              preferred_element_type=jnp.float32)
     rows = a.shape[0]
@@ -195,11 +204,12 @@
     )(*args)
 
 
-def k_first(seg, decay_ref, coupling_ref, links_ref, cw_ref, ref_ref, len_ref, pwb_ref, w1_ref,
-            e1_ref):
+def k_first(seg, decay_ref, coupling_ref, links_ref, cw_ref, ref_ref, len_ref, phi_ref, plo_ref,
+            w1_ref, e1_ref):
+    pwb_ref = _Pair(phi_ref, plo_ref)
     local_levels = seg.bit_length() - 1
     power = _build(decay_ref, coupling_ref, links_ref)
-    pwb_ref[0] = power
+    phi_ref[0], plo_ref[0] = _split(power)
     for level in range(1, pwb_ref.shape[0]):
         if level == local_levels:
             cut = _cut_rows(len_ref, cw_ref.shape, seg, False)
@@ -207,11 +217,12 @@
             w1_ref[...] = w1
             e1_ref[...] = _ends(_scan(w1, cut, pwb_ref, seg, True), seg, True, e1_ref.shape[0])
         power = _dot(power, power)
-        pwb_ref[level] = power
-
-
-def k_states_in(seg, w1_ref, len_ref, c1_ref, xi_ref, gain_ref, imap_ref, pwb_ref,
-                pwf_ref, d2_ref, e2_ref):
+        phi_ref[level], plo_ref[level] = _split(power)
+
+
+def k_states_in(seg, w1_ref, len_ref, c1_ref, xi_ref, gain_ref, imap_ref, phi_ref, plo_ref, d2_ref,
+                e2_ref):
+    pwb_ref = pwf_ref = _Pair(phi_ref, plo_ref)
     shape = w1_ref.shape
     cut_e = _cut_rows(len_ref, shape, seg, False)
     cut_s = _cut_rows(len_ref, shape, seg, True)
@@ -221,15 +232,16 @@
     forcing = -_mm(controls, imap_ref[...], nt=True)
     rows, width = shape
     scen = rows // seg
-    image = _dot_nt(xi_ref[...], pwf_ref[0])
+    image = _mm(xi_ref[...], pwf_ref[0], nt=True)
     init = jnp.broadcast_to(image[:, None, :], (scen, seg, width)).reshape(rows, width)
     d2 = forcing + cut_s * init
     d2_ref[...] = d2
     e2_ref[...] = _ends(_scan(d2, cut_s, pwf_ref, seg, False), seg, False, e2_ref.shape[0])
 
 
-def k_adjoint_in(seg, scale, d2_ref, len_ref, c2_ref, cw_ref, ref_ref, pwf_ref, pwb_ref,
-                 x_ref, w3_ref, e3_ref):
+def k_adjoint_in(seg, scale, d2_ref, len_ref, c2_ref, cw_ref, ref_ref, phi_ref, plo_ref, x_ref,
+                 w3_ref, e3_ref):
+    pwb_ref = pwf_ref = _Pair(phi_ref, plo_ref)
     shape = d2_ref.shape
     rows, width = shape
     scen = rows // seg
@@ -252,8 +264,9 @@
     e3_ref[:, :, :width] = _ends(_scan(w3, cut_e, pwb_ref, seg, True), seg, True, copies)
 
 
-def k_value_adjoint_in(seg, w3_ref, len_ref, c3_ref, imap_ref, gain_ref, pwb_ref,
-                       pwf_ref, s4_ref, e4_ref):
+def k_value_adjoint_in(seg, w3_ref, len_ref, c3_ref, imap_ref, gain_ref, phi_ref, plo_ref, s4_ref,
+                       e4_ref):
+    pwb_ref = pwf_ref = _Pair(phi_ref, plo_ref)
     shape = w3_ref.shape
     cut_e = _cut_rows(len_ref, shape, seg, False)
     cut_s = _cut_rows(len_ref, shape, seg, True)
@@ -265,7 +278,8 @@
     e4_ref[...] = _ends(_scan(source, cut_s, pwf_ref, seg, False), seg, False, e4_ref.shape[0])
 
 
-def k_last(seg, s4_ref, len_ref, c4_ref, x_ref, ref_ref, pwf_ref, g_ref):
+def k_last(seg, s4_ref, len_ref, c4_ref, x_ref, ref_ref, phi_ref, plo_ref, g_ref):
+    pwf_ref = _Pair(phi_ref, plo_ref)
     shape = s4_ref.shape
     cut_s = _cut_rows(len_ref, shape, seg, True)
     c4 = _carry(c4_ref, len_ref, pwf_ref, s4_ref.shape[0] // seg, False, seg)
@@ -295,25 +309,24 @@
         every = lax.all_to_all(copies, "tm", 0, 0, tiled=True)
         return every.reshape(devices * scen_count, copies.shape[2])
 
-    powers = jax.ShapeDtypeStruct((power_count, width, width), f32)
-    pwb, w1, e1 = _call(
-        functools.partial(k_first, seg), (powers, full, ends),
+    powers = jax.ShapeDtypeStruct((power_count, width, width), jnp.bfloat16)
+    phi, plo, w1, e1 = _call(
+        functools.partial(k_first, seg), (powers, powers, full, ends),
         decay.reshape(1, width), coupling, links.T, cw, ref, lengths, smem=(2, 5))
-    pwf = pwb
     d2, e2 = _call(
         functools.partial(k_states_in, seg), (full, ends),
-        w1, lengths, gather(e1), x_init, ff_gain, input_map, pwb, pwf, smem=(1,))
+        w1, lengths, gather(e1), x_init, ff_gain, input_map, phi, plo, smem=(1,))
     packed = jax.ShapeDtypeStruct((devices, scen_count, width + 128), f32)
     states, w3, e3 = _call(
         functools.partial(k_adjoint_in, seg, 0.5 / total), (full, full, packed),
-        d2, lengths, gather(e2), cw, ref, pwf, pwb, smem=(1,))
+        d2, lengths, gather(e2), cw, ref, phi, plo, smem=(1,))
     g3 = gather(e3)
     cost = jnp.sum(g3[:, width].reshape(devices, scen_count), axis=0)
     s4, e4 = _call(
         functools.partial(k_value_adjoint_in, seg), (full, ends),
-        w3, lengths, g3, input_map, ff_gain, pwb, pwf, smem=(1,))
+        w3, lengths, g3, input_map, ff_gain, phi, plo, smem=(1,))
     (grad,) = _call(
-        functools.partial(k_last, seg), (full,), s4, lengths, gather(e4), states, ref, pwf,
+        functools.partial(k_last, seg), (full,), s4, lengths, gather(e4), states, ref, phi, plo,
         smem=(1,))
     shape3 = (scen_count, seg_steps, width)
     return (states.reshape(shape3), grad.reshape(shape3), cost)

time: 90.9 us -> 88.5 us (0.974)
  Pallas kernels: 41.3 us -> 38.6 us
    pallas_call x5, Pallas kernels: 41.3 us -> 38.6 us  [_call(): pl.pallas_call(kernel, out_shape=outs, in_specs=specs, out_specs=tuple(_v...]
  transfers between devices with their start and end apart: 2 -> 2, of which waited for: 2 -> 2; matrix products, arithmetic and copies ran while one was open for 3% -> 4% of each run, Pallas kernels for 0% -> 0%
where the time goes in v14:
time: 88.5 us; the launch traced here: 87.9 us
  Pallas kernels  38.6 us (44%)
  blocking collectives  21.4 us (24%)
  starting transfers between devices  10.8 us (12%)
  waiting for transfers between devices  10.7 us (12%)
  local copies, waits for them, and re-layouts  5.16 us (6%)
    pallas_call x5, Pallas kernels, _call(): pl.pallas_call(kernel, out_shape=outs, in_specs=specs, out_specs=tuple(_v...  38.6 us
    all_to_all x2, blocking collectives, gather(): every = lax.all_to_all(copies, 'tm', 0, 0, tiled=True)  21.4 us
    all_to_all x2, starting transfers between devices, gather(): every = lax.all_to_all(copies, 'tm', 0, 0, tiled=True)  10.8 us
    all_to_all x2, waiting for transfers between devices, gather(): every = lax.all_to_all(copies, 'tm', 0, 0, tiled=True)  10.7 us
    reshape x4, local copies, waits for them, and re-layouts, gather(): return every.reshape(devices * scen_count, copies.shape[2])  2.63 us
  transfers between devices with their start and end apart: 2, of which 2 were waited for; matrix products, arithmetic and copies ran while one was open for 4% of the time, Pallas kernels for 0%

profile of v14, /device:TPU:0, one launch (start us, length us, event | category | flops | bytes accessed | tf_op | source)
XLA Modules:
  0.0 87.9 jit_solution(6477073653662883038)
XLA Ops:
  0.6 10.2 %shard_map.112 = (bf16[10,256,256]{2,1,0:T(8,128)(2,1)}, bf16[10,256,256]{2,1,0:T(8,128)(2,1)}, f32[256,256]{1,0:T(8,128)}, f32[16,4,256]{2,1,0:T(4,128)}) custom-call(f32[1,256]{1,0:T(1,128)} %bitcast.13, f32[3,64,64]{2,1,0:T(8,128)} %coupling_ref.1, s32[2,3]{1,0:T(2,128)} %bitcast.14, f32[256,256]{1,0:T(8,128)} %bitcast.9, f32[256,256]{1,0:T(8,128)} %bitcast.6, ...), custom_call_target="tpu_custom_call" | custom-call | tf_op jit(solution)/shard_map/pallas_call | solution.py:199
  10.8 7.4 %all-to-all-start = ((f32[16,4,256]{2,1,0:T(4,128)}), f32[16,4,256]{2,1,0:T(4,128)S(1)}, u32[]{:S(2)}, u32[]{:S(2)}) async-start(f32[16,4,256]{2,1,0:T(4,128)} %get-tuple-element.15), calls=%async_computation | async-start | bytes 131072 | tf_op jit(solution)/shard_map/all_to_all | solution.py:309
  18.2 1.6 %copy.14.imap_ref = f32[256,64]{1,0:T(8,128)} copy(f32[256,64]{0,1:T(8,128)} %param.15) | data formatting | bytes 131072 | tf_op args[6]
  19.7 5.3 %all-to-all-done = f32[16,4,256]{2,1,0:T(4,128)S(1)} async-done(((f32[16,4,256]{2,1,0:T(4,128)}), f32[16,4,256]{2,1,0:T(4,128)S(1)}, u32[]{:S(2)}, u32[]{:S(2)}) %all-to-all-start) | async-done | bytes 65568 | tf_op jit(solution)/shard_map/all_to_all | solution.py:309
  25.1 0.7 reshape.36.c1_ref
  25.7 7.8 %shard_map.113 = (f32[256,256]{1,0:T(8,128)}, f32[16,4,256]{2,1,0:T(4,128)}) custom-call(f32[256,256]{1,0:T(8,128)} %get-tuple-element.14.w1_ref, s32[4,4]{1,0:T(4,128)} %len_ref.9, f32[64,256]{1,0:T(8,128)} %reshape.36.c1_ref, f32[4,256]{1,0:T(4,128)} %xi_ref.1, f32[64,256]{1,0:T(8,128)} %gain_ref.3, f32[256,64]{1,0:T(8,128)} %copy.14.imap_ref, ...), custom_call_target="tpu_custom_call" | custom-call | tf_op jit(solution)/shard_map/pallas_call | solution.py:199
  33.5 10.3 %all_to_all.20 = f32[16,4,256]{2,1,0:T(4,128)S(1)} all-to-all(f32[16,4,256]{2,1,0:T(4,128)} %get-tuple-element.19), channel_id=1, replica_groups=mesh['groups'=2,'tm'=16] {'tm'}, dimensions={0} | all-to-all | bytes 131072 | tf_op jit(solution)/shard_map/all_to_all | solution.py:309
  43.8 0.6 reshape.37.c2_ref
  44.5 7.5 %shard_map.114 = (f32[256,256]{1,0:T(8,128)}, f32[256,256]{1,0:T(8,128)}, f32[16,4,384]{2,1,0:T(4,128)}) custom-call(f32[256,256]{1,0:T(8,128)} %get-tuple-element.18.d2_ref, s32[4,4]{1,0:T(4,128)} %len_ref.9, f32[64,256]{1,0:T(8,128)} %reshape.37.c2_ref, f32[256,256]{1,0:T(8,128)} %bitcast.10, f32[256,256]{1,0:T(8,128)} %bitcast.7, ...), custom_call_target="tpu_custom_call" | custom-call | tf_op jit(solution)/shard_map/pallas_call | solution.py:199
  51.9 11.0 %all_to_all.21 = f32[16,4,384]{2,1,0:T(4,128)S(1)} all-to-all(f32[16,4,384]{2,1,0:T(4,128)} %get-tuple-element.22), channel_id=1, replica_groups=mesh['groups'=2,'tm'=16] {'tm'}, dimensions={0} | all-to-all | bytes 196608 | tf_op jit(solution)/shard_map/all_to_all | solution.py:309
  63.0 0.7 reshape.39.c3_ref
  63.7 7.7 %shard_map.115 = (f32[256,256]{1,0:T(8,128)}, f32[16,4,256]{2,1,0:T(4,128)}) custom-call(f32[256,256]{1,0:T(8,128)} %get-tuple-element.21.w3_ref, s32[4,4]{1,0:T(4,128)} %len_ref.9, f32[64,384]{1,0:T(8,128)} %reshape.39.c3_ref, f32[256,64]{1,0:T(8,128)} %copy.14.imap_ref, f32[64,256]{1,0:T(8,128)} %gain_ref.3, ...), custom_call_target="tpu_custom_call" | custom-call | tf_op jit(solution)/shard_map/pallas_call | solution.py:199
  71.4 3.5 %all-to-all-start.3 = ((f32[16,4,256]{2,1,0:T(4,128)}), f32[16,4,256]{2,1,0:T(4,128)S(1)}, u32[]{:S(2)}, u32[]{:S(2)}) async-start(f32[16,4,256]{2,1,0:T(4,128)} %get-tuple-element.24), calls=%async_computation.3 | async-start | bytes 131072 | tf_op jit(solution)/shard_map/all_to_all | solution.py:309
  74.9 0.9 slice_reduce_fusion
  75.8 0.1 reshape_squeeze.3
  75.8 0.6 reduce_sum.9
  76.4 5.4 %all-to-all-done.3 = f32[16,4,256]{2,1,0:T(4,128)S(1)} async-done(((f32[16,4,256]{2,1,0:T(4,128)}), f32[16,4,256]{2,1,0:T(4,128)S(1)}, u32[]{:S(2)}, u32[]{:S(2)}) %all-to-all-start.3) | async-done | bytes 65568 | tf_op jit(solution)/shard_map/all_to_all | solution.py:309
  81.7 0.6 reshape.40.c4_ref
  82.4 5.5 %shard_map.116 = f32[256,256]{1,0:T(8,128)} custom-call(f32[256,256]{1,0:T(8,128)} %get-tuple-element.23.s4_ref, s32[4,4]{1,0:T(4,128)} %len_ref.9, f32[64,256]{1,0:T(8,128)} %reshape.40.c4_ref, f32[256,256]{1,0:T(8,128)} %get-tuple-element.20.x_ref, f32[256,256]{1,0:T(8,128)} %bitcast.8, bf16[10,256,256]{2,1,0:T(8,128)(2,1)} %get-tuple-element.16.phi_ref, ...), custom_call_target="tpu_custom_call" | custom-call | tf_op jit(solution)/shard_map/pallas_call | solution.py:199
Async XLA Ops:
  10.8 14.3 %all-to-all-start = ((f32[16,4,256]{2,1,0:T(4,128)}), f32[16,4,256]{2,1,0:T(4,128)S(1)}, u32[]{:S(2)}, u32[]{:S(2)}) async-start(f32[16,4,256]{2,1,0:T(4,128)} %get-tuple-element.15), calls=%async_computation | async-start | bytes 131072 | tf_op jit(solution)/shard_map/all_to_all | solution.py:309
  71.4 10.4 %all-to-all-start.3 = ((f32[16,4,256]{2,1,0:T(4,128)}), f32[16,4,256]{2,1,0:T(4,128)S(1)}, u32[]{:S(2)}, u32[]{:S(2)}) async-start(f32[16,4,256]{2,1,0:T(4,128)} %get-tuple-element.24), calls=%async_computation.3 | async-start | bytes 131072 | tf_op jit(solution)/shard_map/all_to_all | solution.py:309

commit v15 on v14

--- a/solution.py
+++ b/solution.py
@@ -118,7 +118,6 @@
     g = g_ref[...][:, :width]
     rows = g.shape[0]
     devices = rows // scen
-    local_levels = pw_ref.shape[0] - max((devices - 1).bit_length(), 1)
     r = lax.broadcasted_iota(jnp.int32, (rows, width), 0)
     flags = jnp.broadcast_to(_seg_flags(len_ref, devices, seg, not backward), (rows, width))
     step = functools.partial(_mm, nt=not backward)
@@ -134,7 +133,7 @@
             valid = r >= stride
         prior_g = jnp.where(valid, prior_g, 0.0)
         prior_f = jnp.where(valid, prior_f, 1.0)
-        g = g + flags * step(prior_g, pw_ref[local_levels + level])
+        g = g + flags * step(prior_g, pw_ref[level])
         flags = flags * prior_f
     me = lax.axis_index("tm")
     target = me + 1 if backward else me - 1
@@ -205,28 +204,34 @@
 
 
 def k_first(seg, decay_ref, coupling_ref, links_ref, cw_ref, ref_ref, len_ref, phi_ref, plo_ref,
-            w1_ref, e1_ref):
+            top_ref, w1_ref, e1_ref):
     pwb_ref = _Pair(phi_ref, plo_ref)
-    local_levels = seg.bit_length() - 1
     power = _build(decay_ref, coupling_ref, links_ref)
     phi_ref[0], plo_ref[0] = _split(power)
     for level in range(1, pwb_ref.shape[0]):
-        if level == local_levels:
-            cut = _cut_rows(len_ref, cw_ref.shape, seg, False)
-            w1 = cw_ref[...] * ref_ref[...]
-            w1_ref[...] = w1
-            e1_ref[...] = _ends(_scan(w1, cut, pwb_ref, seg, True), seg, True, e1_ref.shape[0])
         power = _dot(power, power)
         phi_ref[level], plo_ref[level] = _split(power)
-
-
-def k_states_in(seg, w1_ref, len_ref, c1_ref, xi_ref, gain_ref, imap_ref, phi_ref, plo_ref, d2_ref,
+    top_ref[...] = power
+    cut = _cut_rows(len_ref, cw_ref.shape, seg, False)
+    w1 = cw_ref[...] * ref_ref[...]
+    w1_ref[...] = w1
+    e1_ref[...] = _ends(_scan(w1, cut, pwb_ref, seg, True), seg, True, e1_ref.shape[0])
+
+
+def k_device_powers(top_ref, dhi_ref, dlo_ref):
+    power = top_ref[...]
+    for level in range(dhi_ref.shape[0]):
+        power = _dot(power, power)
+        dhi_ref[level], dlo_ref[level] = _split(power)
+
+
+def k_states_in(seg, w1_ref, len_ref, c1_ref, xi_ref, gain_ref, imap_ref, phi_ref, plo_ref, dhi_ref, dlo_ref, d2_ref,
                 e2_ref):
     pwb_ref = pwf_ref = _Pair(phi_ref, plo_ref)
     shape = w1_ref.shape
     cut_e = _cut_rows(len_ref, shape, seg, False)
     cut_s = _cut_rows(len_ref, shape, seg, True)
-    c1 = _carry(c1_ref, len_ref, pwb_ref, w1_ref.shape[0] // seg, True, seg)
+    c1 = _carry(c1_ref, len_ref, _Pair(dhi_ref, dlo_ref), w1_ref.shape[0] // seg, True, seg)
     vt = _scan(w1_ref[...], cut_e, pwb_ref, seg, True, c1)
     controls = _mm(vt, gain_ref[...], nt=True)
     forcing = -_mm(controls, imap_ref[...], nt=True)
@@ -239,7 +244,7 @@
     e2_ref[...] = _ends(_scan(d2, cut_s, pwf_ref, seg, False), seg, False, e2_ref.shape[0])
 
 
-def k_adjoint_in(seg, scale, d2_ref, len_ref, c2_ref, cw_ref, ref_ref, phi_ref, plo_ref, x_ref,
+def k_adjoint_in(seg, scale, d2_ref, len_ref, c2_ref, cw_ref, ref_ref, phi_ref, plo_ref, dhi_ref, dlo_ref, x_ref,
                  w3_ref, e3_ref):
     pwb_ref = pwf_ref = _Pair(phi_ref, plo_ref)
     shape = d2_ref.shape
@@ -247,7 +252,7 @@
     scen = rows // seg
     cut_s = _cut_rows(len_ref, shape, seg, True)
     cut_e = _cut_rows(len_ref, shape, seg, False)
-    c2 = _carry(c2_ref, len_ref, pwf_ref, scen, False, seg)
+    c2 = _carry(c2_ref, len_ref, _Pair(dhi_ref, dlo_ref), scen, False, seg)
     states = _scan(d2_ref[...], cut_s, pwf_ref, seg, False, c2)
     x_ref[...] = states
     offset = states - ref_ref[...]
@@ -264,13 +269,13 @@
     e3_ref[:, :, :width] = _ends(_scan(w3, cut_e, pwb_ref, seg, True), seg, True, copies)
 
 
-def k_value_adjoint_in(seg, w3_ref, len_ref, c3_ref, imap_ref, gain_ref, phi_ref, plo_ref, s4_ref,
+def k_value_adjoint_in(seg, w3_ref, len_ref, c3_ref, imap_ref, gain_ref, phi_ref, plo_ref, dhi_ref, dlo_ref, s4_ref,
                        e4_ref):
     pwb_ref = pwf_ref = _Pair(phi_ref, plo_ref)
     shape = w3_ref.shape
     cut_e = _cut_rows(len_ref, shape, seg, False)
     cut_s = _cut_rows(len_ref, shape, seg, True)
-    c3 = _carry(c3_ref, len_ref, pwb_ref, w3_ref.shape[0] // seg, True, seg)
+    c3 = _carry(c3_ref, len_ref, _Pair(dhi_ref, dlo_ref), w3_ref.shape[0] // seg, True, seg)
     adjoint = _scan(w3_ref[...], cut_e, pwb_ref, seg, True, c3)
     pulled = _mm(adjoint, imap_ref[...])
     source = -_mm(pulled, gain_ref[...])
@@ -278,11 +283,11 @@
     e4_ref[...] = _ends(_scan(source, cut_s, pwf_ref, seg, False), seg, False, e4_ref.shape[0])
 
 
-def k_last(seg, s4_ref, len_ref, c4_ref, x_ref, ref_ref, phi_ref, plo_ref, g_ref):
+def k_last(seg, s4_ref, len_ref, c4_ref, x_ref, ref_ref, phi_ref, plo_ref, dhi_ref, dlo_ref, g_ref):
     pwf_ref = _Pair(phi_ref, plo_ref)
     shape = s4_ref.shape
     cut_s = _cut_rows(len_ref, shape, seg, True)
-    c4 = _carry(c4_ref, len_ref, pwf_ref, s4_ref.shape[0] // seg, False, seg)
+    c4 = _carry(c4_ref, len_ref, _Pair(dhi_ref, dlo_ref), s4_ref.shape[0] // seg, False, seg)
     va = _scan(s4_ref[...], cut_s, pwf_ref, seg, False, c4)
     ref = ref_ref[...]
     offset = x_ref[...] - ref
@@ -309,24 +314,27 @@
         every = lax.all_to_all(copies, "tm", 0, 0, tiled=True)
         return every.reshape(devices * scen_count, copies.shape[2])
 
-    powers = jax.ShapeDtypeStruct((power_count, width, width), jnp.bfloat16)
-    phi, plo, w1, e1 = _call(
-        functools.partial(k_first, seg), (powers, powers, full, ends),
+    powers = jax.ShapeDtypeStruct((local_levels, width, width), jnp.bfloat16)
+    square = jax.ShapeDtypeStruct((width, width), f32)
+    phi, plo, top, w1, e1 = _call(
+        functools.partial(k_first, seg), (powers, powers, square, full, ends),
         decay.reshape(1, width), coupling, links.T, cw, ref, lengths, smem=(2, 5))
+    dev = jax.ShapeDtypeStruct((max(device_levels, 1), width, width), jnp.bfloat16)
+    dhi, dlo = _call(k_device_powers, (dev, dev), top)
     d2, e2 = _call(
         functools.partial(k_states_in, seg), (full, ends),
-        w1, lengths, gather(e1), x_init, ff_gain, input_map, phi, plo, smem=(1,))
+        w1, lengths, gather(e1), x_init, ff_gain, input_map, phi, plo, dhi, dlo, smem=(1,))
     packed = jax.ShapeDtypeStruct((devices, scen_count, width + 128), f32)
     states, w3, e3 = _call(
         functools.partial(k_adjoint_in, seg, 0.5 / total), (full, full, packed),
-        d2, lengths, gather(e2), cw, ref, phi, plo, smem=(1,))
+        d2, lengths, gather(e2), cw, ref, phi, plo, dhi, dlo, smem=(1,))
     g3 = gather(e3)
     cost = jnp.sum(g3[:, width].reshape(devices, scen_count), axis=0)
     s4, e4 = _call(
         functools.partial(k_value_adjoint_in, seg), (full, ends),
-        w3, lengths, g3, input_map, ff_gain, phi, plo, smem=(1,))
+        w3, lengths, g3, input_map, ff_gain, phi, plo, dhi, dlo, smem=(1,))
     (grad,) = _call(
-        functools.partial(k_last, seg), (full,), s4, lengths, gather(e4), states, ref, phi, plo,
+        functools.partial(k_last, seg), (full,), s4, lengths, gather(e4), states, ref, phi, plo, dhi, dlo,
         smem=(1,))
     shape3 = (scen_count, seg_steps, width)
     return (states.reshape(shape3), grad.reshape(shape3), cost)

time: 88.5 us -> 86.2 us (0.974)
  waiting for transfers between devices: 10.7 us -> 7.45 us
  Pallas kernels: 38.6 us -> 39.7 us
    all_to_all x2, waiting for transfers between devices: 10.7 us -> 7.45 us  [gather(): every = lax.all_to_all(copies, 'tm', 0, 0, tiled=True)]
    pallas_call x5 -> x6, Pallas kernels: 38.6 us -> 39.7 us  [_call(): pl.pallas_call(kernel, out_shape=outs, in_specs=specs, out_specs=tuple(_v...]
  transfers between devices with their start and end apart: 2 -> 2, of which waited for: 2 -> 2; matrix products, arithmetic and copies ran while one was open for 4% -> 3% of each run, Pallas kernels for 0% -> 5%
where the time goes in v15:
time: 86.2 us; the launch traced here: 85.5 us
  Pallas kernels  39.7 us (46%)
  blocking collectives  21.9 us (25%)
  starting transfers between devices  11 us (13%)
  waiting for transfers between devices  7.45 us (9%)
  local copies, waits for them, and re-layouts  4.32 us (5%)
    pallas_call x6, Pallas kernels, _call(): pl.pallas_call(kernel, out_shape=outs, in_specs=specs, out_specs=tuple(_v...  39.7 us
    all_to_all x2, blocking collectives, gather(): every = lax.all_to_all(copies, 'tm', 0, 0, tiled=True)  21.9 us
    all_to_all x2, starting transfers between devices, gather(): every = lax.all_to_all(copies, 'tm', 0, 0, tiled=True)  11 us
    all_to_all x2, waiting for transfers between devices, gather(): every = lax.all_to_all(copies, 'tm', 0, 0, tiled=True)  7.45 us
    reshape x4, local copies, waits for them, and re-layouts, gather(): return every.reshape(devices * scen_count, copies.shape[2])  2.62 us
  transfers between devices with their start and end apart: 2, of which 2 were waited for; matrix products, arithmetic and copies ran while one was open for 3% of the time, Pallas kernels for 5%

profile of v15, /device:TPU:0, one launch (start us, length us, event | category | flops | bytes accessed | tf_op | source)
XLA Modules:
  0.0 85.5 jit_solution(11234057646927163386)
XLA Ops:
  0.6 7.4 %shard_map.112 = (bf16[6,256,256]{2,1,0:T(8,128)(2,1)}, bf16[6,256,256]{2,1,0:T(8,128)(2,1)}, f32[256,256]{1,0:T(8,128)}, f32[256,256]{1,0:T(8,128)}, f32[16,4,256]{2,1,0:T(4,128)}) custom-call(f32[1,256]{1,0:T(1,128)} %bitcast.13, f32[3,64,64]{2,1,0:T(8,128)} %coupling_ref.1, s32[2,3]{1,0:T(2,128)} %bitcast.14, f32[256,256]{1,0:T(8,128)} %bitcast.9, ...), custom_call_target="tpu_custom_call" | custom-call | tf_op jit(solution)/shard_map/pallas_call | solution.py:198
  8.1 0.0 copy-start
  8.1 7.5 %all-to-all-start = ((f32[16,4,256]{2,1,0:T(4,128)}), f32[16,4,256]{2,1,0:T(4,128)S(1)}, u32[]{:S(2)}, u32[]{:S(2)}) async-start(f32[16,4,256]{2,1,0:T(4,128)} %get-tuple-element.18), calls=%async_computation | async-start | bytes 131072 | tf_op jit(solution)/shard_map/all_to_all | solution.py:314
  15.6 0.0 copy-done
  15.6 0.8 copy.14.imap_ref
  16.3 4.0 %shard_map.113 = (bf16[4,256,256]{2,1,0:T(8,128)(2,1)}, bf16[4,256,256]{2,1,0:T(8,128)(2,1)}) custom-call(f32[256,256]{1,0:T(8,128)} %get-tuple-element.21.top_ref), custom_call_target="tpu_custom_call" | custom-call | tf_op jit(solution)/shard_map/pallas_call | solution.py:198
  20.4 2.1 %all-to-all-done = f32[16,4,256]{2,1,0:T(4,128)S(1)} async-done(((f32[16,4,256]{2,1,0:T(4,128)}), f32[16,4,256]{2,1,0:T(4,128)S(1)}, u32[]{:S(2)}, u32[]{:S(2)}) %all-to-all-start) | async-done | bytes 65568 | tf_op jit(solution)/shard_map/all_to_all | solution.py:314
  22.5 0.6 reshape.36.c1_ref
  23.1 7.7 %shard_map.114 = (f32[256,256]{1,0:T(8,128)}, f32[16,4,256]{2,1,0:T(4,128)}) custom-call(f32[256,256]{1,0:T(8,128)} %get-tuple-element.17.w1_ref, s32[4,4]{1,0:T(4,128)} %len_ref.9, f32[64,256]{1,0:T(8,128)} %reshape.36.c1_ref, f32[4,256]{1,0:T(4,128)} %xi_ref.1, f32[64,256]{1,0:T(8,128)} %gain_ref.3, f32[256,64]{1,0:T(8,128)} %copy.14.imap_ref, ...), custom_call_target="tpu_custom_call" | custom-call | tf_op jit(solution)/shard_map/pallas_call | solution.py:198
  30.8 10.8 %all_to_all.20 = f32[16,4,256]{2,1,0:T(4,128)S(1)} all-to-all(f32[16,4,256]{2,1,0:T(4,128)} %get-tuple-element.25), channel_id=1, replica_groups=mesh['groups'=2,'tm'=16] {'tm'}, dimensions={0} | all-to-all | bytes 131072 | tf_op jit(solution)/shard_map/all_to_all | solution.py:314
  41.7 0.7 reshape.37.c2_ref
  42.3 7.4 %shard_map.115 = (f32[256,256]{1,0:T(8,128)}, f32[256,256]{1,0:T(8,128)}, f32[16,4,384]{2,1,0:T(4,128)}) custom-call(f32[256,256]{1,0:T(8,128)} %get-tuple-element.24.d2_ref, s32[4,4]{1,0:T(4,128)} %len_ref.9, f32[64,256]{1,0:T(8,128)} %reshape.37.c2_ref, f32[256,256]{1,0:T(8,128)} %bitcast.10, f32[256,256]{1,0:T(8,128)} %bitcast.7, ...), custom_call_target="tpu_custom_call" | custom-call | tf_op jit(solution)/shard_map/pallas_call | solution.py:198
  49.7 11.0 %all_to_all.21 = f32[16,4,384]{2,1,0:T(4,128)S(1)} all-to-all(f32[16,4,384]{2,1,0:T(4,128)} %get-tuple-element.28), channel_id=1, replica_groups=mesh['groups'=2,'tm'=16] {'tm'}, dimensions={0} | all-to-all | bytes 196608 | tf_op jit(solution)/shard_map/all_to_all | solution.py:314
  60.8 0.7 reshape.39.c3_ref
  61.5 7.7 %shard_map.116 = (f32[256,256]{1,0:T(8,128)}, f32[16,4,256]{2,1,0:T(4,128)}) custom-call(f32[256,256]{1,0:T(8,128)} %get-tuple-element.27.w3_ref, s32[4,4]{1,0:T(4,128)} %len_ref.9, f32[64,384]{1,0:T(8,128)} %reshape.39.c3_ref, f32[256,64]{1,0:T(8,128)} %copy.14.imap_ref, f32[64,256]{1,0:T(8,128)} %gain_ref.3, ...), custom_call_target="tpu_custom_call" | custom-call | tf_op jit(solution)/shard_map/pallas_call | solution.py:198
  69.1 3.5 %all-to-all-start.3 = ((f32[16,4,256]{2,1,0:T(4,128)}), f32[16,4,256]{2,1,0:T(4,128)S(1)}, u32[]{:S(2)}, u32[]{:S(2)}) async-start(f32[16,4,256]{2,1,0:T(4,128)} %get-tuple-element.30), calls=%async_computation.3 | async-start | bytes 131072 | tf_op jit(solution)/shard_map/all_to_all | solution.py:314
  72.6 0.9 %slice_reduce_fusion = f32[64]{0:T(128)S(1)} fusion(f32[64,384]{1,0:T(8,128)} %reshape.39.c3_ref), kind=kLoop, calls=%fused_computation | loop fusion | bytes 512 | tf_op jit(solution)/shard_map/slice | solution.py:332
  73.5 0.1 reshape_squeeze.3
  73.6 0.6 reduce_sum.9
  74.1 5.4 %all-to-all-done.3 = f32[16,4,256]{2,1,0:T(4,128)S(1)} async-done(((f32[16,4,256]{2,1,0:T(4,128)}), f32[16,4,256]{2,1,0:T(4,128)S(1)}, u32[]{:S(2)}, u32[]{:S(2)}) %all-to-all-start.3) | async-done | bytes 65568 | tf_op jit(solution)/shard_map/all_to_all | solution.py:314
  79.5 0.6 reshape.40.c4_ref
  80.1 5.4 %shard_map.117 = f32[256,256]{1,0:T(8,128)} custom-call(f32[256,256]{1,0:T(8,128)} %get-tuple-element.29.s4_ref, s32[4,4]{1,0:T(4,128)} %len_ref.9, f32[64,256]{1,0:T(8,128)} %reshape.40.c4_ref, f32[256,256]{1,0:T(8,128)} %get-tuple-element.26.x_ref, f32[256,256]{1,0:T(8,128)} %bitcast.8, bf16[6,256,256]{2,1,0:T(8,128)(2,1)} %get-tuple-element.19.phi_ref, ...), custom_call_target="tpu_custom_call" | custom-call | tf_op jit(solution)/shard_map/pallas_call | solution.py:198
Async XLA Ops:
  8.1 7.5 %copy-start = (f32[256,64]{0,1:T(8,128)S(1)}, f32[256,64]{0,1:T(8,128)}, u32[]{:S(2)}) copy-start(f32[256,64]{0,1:T(8,128)} %param.15) | copy-start | bytes 196612
  8.1 14.4 %all-to-all-start = ((f32[16,4,256]{2,1,0:T(4,128)}), f32[16,4,256]{2,1,0:T(4,128)S(1)}, u32[]{:S(2)}, u32[]{:S(2)}) async-start(f32[16,4,256]{2,1,0:T(4,128)} %get-tuple-element.18), calls=%async_computation | async-start | bytes 131072 | tf_op jit(solution)/shard_map/all_to_all | solution.py:314
  69.1 10.4 %all-to-all-start.3 = ((f32[16,4,256]{2,1,0:T(4,128)}), f32[16,4,256]{2,1,0:T(4,128)S(1)}, u32[]{:S(2)}, u32[]{:S(2)}) async-start(f32[16,4,256]{2,1,0:T(4,128)} %get-tuple-element.30), calls=%async_computation.3 | async-start | bytes 131072 | tf_op jit(solution)/shard_map/all_to_all | solution.py:314

commit v16 on v15

--- a/solution.py
+++ b/solution.py
@@ -205,17 +205,28 @@
 
 def k_first(seg, decay_ref, coupling_ref, links_ref, cw_ref, ref_ref, len_ref, phi_ref, plo_ref,
             top_ref, w1_ref, e1_ref):
-    pwb_ref = _Pair(phi_ref, plo_ref)
     power = _build(decay_ref, coupling_ref, links_ref)
-    phi_ref[0], plo_ref[0] = _split(power)
-    for level in range(1, pwb_ref.shape[0]):
-        power = _dot(power, power)
-        phi_ref[level], plo_ref[level] = _split(power)
+    cut = _cut_rows(len_ref, cw_ref.shape, seg, False)
+    v = cw_ref[...] * ref_ref[...]
+    w1_ref[...] = v
+    rows, width = v.shape
+    t = lax.broadcasted_iota(jnp.int32, (rows, width), 0) % seg
+    flags = 1.0 - cut
+    for level in range(phi_ref.shape[0]):
+        if level:
+            power = _dot(power, power)
+        pair = _split(power)
+        phi_ref[level], plo_ref[level] = pair
+        stride = 2**level
+        prior_v = pltpu.roll(v, rows - stride, 0)
+        prior_f = pltpu.roll(flags, rows - stride, 0)
+        valid = t < seg - stride
+        prior_v = jnp.where(valid, prior_v, 0.0)
+        prior_f = jnp.where(valid, prior_f, 1.0)
+        v = v + flags * _mm(prior_v, pair)
+        flags = flags * prior_f
     top_ref[...] = power
-    cut = _cut_rows(len_ref, cw_ref.shape, seg, False)
-    w1 = cw_ref[...] * ref_ref[...]
-    w1_ref[...] = w1
-    e1_ref[...] = _ends(_scan(w1, cut, pwb_ref, seg, True), seg, True, e1_ref.shape[0])
+    e1_ref[...] = _ends(v, seg, True, e1_ref.shape[0])
 
 
 def k_device_powers(top_ref, dhi_ref, dlo_ref):

time: 86.2 us -> 86.1 us (level)
  no operation moved by 1% of the time
where the time goes in v16:
time: 86.1 us; the launch traced here: 85.5 us
  Pallas kernels  39.8 us (46%)
  blocking collectives  21.7 us (25%)
  starting transfers between devices  11 us (13%)
  waiting for transfers between devices  7.45 us (9%)
  local copies, waits for them, and re-layouts  4.32 us (5%)
    pallas_call x6, Pallas kernels, _call(): pl.pallas_call(kernel, out_shape=outs, in_specs=specs, out_specs=tuple(_v...  39.8 us
    all_to_all x2, blocking collectives, gather(): every = lax.all_to_all(copies, 'tm', 0, 0, tiled=True)  21.7 us
    all_to_all x2, starting transfers between devices, gather(): every = lax.all_to_all(copies, 'tm', 0, 0, tiled=True)  11 us
    all_to_all x2, waiting for transfers between devices, gather(): every = lax.all_to_all(copies, 'tm', 0, 0, tiled=True)  7.45 us
    reshape x4, local copies, waits for them, and re-layouts, gather(): return every.reshape(devices * scen_count, copies.shape[2])  2.62 us
  transfers between devices with their start and end apart: 2, of which 2 were waited for; matrix products, arithmetic and copies ran while one was open for 3% of the time, Pallas kernels for 5%

profile of v16, /device:TPU:0, one launch (start us, length us, event | category | flops | bytes accessed | tf_op | source)
XLA Modules:
  0.0 85.5 jit_solution(15348268929342573850)
XLA Ops:
  0.6 7.5 %shard_map.112 = (bf16[6,256,256]{2,1,0:T(8,128)(2,1)}, bf16[6,256,256]{2,1,0:T(8,128)(2,1)}, f32[256,256]{1,0:T(8,128)}, f32[256,256]{1,0:T(8,128)}, f32[16,4,256]{2,1,0:T(4,128)}) custom-call(f32[1,256]{1,0:T(1,128)} %bitcast.13, f32[3,64,64]{2,1,0:T(8,128)} %coupling_ref.1, s32[2,3]{1,0:T(2,128)} %bitcast.14, f32[256,256]{1,0:T(8,128)} %bitcast.9, ...), custom_call_target="tpu_custom_call" | custom-call | tf_op jit(solution)/shard_map/pallas_call | solution.py:198
  8.2 0.0 copy-start
  8.2 7.5 %all-to-all-start = ((f32[16,4,256]{2,1,0:T(4,128)}), f32[16,4,256]{2,1,0:T(4,128)S(1)}, u32[]{:S(2)}, u32[]{:S(2)}) async-start(f32[16,4,256]{2,1,0:T(4,128)} %get-tuple-element.18), calls=%async_computation | async-start | bytes 131072 | tf_op jit(solution)/shard_map/all_to_all | solution.py:325
  15.7 0.0 copy-done
  15.7 0.8 copy.14.imap_ref
  16.4 4.0 %shard_map.113 = (bf16[4,256,256]{2,1,0:T(8,128)(2,1)}, bf16[4,256,256]{2,1,0:T(8,128)(2,1)}) custom-call(f32[256,256]{1,0:T(8,128)} %get-tuple-element.21.top_ref), custom_call_target="tpu_custom_call" | custom-call | tf_op jit(solution)/shard_map/pallas_call | solution.py:198
  20.5 2.1 %all-to-all-done = f32[16,4,256]{2,1,0:T(4,128)S(1)} async-done(((f32[16,4,256]{2,1,0:T(4,128)}), f32[16,4,256]{2,1,0:T(4,128)S(1)}, u32[]{:S(2)}, u32[]{:S(2)}) %all-to-all-start) | async-done | bytes 65568 | tf_op jit(solution)/shard_map/all_to_all | solution.py:325
  22.6 0.6 reshape.36.c1_ref
  23.2 7.7 %shard_map.114 = (f32[256,256]{1,0:T(8,128)}, f32[16,4,256]{2,1,0:T(4,128)}) custom-call(f32[256,256]{1,0:T(8,128)} %get-tuple-element.17.w1_ref, s32[4,4]{1,0:T(4,128)} %len_ref.9, f32[64,256]{1,0:T(8,128)} %reshape.36.c1_ref, f32[4,256]{1,0:T(4,128)} %xi_ref.1, f32[64,256]{1,0:T(8,128)} %gain_ref.3, f32[256,64]{1,0:T(8,128)} %copy.14.imap_ref, ...), custom_call_target="tpu_custom_call" | custom-call | tf_op jit(solution)/shard_map/pallas_call | solution.py:198
  30.9 10.8 %all_to_all.20 = f32[16,4,256]{2,1,0:T(4,128)S(1)} all-to-all(f32[16,4,256]{2,1,0:T(4,128)} %get-tuple-element.25), channel_id=1, replica_groups=mesh['groups'=2,'tm'=16] {'tm'}, dimensions={0} | all-to-all | bytes 131072 | tf_op jit(solution)/shard_map/all_to_all | solution.py:325
  41.7 0.7 reshape.37.c2_ref
  42.4 7.4 %shard_map.115 = (f32[256,256]{1,0:T(8,128)}, f32[256,256]{1,0:T(8,128)}, f32[16,4,384]{2,1,0:T(4,128)}) custom-call(f32[256,256]{1,0:T(8,128)} %get-tuple-element.24.d2_ref, s32[4,4]{1,0:T(4,128)} %len_ref.9, f32[64,256]{1,0:T(8,128)} %reshape.37.c2_ref, f32[256,256]{1,0:T(8,128)} %bitcast.10, f32[256,256]{1,0:T(8,128)} %bitcast.7, ...), custom_call_target="tpu_custom_call" | custom-call | tf_op jit(solution)/shard_map/pallas_call | solution.py:198
  49.8 10.9 %all_to_all.21 = f32[16,4,384]{2,1,0:T(4,128)S(1)} all-to-all(f32[16,4,384]{2,1,0:T(4,128)} %get-tuple-element.28), channel_id=1, replica_groups=mesh['groups'=2,'tm'=16] {'tm'}, dimensions={0} | all-to-all | bytes 196608 | tf_op jit(solution)/shard_map/all_to_all | solution.py:325
  60.7 0.7 reshape.39.c3_ref
  61.4 7.7 %shard_map.116 = (f32[256,256]{1,0:T(8,128)}, f32[16,4,256]{2,1,0:T(4,128)}) custom-call(f32[256,256]{1,0:T(8,128)} %get-tuple-element.27.w3_ref, s32[4,4]{1,0:T(4,128)} %len_ref.9, f32[64,384]{1,0:T(8,128)} %reshape.39.c3_ref, f32[256,64]{1,0:T(8,128)} %copy.14.imap_ref, f32[64,256]{1,0:T(8,128)} %gain_ref.3, ...), custom_call_target="tpu_custom_call" | custom-call | tf_op jit(solution)/shard_map/pallas_call | solution.py:198
  69.0 3.5 %all-to-all-start.3 = ((f32[16,4,256]{2,1,0:T(4,128)}), f32[16,4,256]{2,1,0:T(4,128)S(1)}, u32[]{:S(2)}, u32[]{:S(2)}) async-start(f32[16,4,256]{2,1,0:T(4,128)} %get-tuple-element.30), calls=%async_computation.3 | async-start | bytes 131072 | tf_op jit(solution)/shard_map/all_to_all | solution.py:325
  72.5 0.9 %slice_reduce_fusion = f32[64]{0:T(128)S(1)} fusion(f32[64,384]{1,0:T(8,128)} %reshape.39.c3_ref), kind=kLoop, calls=%fused_computation | loop fusion | bytes 512 | tf_op jit(solution)/shard_map/slice | solution.py:343
  73.4 0.1 reshape_squeeze.3
  73.5 0.6 reduce_sum.9
  74.0 5.4 %all-to-all-done.3 = f32[16,4,256]{2,1,0:T(4,128)S(1)} async-done(((f32[16,4,256]{2,1,0:T(4,128)}), f32[16,4,256]{2,1,0:T(4,128)S(1)}, u32[]{:S(2)}, u32[]{:S(2)}) %all-to-all-start.3) | async-done | bytes 65568 | tf_op jit(solution)/shard_map/all_to_all | solution.py:325
  79.4 0.6 reshape.40.c4_ref
  80.0 5.4 %shard_map.117 = f32[256,256]{1,0:T(8,128)} custom-call(f32[256,256]{1,0:T(8,128)} %get-tuple-element.29.s4_ref, s32[4,4]{1,0:T(4,128)} %len_ref.9, f32[64,256]{1,0:T(8,128)} %reshape.40.c4_ref, f32[256,256]{1,0:T(8,128)} %get-tuple-element.26.x_ref, f32[256,256]{1,0:T(8,128)} %bitcast.8, bf16[6,256,256]{2,1,0:T(8,128)(2,1)} %get-tuple-element.19.phi_ref, ...), custom_call_target="tpu_custom_call" | custom-call | tf_op jit(solution)/shard_map/pallas_call | solution.py:198
Async XLA Ops:
  8.2 7.5 %copy-start = (f32[256,64]{0,1:T(8,128)S(1)}, f32[256,64]{0,1:T(8,128)}, u32[]{:S(2)}) copy-start(f32[256,64]{0,1:T(8,128)} %param.15) | copy-start | bytes 196612
  8.2 14.4 %all-to-all-start = ((f32[16,4,256]{2,1,0:T(4,128)}), f32[16,4,256]{2,1,0:T(4,128)S(1)}, u32[]{:S(2)}, u32[]{:S(2)}) async-start(f32[16,4,256]{2,1,0:T(4,128)} %get-tuple-element.18), calls=%async_computation | async-start | bytes 131072 | tf_op jit(solution)/shard_map/all_to_all | solution.py:325
  69.0 10.4 %all-to-all-start.3 = ((f32[16,4,256]{2,1,0:T(4,128)}), f32[16,4,256]{2,1,0:T(4,128)S(1)}, u32[]{:S(2)}, u32[]{:S(2)}) async-start(f32[16,4,256]{2,1,0:T(4,128)} %get-tuple-element.30), calls=%async_computation.3 | async-start | bytes 131072 | tf_op jit(solution)/shard_map/all_to_all | solution.py:325

commit v17 on v15

--- a/solution.py
+++ b/solution.py
@@ -145,9 +145,7 @@
 def _ends(v, seg, backward, out_rows):
     rows, width = v.shape
     scen = rows // seg
-    pick = lax.broadcasted_iota(jnp.int32, (scen, rows), 1)
-    want = lax.broadcasted_iota(jnp.int32, (scen, rows), 0) * seg + (0 if backward else seg - 1)
-    ends = _dot((pick == want).astype(jnp.float32), v)
+    ends = v.reshape(scen, seg, width)[:, 0 if backward else seg - 1, :]
     return jnp.broadcast_to(ends[None], (out_rows,) + ends.shape)
 
 

time: 86.2 us -> 84.8 us (0.984)
  Pallas kernels: 39.7 us -> 38.5 us
    pallas_call x6, Pallas kernels: 39.7 us -> 38.5 us  [_call(): pl.pallas_call(kernel, out_shape=outs, in_specs=specs, out_specs=tuple(_v...]
where the time goes in v17:
time: 84.8 us; the launch traced here: 84.2 us
  Pallas kernels  38.5 us (45%)
  blocking collectives  21.7 us (26%)
  starting transfers between devices  11 us (13%)
  waiting for transfers between devices  7.45 us (9%)
  local copies, waits for them, and re-layouts  4.32 us (5%)
    pallas_call x6, Pallas kernels, _call(): pl.pallas_call(kernel, out_shape=outs, in_specs=specs, out_specs=tuple(_v...  38.5 us
    all_to_all x2, blocking collectives, gather(): every = lax.all_to_all(copies, 'tm', 0, 0, tiled=True)  21.7 us
    all_to_all x2, starting transfers between devices, gather(): every = lax.all_to_all(copies, 'tm', 0, 0, tiled=True)  11 us
    all_to_all x2, waiting for transfers between devices, gather(): every = lax.all_to_all(copies, 'tm', 0, 0, tiled=True)  7.45 us
    reshape x4, local copies, waits for them, and re-layouts, gather(): return every.reshape(devices * scen_count, copies.shape[2])  2.62 us
  transfers between devices with their start and end apart: 2, of which 2 were waited for; matrix products, arithmetic and copies ran while one was open for 3% of the time, Pallas kernels for 5%

profile of v17, /device:TPU:0, one launch (start us, length us, event | category | flops | bytes accessed | tf_op | source)
XLA Modules:
  0.0 84.2 jit_solution(16846504263462042895)
XLA Ops:
  0.6 7.1 %shard_map.112 = (bf16[6,256,256]{2,1,0:T(8,128)(2,1)}, bf16[6,256,256]{2,1,0:T(8,128)(2,1)}, f32[256,256]{1,0:T(8,128)}, f32[256,256]{1,0:T(8,128)}, f32[16,4,256]{2,1,0:T(4,128)}) custom-call(f32[1,256]{1,0:T(1,128)} %bitcast.13, f32[3,64,64]{2,1,0:T(8,128)} %coupling_ref.1, s32[2,3]{1,0:T(2,128)} %bitcast.14, f32[256,256]{1,0:T(8,128)} %bitcast.9, ...), custom_call_target="tpu_custom_call" | custom-call | tf_op jit(solution)/shard_map/pallas_call | solution.py:196
  7.7 0.0 copy-start
  7.7 7.5 %all-to-all-start = ((f32[16,4,256]{2,1,0:T(4,128)}), f32[16,4,256]{2,1,0:T(4,128)S(1)}, u32[]{:S(2)}, u32[]{:S(2)}) async-start(f32[16,4,256]{2,1,0:T(4,128)} %get-tuple-element.18), calls=%async_computation | async-start | bytes 131072 | tf_op jit(solution)/shard_map/all_to_all | solution.py:312
  15.2 0.0 copy-done
  15.2 0.8 copy.14.imap_ref
  16.0 4.0 %shard_map.113 = (bf16[4,256,256]{2,1,0:T(8,128)(2,1)}, bf16[4,256,256]{2,1,0:T(8,128)(2,1)}) custom-call(f32[256,256]{1,0:T(8,128)} %get-tuple-element.21.top_ref), custom_call_target="tpu_custom_call" | custom-call | tf_op jit(solution)/shard_map/pallas_call | solution.py:196
  20.0 2.1 %all-to-all-done = f32[16,4,256]{2,1,0:T(4,128)S(1)} async-done(((f32[16,4,256]{2,1,0:T(4,128)}), f32[16,4,256]{2,1,0:T(4,128)S(1)}, u32[]{:S(2)}, u32[]{:S(2)}) %all-to-all-start) | async-done | bytes 65568 | tf_op jit(solution)/shard_map/all_to_all | solution.py:312
  22.1 0.6 reshape.36.c1_ref
  22.8 7.5 %shard_map.114 = (f32[256,256]{1,0:T(8,128)}, f32[16,4,256]{2,1,0:T(4,128)}) custom-call(f32[256,256]{1,0:T(8,128)} %get-tuple-element.17.w1_ref, s32[4,4]{1,0:T(4,128)} %len_ref.9, f32[64,256]{1,0:T(8,128)} %reshape.36.c1_ref, f32[4,256]{1,0:T(4,128)} %xi_ref.1, f32[64,256]{1,0:T(8,128)} %gain_ref.3, f32[256,64]{1,0:T(8,128)} %copy.14.imap_ref, ...), custom_call_target="tpu_custom_call" | custom-call | tf_op jit(solution)/shard_map/pallas_call | solution.py:196
  30.2 10.8 %all_to_all.20 = f32[16,4,256]{2,1,0:T(4,128)S(1)} all-to-all(f32[16,4,256]{2,1,0:T(4,128)} %get-tuple-element.25), channel_id=1, replica_groups=mesh['groups'=2,'tm'=16] {'tm'}, dimensions={0} | all-to-all | bytes 131072 | tf_op jit(solution)/shard_map/all_to_all | solution.py:312
  41.0 0.7 reshape.37.c2_ref
  41.7 7.1 %shard_map.115 = (f32[256,256]{1,0:T(8,128)}, f32[256,256]{1,0:T(8,128)}, f32[16,4,384]{2,1,0:T(4,128)}) custom-call(f32[256,256]{1,0:T(8,128)} %get-tuple-element.24.d2_ref, s32[4,4]{1,0:T(4,128)} %len_ref.9, f32[64,256]{1,0:T(8,128)} %reshape.37.c2_ref, f32[256,256]{1,0:T(8,128)} %bitcast.10, f32[256,256]{1,0:T(8,128)} %bitcast.7, ...), custom_call_target="tpu_custom_call" | custom-call | tf_op jit(solution)/shard_map/pallas_call | solution.py:196
  48.8 10.9 %all_to_all.21 = f32[16,4,384]{2,1,0:T(4,128)S(1)} all-to-all(f32[16,4,384]{2,1,0:T(4,128)} %get-tuple-element.28), channel_id=1, replica_groups=mesh['groups'=2,'tm'=16] {'tm'}, dimensions={0} | all-to-all | bytes 196608 | tf_op jit(solution)/shard_map/all_to_all | solution.py:312
  59.7 0.7 reshape.39.c3_ref
  60.4 7.4 %shard_map.116 = (f32[256,256]{1,0:T(8,128)}, f32[16,4,256]{2,1,0:T(4,128)}) custom-call(f32[256,256]{1,0:T(8,128)} %get-tuple-element.27.w3_ref, s32[4,4]{1,0:T(4,128)} %len_ref.9, f32[64,384]{1,0:T(8,128)} %reshape.39.c3_ref, f32[256,64]{1,0:T(8,128)} %copy.14.imap_ref, f32[64,256]{1,0:T(8,128)} %gain_ref.3, ...), custom_call_target="tpu_custom_call" | custom-call | tf_op jit(solution)/shard_map/pallas_call | solution.py:196
  67.8 3.5 %all-to-all-start.3 = ((f32[16,4,256]{2,1,0:T(4,128)}), f32[16,4,256]{2,1,0:T(4,128)S(1)}, u32[]{:S(2)}, u32[]{:S(2)}) async-start(f32[16,4,256]{2,1,0:T(4,128)} %get-tuple-element.30), calls=%async_computation.3 | async-start | bytes 131072 | tf_op jit(solution)/shard_map/all_to_all | solution.py:312
  71.3 0.9 %slice_reduce_fusion = f32[64]{0:T(128)S(1)} fusion(f32[64,384]{1,0:T(8,128)} %reshape.39.c3_ref), kind=kLoop, calls=%fused_computation | loop fusion | bytes 512 | tf_op jit(solution)/shard_map/slice | solution.py:330
  72.1 0.1 reshape_squeeze.3
  72.2 0.6 reduce_sum.9
  72.8 5.4 %all-to-all-done.3 = f32[16,4,256]{2,1,0:T(4,128)S(1)} async-done(((f32[16,4,256]{2,1,0:T(4,128)}), f32[16,4,256]{2,1,0:T(4,128)S(1)}, u32[]{:S(2)}, u32[]{:S(2)}) %all-to-all-start.3) | async-done | bytes 65568 | tf_op jit(solution)/shard_map/all_to_all | solution.py:312
  78.1 0.6 reshape.40.c4_ref
  78.8 5.4 %shard_map.117 = f32[256,256]{1,0:T(8,128)} custom-call(f32[256,256]{1,0:T(8,128)} %get-tuple-element.29.s4_ref, s32[4,4]{1,0:T(4,128)} %len_ref.9, f32[64,256]{1,0:T(8,128)} %reshape.40.c4_ref, f32[256,256]{1,0:T(8,128)} %get-tuple-element.26.x_ref, f32[256,256]{1,0:T(8,128)} %bitcast.8, bf16[6,256,256]{2,1,0:T(8,128)(2,1)} %get-tuple-element.19.phi_ref, ...), custom_call_target="tpu_custom_call" | custom-call | tf_op jit(solution)/shard_map/pallas_call | solution.py:196
Async XLA Ops:
  7.7 7.5 %copy-start = (f32[256,64]{0,1:T(8,128)S(1)}, f32[256,64]{0,1:T(8,128)}, u32[]{:S(2)}) copy-start(f32[256,64]{0,1:T(8,128)} %param.15) | copy-start | bytes 196612
  7.7 14.4 %all-to-all-start = ((f32[16,4,256]{2,1,0:T(4,128)}), f32[16,4,256]{2,1,0:T(4,128)S(1)}, u32[]{:S(2)}, u32[]{:S(2)}) async-start(f32[16,4,256]{2,1,0:T(4,128)} %get-tuple-element.18), calls=%async_computation | async-start | bytes 131072 | tf_op jit(solution)/shard_map/all_to_all | solution.py:312
  67.8 10.4 %all-to-all-start.3 = ((f32[16,4,256]{2,1,0:T(4,128)}), f32[16,4,256]{2,1,0:T(4,128)S(1)}, u32[]{:S(2)}, u32[]{:S(2)}) async-start(f32[16,4,256]{2,1,0:T(4,128)} %get-tuple-element.30), calls=%async_computation.3 | async-start | bytes 131072 | tf_op jit(solution)/shard_map/all_to_all | solution.py:312

commit v18 on v17

--- a/solution.py
+++ b/solution.py
@@ -259,10 +259,8 @@
     w3_ref[...] = w3
     per_row = jnp.sum(w3 * offset, axis=1, keepdims=True)
     copies = e3_ref.shape[0]
-    pick = lax.broadcasted_iota(jnp.int32, (scen, rows), 1) // seg
-    want = lax.broadcasted_iota(jnp.int32, (scen, rows), 0)
-    sel = (pick == want).astype(jnp.float32)
-    per_scen = _dot(sel, jnp.broadcast_to(per_row, (rows, 128))) * scale
+    per_scen = jnp.sum(per_row.reshape(scen, seg, 1), axis=1) * scale
+    per_scen = jnp.broadcast_to(per_scen, (scen, 128))
     e3_ref[:, :, width:] = jnp.broadcast_to(per_scen[None], (copies, scen, 128))
     e3_ref[:, :, :width] = _ends(_scan(w3, cut_e, pwb_ref, seg, True), seg, True, copies)
 

time: 84.8 us -> 84.6 us (level)
  no operation moved by 1% of the time
where the time goes in v18:
time: 84.6 us; the launch traced here: 84 us
  Pallas kernels  38.4 us (45%)
  blocking collectives  21.7 us (26%)
  starting transfers between devices  11 us (13%)
  waiting for transfers between devices  7.45 us (9%)
  local copies, waits for them, and re-layouts  4.32 us (5%)
    pallas_call x6, Pallas kernels, _call(): pl.pallas_call(kernel, out_shape=outs, in_specs=specs, out_specs=tuple(_v...  38.4 us
    all_to_all x2, blocking collectives, gather(): every = lax.all_to_all(copies, 'tm', 0, 0, tiled=True)  21.7 us
    all_to_all x2, starting transfers between devices, gather(): every = lax.all_to_all(copies, 'tm', 0, 0, tiled=True)  11 us
    all_to_all x2, waiting for transfers between devices, gather(): every = lax.all_to_all(copies, 'tm', 0, 0, tiled=True)  7.45 us
    reshape x4, local copies, waits for them, and re-layouts, gather(): return every.reshape(devices * scen_count, copies.shape[2])  2.62 us
  transfers between devices with their start and end apart: 2, of which 2 were waited for; matrix products, arithmetic and copies ran while one was open for 3% of the time, Pallas kernels for 5%

profile of v18, /device:TPU:0, one launch (start us, length us, event | category | flops | bytes accessed | tf_op | source)
XLA Modules:
  0.0 84.0 jit_solution(10614939518965832469)
XLA Ops:
  0.6 7.1 %shard_map.112 = (bf16[6,256,256]{2,1,0:T(8,128)(2,1)}, bf16[6,256,256]{2,1,0:T(8,128)(2,1)}, f32[256,256]{1,0:T(8,128)}, f32[256,256]{1,0:T(8,128)}, f32[16,4,256]{2,1,0:T(4,128)}) custom-call(f32[1,256]{1,0:T(1,128)} %bitcast.13, f32[3,64,64]{2,1,0:T(8,128)} %coupling_ref.1, s32[2,3]{1,0:T(2,128)} %bitcast.14, f32[256,256]{1,0:T(8,128)} %bitcast.9, ...), custom_call_target="tpu_custom_call" | custom-call | tf_op jit(solution)/shard_map/pallas_call | solution.py:196
  7.7 0.0 copy-start
  7.7 7.5 %all-to-all-start = ((f32[16,4,256]{2,1,0:T(4,128)}), f32[16,4,256]{2,1,0:T(4,128)S(1)}, u32[]{:S(2)}, u32[]{:S(2)}) async-start(f32[16,4,256]{2,1,0:T(4,128)} %get-tuple-element.18), calls=%async_computation | async-start | bytes 131072 | tf_op jit(solution)/shard_map/all_to_all | solution.py:310
  15.2 0.0 copy-done
  15.2 0.8 copy.14.imap_ref
  16.0 4.0 %shard_map.113 = (bf16[4,256,256]{2,1,0:T(8,128)(2,1)}, bf16[4,256,256]{2,1,0:T(8,128)(2,1)}) custom-call(f32[256,256]{1,0:T(8,128)} %get-tuple-element.21.top_ref), custom_call_target="tpu_custom_call" | custom-call | tf_op jit(solution)/shard_map/pallas_call | solution.py:196
  20.0 2.1 %all-to-all-done = f32[16,4,256]{2,1,0:T(4,128)S(1)} async-done(((f32[16,4,256]{2,1,0:T(4,128)}), f32[16,4,256]{2,1,0:T(4,128)S(1)}, u32[]{:S(2)}, u32[]{:S(2)}) %all-to-all-start) | async-done | bytes 65568 | tf_op jit(solution)/shard_map/all_to_all | solution.py:310
  22.1 0.6 reshape.36.c1_ref
  22.8 7.5 %shard_map.114 = (f32[256,256]{1,0:T(8,128)}, f32[16,4,256]{2,1,0:T(4,128)}) custom-call(f32[256,256]{1,0:T(8,128)} %get-tuple-element.17.w1_ref, s32[4,4]{1,0:T(4,128)} %len_ref.9, f32[64,256]{1,0:T(8,128)} %reshape.36.c1_ref, f32[4,256]{1,0:T(4,128)} %xi_ref.1, f32[64,256]{1,0:T(8,128)} %gain_ref.3, f32[256,64]{1,0:T(8,128)} %copy.14.imap_ref, ...), custom_call_target="tpu_custom_call" | custom-call | tf_op jit(solution)/shard_map/pallas_call | solution.py:196
  30.2 10.8 %all_to_all.20 = f32[16,4,256]{2,1,0:T(4,128)S(1)} all-to-all(f32[16,4,256]{2,1,0:T(4,128)} %get-tuple-element.25), channel_id=1, replica_groups=mesh['groups'=2,'tm'=16] {'tm'}, dimensions={0} | all-to-all | bytes 131072 | tf_op jit(solution)/shard_map/all_to_all | solution.py:310
  41.0 0.7 reshape.37.c2_ref
  41.7 6.9 %shard_map.115 = (f32[256,256]{1,0:T(8,128)}, f32[256,256]{1,0:T(8,128)}, f32[16,4,384]{2,1,0:T(4,128)}) custom-call(f32[256,256]{1,0:T(8,128)} %get-tuple-element.24.d2_ref, s32[4,4]{1,0:T(4,128)} %len_ref.9, f32[64,256]{1,0:T(8,128)} %reshape.37.c2_ref, f32[256,256]{1,0:T(8,128)} %bitcast.10, f32[256,256]{1,0:T(8,128)} %bitcast.7, ...), custom_call_target="tpu_custom_call" | custom-call | tf_op jit(solution)/shard_map/pallas_call | solution.py:196
  48.7 10.9 %all_to_all.21 = f32[16,4,384]{2,1,0:T(4,128)S(1)} all-to-all(f32[16,4,384]{2,1,0:T(4,128)} %get-tuple-element.28), channel_id=1, replica_groups=mesh['groups'=2,'tm'=16] {'tm'}, dimensions={0} | all-to-all | bytes 196608 | tf_op jit(solution)/shard_map/all_to_all | solution.py:310
  59.5 0.7 reshape.39.c3_ref
  60.2 7.4 %shard_map.116 = (f32[256,256]{1,0:T(8,128)}, f32[16,4,256]{2,1,0:T(4,128)}) custom-call(f32[256,256]{1,0:T(8,128)} %get-tuple-element.27.w3_ref, s32[4,4]{1,0:T(4,128)} %len_ref.9, f32[64,384]{1,0:T(8,128)} %reshape.39.c3_ref, f32[256,64]{1,0:T(8,128)} %copy.14.imap_ref, f32[64,256]{1,0:T(8,128)} %gain_ref.3, ...), custom_call_target="tpu_custom_call" | custom-call | tf_op jit(solution)/shard_map/pallas_call | solution.py:196
  67.6 3.5 %all-to-all-start.3 = ((f32[16,4,256]{2,1,0:T(4,128)}), f32[16,4,256]{2,1,0:T(4,128)S(1)}, u32[]{:S(2)}, u32[]{:S(2)}) async-start(f32[16,4,256]{2,1,0:T(4,128)} %get-tuple-element.30), calls=%async_computation.3 | async-start | bytes 131072 | tf_op jit(solution)/shard_map/all_to_all | solution.py:310
  71.1 0.9 %slice_reduce_fusion = f32[64]{0:T(128)S(1)} fusion(f32[64,384]{1,0:T(8,128)} %reshape.39.c3_ref), kind=kLoop, calls=%fused_computation | loop fusion | bytes 512 | tf_op jit(solution)/shard_map/slice | solution.py:328
  71.9 0.1 reshape_squeeze.3
  72.0 0.6 reduce_sum.9
  72.6 5.4 %all-to-all-done.3 = f32[16,4,256]{2,1,0:T(4,128)S(1)} async-done(((f32[16,4,256]{2,1,0:T(4,128)}), f32[16,4,256]{2,1,0:T(4,128)S(1)}, u32[]{:S(2)}, u32[]{:S(2)}) %all-to-all-start.3) | async-done | bytes 65568 | tf_op jit(solution)/shard_map/all_to_all | solution.py:310
  77.9 0.6 reshape.40.c4_ref
  78.6 5.4 %shard_map.117 = f32[256,256]{1,0:T(8,128)} custom-call(f32[256,256]{1,0:T(8,128)} %get-tuple-element.29.s4_ref, s32[4,4]{1,0:T(4,128)} %len_ref.9, f32[64,256]{1,0:T(8,128)} %reshape.40.c4_ref, f32[256,256]{1,0:T(8,128)} %get-tuple-element.26.x_ref, f32[256,256]{1,0:T(8,128)} %bitcast.8, bf16[6,256,256]{2,1,0:T(8,128)(2,1)} %get-tuple-element.19.phi_ref, ...), custom_call_target="tpu_custom_call" | custom-call | tf_op jit(solution)/shard_map/pallas_call | solution.py:196
Async XLA Ops:
  7.7 7.5 %copy-start = (f32[256,64]{0,1:T(8,128)S(1)}, f32[256,64]{0,1:T(8,128)}, u32[]{:S(2)}) copy-start(f32[256,64]{0,1:T(8,128)} %param.15) | copy-start | bytes 196612
  7.7 14.4 %all-to-all-start = ((f32[16,4,256]{2,1,0:T(4,128)}), f32[16,4,256]{2,1,0:T(4,128)S(1)}, u32[]{:S(2)}, u32[]{:S(2)}) async-start(f32[16,4,256]{2,1,0:T(4,128)} %get-tuple-element.18), calls=%async_computation | async-start | bytes 131072 | tf_op jit(solution)/shard_map/all_to_all | solution.py:310
  67.6 10.4 %all-to-all-start.3 = ((f32[16,4,256]{2,1,0:T(4,128)}), f32[16,4,256]{2,1,0:T(4,128)S(1)}, u32[]{:S(2)}, u32[]{:S(2)}) async-start(f32[16,4,256]{2,1,0:T(4,128)} %get-tuple-element.30), calls=%async_computation.3 | async-start | bytes 131072 | tf_op jit(solution)/shard_map/all_to_all | solution.py:310

commit v19 on v18

--- a/solution.py
+++ b/solution.py
@@ -137,9 +137,14 @@
         flags = flags * prior_f
     me = lax.axis_index("tm")
     target = me + 1 if backward else me - 1
-    pick = lax.broadcasted_iota(jnp.int32, (scen, rows), 1)
-    want = lax.broadcasted_iota(jnp.int32, (scen, rows), 0) + target * scen
-    return _dot((pick == want).astype(jnp.float32), g)
+    if devices & (devices - 1):
+        pick = lax.broadcasted_iota(jnp.int32, (scen, rows), 1)
+        want = lax.broadcasted_iota(jnp.int32, (scen, rows), 0) + target * scen
+        return _dot((pick == want).astype(jnp.float32), g)
+    picked = jnp.where(r // scen == target, g, 0.0)
+    for level in range((devices - 1).bit_length()):
+        picked = picked + pltpu.roll(picked, scen * 2**level, 0)
+    return picked[:scen]
 
 
 def _ends(v, seg, backward, out_rows):

time: 84.6 us -> 84 us (level)
  no operation moved by 1% of the time
where the time goes in v19:
time: 84 us; the launch traced here: 83.4 us
  Pallas kernels  37.7 us (45%)
  blocking collectives  21.7 us (26%)
  starting transfers between devices  11 us (13%)
  waiting for transfers between devices  7.45 us (9%)
  local copies, waits for them, and re-layouts  4.32 us (5%)
    pallas_call x6, Pallas kernels, _call(): pl.pallas_call(kernel, out_shape=outs, in_specs=specs, out_specs=tuple(_v...  37.7 us
    all_to_all x2, blocking collectives, gather(): every = lax.all_to_all(copies, 'tm', 0, 0, tiled=True)  21.7 us
    all_to_all x2, starting transfers between devices, gather(): every = lax.all_to_all(copies, 'tm', 0, 0, tiled=True)  11 us
    all_to_all x2, waiting for transfers between devices, gather(): every = lax.all_to_all(copies, 'tm', 0, 0, tiled=True)  7.45 us
    reshape x4, local copies, waits for them, and re-layouts, gather(): return every.reshape(devices * scen_count, copies.shape[2])  2.62 us
  transfers between devices with their start and end apart: 2, of which 2 were waited for; matrix products, arithmetic and copies ran while one was open for 3% of the time, Pallas kernels for 5%

profile of v19, /device:TPU:0, one launch (start us, length us, event | category | flops | bytes accessed | tf_op | source)
XLA Modules:
  0.0 83.4 jit_solution(12187276385090243589)
XLA Ops:
  0.6 7.1 %shard_map.112 = (bf16[6,256,256]{2,1,0:T(8,128)(2,1)}, bf16[6,256,256]{2,1,0:T(8,128)(2,1)}, f32[256,256]{1,0:T(8,128)}, f32[256,256]{1,0:T(8,128)}, f32[16,4,256]{2,1,0:T(4,128)}) custom-call(f32[1,256]{1,0:T(1,128)} %bitcast.13, f32[3,64,64]{2,1,0:T(8,128)} %coupling_ref.1, s32[2,3]{1,0:T(2,128)} %bitcast.14, f32[256,256]{1,0:T(8,128)} %bitcast.9, ...), custom_call_target="tpu_custom_call" | custom-call | tf_op jit(solution)/shard_map/pallas_call | solution.py:201
  7.7 0.0 copy-start
  7.7 7.5 %all-to-all-start = ((f32[16,4,256]{2,1,0:T(4,128)}), f32[16,4,256]{2,1,0:T(4,128)S(1)}, u32[]{:S(2)}, u32[]{:S(2)}) async-start(f32[16,4,256]{2,1,0:T(4,128)} %get-tuple-element.18), calls=%async_computation | async-start | bytes 131072 | tf_op jit(solution)/shard_map/all_to_all | solution.py:315
  15.2 0.0 copy-done
  15.2 0.8 copy.14.imap_ref
  16.0 4.0 %shard_map.113 = (bf16[4,256,256]{2,1,0:T(8,128)(2,1)}, bf16[4,256,256]{2,1,0:T(8,128)(2,1)}) custom-call(f32[256,256]{1,0:T(8,128)} %get-tuple-element.21.top_ref), custom_call_target="tpu_custom_call" | custom-call | tf_op jit(solution)/shard_map/pallas_call | solution.py:201
  20.0 2.1 %all-to-all-done = f32[16,4,256]{2,1,0:T(4,128)S(1)} async-done(((f32[16,4,256]{2,1,0:T(4,128)}), f32[16,4,256]{2,1,0:T(4,128)S(1)}, u32[]{:S(2)}, u32[]{:S(2)}) %all-to-all-start) | async-done | bytes 65568 | tf_op jit(solution)/shard_map/all_to_all | solution.py:315
  22.1 0.6 reshape.36.c1_ref
  22.8 7.3 %shard_map.114 = (f32[256,256]{1,0:T(8,128)}, f32[16,4,256]{2,1,0:T(4,128)}) custom-call(f32[256,256]{1,0:T(8,128)} %get-tuple-element.17.w1_ref, s32[4,4]{1,0:T(4,128)} %len_ref.9, f32[64,256]{1,0:T(8,128)} %reshape.36.c1_ref, f32[4,256]{1,0:T(4,128)} %xi_ref.1, f32[64,256]{1,0:T(8,128)} %gain_ref.3, f32[256,64]{1,0:T(8,128)} %copy.14.imap_ref, ...), custom_call_target="tpu_custom_call" | custom-call | tf_op jit(solution)/shard_map/pallas_call | solution.py:201
  30.1 10.8 %all_to_all.20 = f32[16,4,256]{2,1,0:T(4,128)S(1)} all-to-all(f32[16,4,256]{2,1,0:T(4,128)} %get-tuple-element.25), channel_id=1, replica_groups=mesh['groups'=2,'tm'=16] {'tm'}, dimensions={0} | all-to-all | bytes 131072 | tf_op jit(solution)/shard_map/all_to_all | solution.py:315
  40.9 0.7 reshape.37.c2_ref
  41.5 6.8 %shard_map.115 = (f32[256,256]{1,0:T(8,128)}, f32[256,256]{1,0:T(8,128)}, f32[16,4,384]{2,1,0:T(4,128)}) custom-call(f32[256,256]{1,0:T(8,128)} %get-tuple-element.24.d2_ref, s32[4,4]{1,0:T(4,128)} %len_ref.9, f32[64,256]{1,0:T(8,128)} %reshape.37.c2_ref, f32[256,256]{1,0:T(8,128)} %bitcast.10, f32[256,256]{1,0:T(8,128)} %bitcast.7, ...), custom_call_target="tpu_custom_call" | custom-call | tf_op jit(solution)/shard_map/pallas_call | solution.py:201
  48.3 10.9 %all_to_all.21 = f32[16,4,384]{2,1,0:T(4,128)S(1)} all-to-all(f32[16,4,384]{2,1,0:T(4,128)} %get-tuple-element.28), channel_id=1, replica_groups=mesh['groups'=2,'tm'=16] {'tm'}, dimensions={0} | all-to-all | bytes 196608 | tf_op jit(solution)/shard_map/all_to_all | solution.py:315
  59.2 0.7 reshape.39.c3_ref
  59.9 7.2 %shard_map.116 = (f32[256,256]{1,0:T(8,128)}, f32[16,4,256]{2,1,0:T(4,128)}) custom-call(f32[256,256]{1,0:T(8,128)} %get-tuple-element.27.w3_ref, s32[4,4]{1,0:T(4,128)} %len_ref.9, f32[64,384]{1,0:T(8,128)} %reshape.39.c3_ref, f32[256,64]{1,0:T(8,128)} %copy.14.imap_ref, f32[64,256]{1,0:T(8,128)} %gain_ref.3, ...), custom_call_target="tpu_custom_call" | custom-call | tf_op jit(solution)/shard_map/pallas_call | solution.py:201
  67.1 3.5 %all-to-all-start.3 = ((f32[16,4,256]{2,1,0:T(4,128)}), f32[16,4,256]{2,1,0:T(4,128)S(1)}, u32[]{:S(2)}, u32[]{:S(2)}) async-start(f32[16,4,256]{2,1,0:T(4,128)} %get-tuple-element.30), calls=%async_computation.3 | async-start | bytes 131072 | tf_op jit(solution)/shard_map/all_to_all | solution.py:315
  70.6 0.9 %slice_reduce_fusion = f32[64]{0:T(128)S(1)} fusion(f32[64,384]{1,0:T(8,128)} %reshape.39.c3_ref), kind=kLoop, calls=%fused_computation | loop fusion | bytes 512 | tf_op jit(solution)/shard_map/slice | solution.py:333
  71.5 0.1 reshape_squeeze.3
  71.5 0.6 reduce_sum.9
  72.1 5.4 %all-to-all-done.3 = f32[16,4,256]{2,1,0:T(4,128)S(1)} async-done(((f32[16,4,256]{2,1,0:T(4,128)}), f32[16,4,256]{2,1,0:T(4,128)S(1)}, u32[]{:S(2)}, u32[]{:S(2)}) %all-to-all-start.3) | async-done | bytes 65568 | tf_op jit(solution)/shard_map/all_to_all | solution.py:315
  77.4 0.6 reshape.40.c4_ref
  78.1 5.3 %shard_map.117 = f32[256,256]{1,0:T(8,128)} custom-call(f32[256,256]{1,0:T(8,128)} %get-tuple-element.29.s4_ref, s32[4,4]{1,0:T(4,128)} %len_ref.9, f32[64,256]{1,0:T(8,128)} %reshape.40.c4_ref, f32[256,256]{1,0:T(8,128)} %get-tuple-element.26.x_ref, f32[256,256]{1,0:T(8,128)} %bitcast.8, bf16[6,256,256]{2,1,0:T(8,128)(2,1)} %get-tuple-element.19.phi_ref, ...), custom_call_target="tpu_custom_call" | custom-call | tf_op jit(solution)/shard_map/pallas_call | solution.py:201
Async XLA Ops:
  7.7 7.5 %copy-start = (f32[256,64]{0,1:T(8,128)S(1)}, f32[256,64]{0,1:T(8,128)}, u32[]{:S(2)}) copy-start(f32[256,64]{0,1:T(8,128)} %param.15) | copy-start | bytes 196612
  7.7 14.4 %all-to-all-start = ((f32[16,4,256]{2,1,0:T(4,128)}), f32[16,4,256]{2,1,0:T(4,128)S(1)}, u32[]{:S(2)}, u32[]{:S(2)}) async-start(f32[16,4,256]{2,1,0:T(4,128)} %get-tuple-element.18), calls=%async_computation | async-start | bytes 131072 | tf_op jit(solution)/shard_map/all_to_all | solution.py:315
  67.1 10.4 %all-to-all-start.3 = ((f32[16,4,256]{2,1,0:T(4,128)}), f32[16,4,256]{2,1,0:T(4,128)S(1)}, u32[]{:S(2)}, u32[]{:S(2)}) async-start(f32[16,4,256]{2,1,0:T(4,128)} %get-tuple-element.30), calls=%async_computation.3 | async-start | bytes 131072 | tf_op jit(solution)/shard_map/all_to_all | solution.py:315

commit v20 on v19

--- a/solution.py
+++ b/solution.py
@@ -113,10 +113,15 @@
     return v
 
 
-def _carry(g_ref, len_ref, pw_ref, scen, backward, seg):
+def _block(scen):
+    return -(-scen // 8) * 8
+
+
+def _carry(g_ref, len_ref, pw_ref, real, backward, seg):
     width = pw_ref.shape[1]
     g = g_ref[...][:, :width]
     rows = g.shape[0]
+    scen = _block(real)
     devices = rows // scen
     r = lax.broadcasted_iota(jnp.int32, (rows, width), 0)
     flags = jnp.broadcast_to(_seg_flags(len_ref, devices, seg, not backward), (rows, width))
@@ -140,18 +145,25 @@
     if devices & (devices - 1):
         pick = lax.broadcasted_iota(jnp.int32, (scen, rows), 1)
         want = lax.broadcasted_iota(jnp.int32, (scen, rows), 0) + target * scen
-        return _dot((pick == want).astype(jnp.float32), g)
+        return _dot((pick == want).astype(jnp.float32), g)[:real]
     picked = jnp.where(r // scen == target, g, 0.0)
     for level in range((devices - 1).bit_length()):
         picked = picked + pltpu.roll(picked, scen * 2**level, 0)
-    return picked[:scen]
+    return picked[:real]
 
 
 def _ends(v, seg, backward, out_rows):
     rows, width = v.shape
     scen = rows // seg
-    ends = v.reshape(scen, seg, width)[:, 0 if backward else seg - 1, :]
+    ends = _pad(v.reshape(scen, seg, width)[:, 0 if backward else seg - 1, :])
     return jnp.broadcast_to(ends[None], (out_rows,) + ends.shape)
+
+
+def _pad(rows_in):
+    extra = _block(rows_in.shape[0]) - rows_in.shape[0]
+    if not extra:
+        return rows_in
+    return jnp.concatenate([rows_in, jnp.zeros((extra, rows_in.shape[1]), rows_in.dtype)], axis=0)
 
 
 def _cut_rows(len_ref, shape, seg, start):
@@ -172,10 +184,11 @@
 
 def _seg_flags(len_ref, devices, seg, start):
     scen, episodes = len_ref.shape
-    rows = devices * scen
+    block = _block(scen)
+    rows = devices * block
     r = lax.broadcasted_iota(jnp.int32, (rows, 1), 0)
-    which = r % scen
-    lo = r // scen * seg
+    which = r % block
+    lo = r // block * seg
     hit = jnp.zeros((rows, 1), jnp.bool_)
     for s in range(scen):
         edge = 0
@@ -265,8 +278,8 @@
     per_row = jnp.sum(w3 * offset, axis=1, keepdims=True)
     copies = e3_ref.shape[0]
     per_scen = jnp.sum(per_row.reshape(scen, seg, 1), axis=1) * scale
-    per_scen = jnp.broadcast_to(per_scen, (scen, 128))
-    e3_ref[:, :, width:] = jnp.broadcast_to(per_scen[None], (copies, scen, 128))
+    per_scen = _pad(jnp.broadcast_to(per_scen, (scen, 128)))
+    e3_ref[:, :, width:] = jnp.broadcast_to(per_scen[None], (copies,) + per_scen.shape)
     e3_ref[:, :, :width] = _ends(_scan(w3, cut_e, pwb_ref, seg, True), seg, True, copies)
 
 
@@ -308,12 +321,13 @@
     ref = ref_traj.reshape(rows, width)
     f32 = jnp.float32
     full = jax.ShapeDtypeStruct((rows, width), f32)
-    ends = jax.ShapeDtypeStruct((devices, scen_count, width), f32)
+    block = _block(scen_count)
+    ends = jax.ShapeDtypeStruct((devices, block, width), f32)
     seg = seg_steps
 
     def gather(copies):
         every = lax.all_to_all(copies, "tm", 0, 0, tiled=True)
-        return every.reshape(devices * scen_count, copies.shape[2])
+        return every.reshape(devices * block, copies.shape[2])
 
     powers = jax.ShapeDtypeStruct((local_levels, width, width), jnp.bfloat16)
     square = jax.ShapeDtypeStruct((width, width), f32)
@@ -325,12 +339,12 @@
     d2, e2 = _call(
         functools.partial(k_states_in, seg), (full, ends),
         w1, lengths, gather(e1), x_init, ff_gain, input_map, phi, plo, dhi, dlo, smem=(1,))
-    packed = jax.ShapeDtypeStruct((devices, scen_count, width + 128), f32)
+    packed = jax.ShapeDtypeStruct((devices, block, width + 128), f32)
     states, w3, e3 = _call(
         functools.partial(k_adjoint_in, seg, 0.5 / total), (full, full, packed),
         d2, lengths, gather(e2), cw, ref, phi, plo, dhi, dlo, smem=(1,))
     g3 = gather(e3)
-    cost = jnp.sum(g3[:, width].reshape(devices, scen_count), axis=0)
+    cost = jnp.sum(g3[:, width].reshape(devices, block)[:, :scen_count], axis=0)
     s4, e4 = _call(
         functools.partial(k_value_adjoint_in, seg), (full, ends),
         w3, lengths, g3, input_map, ff_gain, phi, plo, dhi, dlo, smem=(1,))

time: 84 us -> 89.9 us (1.070)
  blocking collectives: 21.7 us -> 25.3 us
  waiting for transfers between devices: 7.45 us -> 9.41 us
  Pallas kernels: 37.7 us -> 39.3 us
  local copies, waits for them, and re-layouts: 4.32 us -> 3.09 us
    all_to_all x2, blocking collectives: 21.7 us -> 25.3 us  [gather(): every = lax.all_to_all(copies, 'tm', 0, 0, tiled=True)]
    reshape x4 -> x0, local copies, waits for them, and re-layouts: 2.62 us -> none  [gather(): return every.reshape(devices * scen_count, copies.shape[2])]
    all_to_all x2, waiting for transfers between devices: 7.45 us -> 9.41 us  [gather(): every = lax.all_to_all(copies, 'tm', 0, 0, tiled=True)]
    pallas_call x6, Pallas kernels: 37.7 us -> 39.3 us  [_call(): pl.pallas_call(kernel, out_shape=outs, in_specs=specs, out_specs=tuple(_v...]
    unnamed x3 -> x7, local copies, waits for them, and re-layouts: 0.76 us -> 2.07 us
where the time goes in v20:
time: 89.9 us; the launch traced here: 89.3 us
  Pallas kernels  39.3 us (44%)
  blocking collectives  25.3 us (28%)
  starting transfers between devices  11 us (12%)
  waiting for transfers between devices  9.41 us (10%)
  local copies, waits for them, and re-layouts  3.09 us (3%)
    pallas_call x6, Pallas kernels, _call(): pl.pallas_call(kernel, out_shape=outs, in_specs=specs, out_specs=tuple(_v...  39.3 us
    all_to_all x2, blocking collectives, gather(): every = lax.all_to_all(copies, 'tm', 0, 0, tiled=True)  25.3 us
    all_to_all x2, starting transfers between devices, gather(): every = lax.all_to_all(copies, 'tm', 0, 0, tiled=True)  11 us
    all_to_all x2, waiting for transfers between devices, gather(): every = lax.all_to_all(copies, 'tm', 0, 0, tiled=True)  9.41 us
    unnamed x7, local copies, waits for them, and re-layouts  2.07 us
  transfers between devices with their start and end apart: 2, of which 2 were waited for; matrix products, arithmetic and copies ran while one was open for 3% of the time, Pallas kernels for 5%

profile of v20, /device:TPU:0, one launch (start us, length us, event | category | flops | bytes accessed | tf_op | source)
XLA Modules:
  0.0 89.3 jit_solution(9622047860734601835)
XLA Ops:
  0.6 7.1 %shard_map.112 = (bf16[6,256,256]{2,1,0:T(8,128)(2,1)}, bf16[6,256,256]{2,1,0:T(8,128)(2,1)}, f32[256,256]{1,0:T(8,128)}, f32[256,256]{1,0:T(8,128)}, f32[16,8,256]{2,1,0:T(8,128)}) custom-call(f32[1,256]{1,0:T(1,128)} %bitcast.22, f32[3,64,64]{2,1,0:T(8,128)} %coupling_ref.1, s32[2,3]{1,0:T(2,128)} %bitcast.23, f32[256,256]{1,0:T(8,128)} %bitcast.15, ...), custom_call_target="tpu_custom_call" | custom-call | tf_op jit(solution)/shard_map/pallas_call | solution.py:214
  7.8 0.0 copy-start.2
  7.8 7.5 %all-to-all-start = ((f32[16,8,256]{2,1,0:T(8,128)}), f32[16,8,256]{2,1,0:T(8,128)S(1)}, u32[]{:S(2)}, u32[]{:S(2)}) async-start(f32[16,8,256]{2,1,0:T(8,128)} %get-tuple-element.18), calls=%async_computation | async-start | bytes 262144 | tf_op jit(solution)/shard_map/all_to_all | solution.py:329
  15.3 0.0 copy-done.2
  15.3 0.8 copy.14.imap_ref
  16.0 4.1 %shard_map.113 = (bf16[4,256,256]{2,1,0:T(8,128)(2,1)}, bf16[4,256,256]{2,1,0:T(8,128)(2,1)}) custom-call(f32[256,256]{1,0:T(8,128)} %get-tuple-element.21.top_ref), custom_call_target="tpu_custom_call" | custom-call | tf_op jit(solution)/shard_map/pallas_call | solution.py:214
  20.1 3.1 %all-to-all-done = f32[16,8,256]{2,1,0:T(8,128)S(1)} async-done(((f32[16,8,256]{2,1,0:T(8,128)}), f32[16,8,256]{2,1,0:T(8,128)S(1)}, u32[]{:S(2)}, u32[]{:S(2)}) %all-to-all-start) | async-done | bytes 131104 | tf_op jit(solution)/shard_map/all_to_all | solution.py:329
  23.2 0.0 copy-start.1
  23.2 0.6 copy-done.1
  23.8 7.7 %shard_map.114 = (f32[256,256]{1,0:T(8,128)}, f32[16,8,256]{2,1,0:T(8,128)}) custom-call(f32[256,256]{1,0:T(8,128)} %get-tuple-element.17.w1_ref, s32[4,4]{1,0:T(4,128)} %len_ref.9, f32[128,256]{1,0:T(8,128)} %bitcast.18, f32[4,256]{1,0:T(4,128)} %xi_ref.1, f32[64,256]{1,0:T(8,128)} %gain_ref.3, f32[256,64]{1,0:T(8,128)} %copy.14.imap_ref, ...), custom_call_target="tpu_custom_call" | custom-call | tf_op jit(solution)/shard_map/pallas_call | solution.py:214
  31.6 12.1 %all_to_all.20 = f32[16,8,256]{2,1,0:T(8,128)} all-to-all(f32[16,8,256]{2,1,0:T(8,128)} %get-tuple-element.25), channel_id=1, replica_groups=mesh['groups'=2,'tm'=16] {'tm'}, dimensions={0} | all-to-all | bytes 262144 | tf_op jit(solution)/shard_map/all_to_all | solution.py:329
  43.7 7.2 %shard_map.115 = (f32[256,256]{1,0:T(8,128)}, f32[256,256]{1,0:T(8,128)}, f32[16,8,384]{2,1,0:T(8,128)}) custom-call(f32[256,256]{1,0:T(8,128)} %get-tuple-element.24.d2_ref, s32[4,4]{1,0:T(4,128)} %len_ref.9, f32[128,256]{1,0:T(8,128)} %bitcast.19, f32[256,256]{1,0:T(8,128)} %bitcast.16, f32[256,256]{1,0:T(8,128)} %bitcast.11, ...), custom_call_target="tpu_custom_call" | custom-call | tf_op jit(solution)/shard_map/pallas_call | solution.py:214
  50.8 13.2 %all_to_all.21 = f32[16,8,384]{2,1,0:T(8,128)} all-to-all(f32[16,8,384]{2,1,0:T(8,128)} %get-tuple-element.28), channel_id=1, replica_groups=mesh['groups'=2,'tm'=16] {'tm'}, dimensions={0} | all-to-all | bytes 393216 | tf_op jit(solution)/shard_map/all_to_all | solution.py:329
  64.0 7.6 %shard_map.116 = (f32[256,256]{1,0:T(8,128)}, f32[16,8,256]{2,1,0:T(8,128)}) custom-call(f32[256,256]{1,0:T(8,128)} %get-tuple-element.27.w3_ref, s32[4,4]{1,0:T(4,128)} %len_ref.9, f32[128,384]{1,0:T(8,128)} %bitcast.13, f32[256,64]{1,0:T(8,128)} %copy.14.imap_ref, f32[64,256]{1,0:T(8,128)} %gain_ref.3, bf16[6,256,256]{2,1,0:T(8,128)(2,1)} %get-tuple-element.19.phi_ref, ...), custom_call_target="tpu_custom_call" | custom-call | tf_op jit(solution)/shard_map/pallas_call | solution.py:214
  71.6 3.5 %all-to-all-start.3 = ((f32[16,8,256]{2,1,0:T(8,128)}), f32[16,8,256]{2,1,0:T(8,128)S(1)}, u32[]{:S(2)}, u32[]{:S(2)}) async-start(f32[16,8,256]{2,1,0:T(8,128)} %get-tuple-element.30), calls=%async_computation.3 | async-start | bytes 262144 | tf_op jit(solution)/shard_map/all_to_all | solution.py:329
  75.2 0.9 %slice_reduce_fusion = f32[128]{0:T(128)S(1)} fusion(f32[128,384]{1,0:T(8,128)} %bitcast.14), kind=kLoop, calls=%fused_computation | loop fusion | bytes 1024 | tf_op jit(solution)/shard_map/slice | solution.py:347
  76.1 0.1 reshape_squeeze.3
  76.2 0.6 slice_reduce_fusion.1
  76.8 6.3 %all-to-all-done.3 = f32[16,8,256]{2,1,0:T(8,128)S(1)} async-done(((f32[16,8,256]{2,1,0:T(8,128)}), f32[16,8,256]{2,1,0:T(8,128)S(1)}, u32[]{:S(2)}, u32[]{:S(2)}) %all-to-all-start.3) | async-done | bytes 131104 | tf_op jit(solution)/shard_map/all_to_all | solution.py:329
  83.1 0.0 copy-start
  83.1 0.7 copy-done
  83.7 5.6 %shard_map.117 = f32[256,256]{1,0:T(8,128)} custom-call(f32[256,256]{1,0:T(8,128)} %get-tuple-element.29.s4_ref, s32[4,4]{1,0:T(4,128)} %len_ref.9, f32[128,256]{1,0:T(8,128)} %bitcast.17, f32[256,256]{1,0:T(8,128)} %get-tuple-element.26.x_ref, f32[256,256]{1,0:T(8,128)} %bitcast.12, bf16[6,256,256]{2,1,0:T(8,128)(2,1)} %get-tuple-element.19.phi_ref, ...), custom_call_target="tpu_custom_call" | custom-call | tf_op jit(solution)/shard_map/pallas_call | solution.py:214
Async XLA Ops:
  7.8 7.5 %copy-start.2 = (f32[256,64]{0,1:T(8,128)S(1)}, f32[256,64]{0,1:T(8,128)}, u32[]{:S(2)}) copy-start(f32[256,64]{0,1:T(8,128)} %param.15) | copy-start | bytes 196612
  7.8 15.4 %all-to-all-start = ((f32[16,8,256]{2,1,0:T(8,128)}), f32[16,8,256]{2,1,0:T(8,128)S(1)}, u32[]{:S(2)}, u32[]{:S(2)}) async-start(f32[16,8,256]{2,1,0:T(8,128)} %get-tuple-element.18), calls=%async_computation | async-start | bytes 262144 | tf_op jit(solution)/shard_map/all_to_all | solution.py:329
  23.2 0.6 copy-start.1
  71.6 11.4 %all-to-all-start.3 = ((f32[16,8,256]{2,1,0:T(8,128)}), f32[16,8,256]{2,1,0:T(8,128)S(1)}, u32[]{:S(2)}, u32[]{:S(2)}) async-start(f32[16,8,256]{2,1,0:T(8,128)} %get-tuple-element.30), calls=%async_computation.3 | async-start | bytes 262144 | tf_op jit(solution)/shard_map/all_to_all | solution.py:329
  83.1 0.7 copy-start
